TPU v7x, 512 devices: a whole 4x4x16 slice. The times are simulated.
512 devices in a mesh: vox: 32 (over y, x, core), tm: 16 (over z).
Axes of the slice: x: 4, y: 4, z: 16, core: 2. Of those that a mesh axis runs over, the one named last changes fastest.
Arguments:
- series: float32 [2048, 65536], P('tm', 'vox'), may hold values from -40 to 40
- spikes: int32 [2048, 65536], P('tm', 'vox'), may hold values from 0 to 15
- motion: float32 [2048, 6], P('tm'), may hold values from -5 to 5
- tissue: float32 [3, 65536], P(None, 'vox'), may hold values from 0.01 to 12, as said below
Outputs:
- cleaned: float32 [2048, 65536], P('tm', 'vox')
Inputs may be any that keep to these rules, and one draw needn't show every extreme that they name: Bit j-1 of an entry (spikes // 2^(j-1) odd) flags that frame's level-j coefficient of that voxel as a spike. `tissue`: all weights are positive.
All inputs are finite; a program needn't handle non-finite values.
Results may differ from a plain program's by a relative error of at most 0.0003.
Values sent between devices are 32-bit elements; how exact they have to be, the bound alone decides.
No kernel may reach another device: no remote copies, remote signals or barrier semaphores. Data moves between devices by JAX's collectives and lax.ppermute only.
A program may use at most 64 MiB of HBM per device.

v0:
```python
import jax
import jax.numpy as jnp
from jax import lax
from jax.sharding import PartitionSpec as P

LEVELS = 4


def from_behind(block, axis, distance):
    devices = range(lax.axis_size(axis))
    route = [((i - distance) % len(devices), i) for i in devices]
    return lax.ppermute(block, axis, route)


def shifted(block, axis, distance):
    devices = range(lax.axis_size(axis))
    route = [(i - distance, i) for i in devices if i - distance in devices]
    return lax.ppermute(block, axis, route)


def precise_product(left, right):
    return jnp.dot(left, right, precision=lax.Precision.HIGHEST, preferred_element_type=jnp.float32)


def keep_level(spikes, level):
    return 1.0 - (spikes // 2**level % 2).astype(jnp.float32)


def despike_levelwise(series, spikes):
    frames = series.shape[0]
    approx = series
    kept_list = []
    for level in range(LEVELS):
        shift_rows = 2**level
        earlier = from_behind(approx[frames - shift_rows :], "tm", 1)
        lagged = jnp.concatenate([earlier, approx[: frames - shift_rows]], axis=0)
        detail = (approx - lagged) * 0.5
        kept_list.append(detail * keep_level(spikes, level))
        approx = (approx + lagged) * 0.5
    for level in range(LEVELS - 1, -1, -1):
        shift_rows = 2**level
        kept = kept_list[level]
        heads = from_behind(jnp.stack([approx[:shift_rows], kept[:shift_rows]]), "tm", -1)
        lead_approx = jnp.concatenate([approx[shift_rows:], heads[0]], axis=0)
        lead_kept = jnp.concatenate([kept[shift_rows:], heads[1]], axis=0)
        approx = (approx + lead_approx) * 0.5 + (kept - lead_kept) * 0.5
    return approx


def local(series, spikes, motion, tissue):
    spike_free_series = despike_levelwise(series, spikes)
    numer = precise_product(spike_free_series, tissue.T)
    numer = lax.psum(numer, "vox")
    voxel_signals = numer / float(tissue.shape[1] * lax.axis_size("vox"))
    base_regressors = jnp.concatenate([motion, voxel_signals], axis=1)
    previous_frames = shifted(base_regressors[base_regressors.shape[0] - 1 :], "tm", 1)
    before = jnp.concatenate([previous_frames, base_regressors[:-1]], axis=0)
    temporal_derivative = base_regressors - before
    nuisance_matrix = jnp.concatenate(
        [
            base_regressors,
            temporal_derivative,
            base_regressors * base_regressors,
            temporal_derivative * temporal_derivative,
        ],
        axis=1,
    )
    gram_matrix = precise_product(nuisance_matrix.T, nuisance_matrix)
    cross_products = precise_product(nuisance_matrix.T, spike_free_series)
    gram_matrix, cross_products = lax.psum((gram_matrix, cross_products), "tm")
    factor = jnp.linalg.cholesky(gram_matrix)
    beta_estimates = jax.scipy.linalg.cho_solve((factor, True), cross_products)
    return spike_free_series - precise_product(nuisance_matrix, beta_estimates)


def solution(mesh):
    return jax.shard_map(
        local,
        mesh=mesh,
        in_specs=(P("tm", "vox"), P("tm", "vox"), P("tm", None), P(None, "vox")),
        out_specs=P("tm", "vox"),
        check_vma=False,
    )
```

profile of v0, /device:TPU:4, one launch (start us, length us, event | category | flops | bytes accessed | tf_op | source)
XLA Modules:
  0.0 347.5 jit_solution(11441887220270911308)
XLA Ops:
  6.5 0.9 slice.120
  7.4 3.8 %collective-permute-start = (f32[1,2048]{1,0:T(1,128)S(1)}, f32[1,2048]{1,0:T(1,128)S(1)}, u32[]{:S(2)}, u32[]{:S(2)}) collective-permute-start(f32[1,2048]{1,0:T(1,128)S(1)} %slice.120), channel_id=1, source_target_pairs={{15,0},{0,1},{1,2},{2,3},{3,4},{4,5},{5,6},{6,7},{7,8},{8,9},{9,10... | collective-permute-start | bytes 24584 | tf_op jit(solution)/shard_map/ppermute | solution.py:12
  11.2 9.2 %collective-permute-done = f32[1,2048]{1,0:T(1,128)S(1)} collective-permute-done((f32[1,2048]{1,0:T(1,128)S(1)}, f32[1,2048]{1,0:T(1,128)S(1)}, u32[]{:S(2)}, u32[]{:S(2)}) %collective-permute-start) | collective-permute-done | bytes 8224 | tf_op jit(solution)/shard_map/ppermute | solution.py:12
  20.4 2.6 fusion.16
  23.1 1.9 collective-permute-start.1
  25.0 4.9 %collective-permute-done.1 = f32[2,2048]{1,0:T(2,128)S(1)} collective-permute-done((f32[2,2048]{1,0:T(2,128)S(1)}, f32[2,2048]{1,0:T(2,128)S(1)}, u32[]{:S(2)}, u32[]{:S(2)}) %collective-permute-start.1) | collective-permute-done | bytes 16416 | tf_op jit(solution)/shard_map/ppermute | solution.py:12
  29.9 1.3 fusion.13
  31.2 1.9 collective-permute-start.2
  33.1 5.1 %collective-permute-done.2 = f32[4,2048]{1,0:T(4,128)S(1)} collective-permute-done((f32[4,2048]{1,0:T(4,128)S(1)}, f32[4,2048]{1,0:T(4,128)S(1)}, u32[]{:S(2)}, u32[]{:S(2)}) %collective-permute-start.2) | collective-permute-done | bytes 32800 | tf_op jit(solution)/shard_map/ppermute | solution.py:12
  38.2 1.3 fusion.9
  39.5 1.9 collective-permute-start.3
  41.5 5.3 %collective-permute-done.3 = f32[8,2048]{1,0:T(8,128)S(1)} collective-permute-done((f32[8,2048]{1,0:T(8,128)S(1)}, f32[8,2048]{1,0:T(8,128)S(1)}, u32[]{:S(2)}, u32[]{:S(2)}) %collective-permute-start.3) | collective-permute-done | bytes 65568 | tf_op jit(solution)/shard_map/ppermute | solution.py:12
  46.9 1.2 fusion.4
  48.1 1.9 collective-permute-start.4
  50.1 0.1 slice.164
  50.2 5.4 %collective-permute-done.4 = f32[2,8,2048]{2,1,0:T(8,128)S(1)} collective-permute-done((f32[2,8,2048]{2,1,0:T(8,128)S(1)}, f32[2,8,2048]{2,1,0:T(8,128)S(1)}, u32[]{:S(2)}, u32[]{:S(2)}) %collective-permute-start.4) | collective-permute-done | bytes 131104 | tf_op jit(solution)/shard_map/ppermute | solution.py:12
  55.7 0.3 fusion.18
  56.1 2.4 collective-permute-start.5
  58.5 0.1 slice.170
  58.6 0.1 slice.166
  58.7 3.5 %collective-permute-done.5 = f32[2,4,2048]{2,1,0:T(4,128)S(1)} collective-permute-done((f32[2,4,2048]{2,1,0:T(4,128)S(1)}, f32[2,4,2048]{2,1,0:T(4,128)S(1)}, u32[]{:S(2)}, u32[]{:S(2)}) %collective-permute-start.5) | collective-permute-done | bytes 65568 | tf_op jit(solution)/shard_map/ppermute | solution.py:12
  62.2 0.3 fusion.20
  62.6 4.0 %collective-permute-start.6 = (f32[2,2,2048]{2,1,0:T(2,128)S(1)}, f32[2,2,2048]{2,1,0:T(2,128)S(1)}, u32[]{:S(2)}, u32[]{:S(2)}) collective-permute-start(f32[2,2,2048]{2,1,0:T(2,128)S(1)} %pad_maximum_fusion.6), channel_id=1, source_target_pairs={{1,0},{2,1},{3,2},{4,3},{5,4},{6,5},{7,6},{8,7},{9,8},{10,9},{11,1... | collective-permute-start | bytes 98312 | tf_op jit(solution)/shard_map/ppermute | solution.py:12
  66.6 0.1 slice.176
  66.7 0.1 slice.172
  66.8 1.6 collective-permute-done.6
  68.4 0.4 fusion.22
  68.8 5.2 %collective-permute-start.7 = (f32[2,1,2048]{2,1,0:T(1,128)S(1)}, f32[2,1,2048]{2,1,0:T(1,128)S(1)}, u32[]{:S(2)}, u32[]{:S(2)}) collective-permute-start(f32[2,1,2048]{2,1,0:T(1,128)S(1)} %pad_maximum_fusion.7), channel_id=1, source_target_pairs={{1,0},{2,1},{3,2},{4,3},{5,4},{6,5},{7,6},{8,7},{9,8},{10,9},{11,1... | collective-permute-start | bytes 49160 | tf_op jit(solution)/shard_map/ppermute | solution.py:12
  74.1 0.1 slice.178
  74.2 1.2 collective-permute-done.7
  75.5 0.3 fusion.24
  75.8 0.9 fusion.38
  76.7 52.6 %psum.21 = f32[128,3]{0,1:T(4,128)S(1)} all-reduce(f32[128,3]{0,1:T(4,128)S(1)} %fusion.38), channel_id=1, replica_groups=mesh['vox'=32,'tm'=16] {'vox'}, use_global_device_ids=true, to_apply=%region_0.1 | all-reduce | flops 384 | bytes 3072 | tf_op jit(solution)/shard_map/psum | solution.py:53
  129.4 1.3 collective-permute-start.8
  130.7 1.3 collective-permute-done.8
  132.1 0.4 concatenate.60
  132.5 0.2 fusion.39
  132.7 1.4 fusion.40
  134.1 58.9 %psum.22 = f32[36,36]{0,1:T(8,128)S(1)} all-reduce(f32[36,36]{0,1:T(8,128)S(1)} %fusion.39), channel_id=1, replica_groups=mesh['vox'=32,'tm'=16] {'tm'}, use_global_device_ids=true, to_apply=%region_1.2 | all-reduce | flops 1296 | bytes 10368 | tf_op jit(solution)/shard_map/psum | solution.py:70
  193.0 0.1 copy.6
  193.1 3.3 cholesky.16
  196.4 0.7 compare_reduce_fusion
  197.1 0.6 fusion.28
  197.7 2.8 custom-call.10
  200.5 136.3 %all-reduce.2.cloned.1.call-done = f32[36,2048]{1,0:T(8,128)} async-done(((f32[36,2048]{1,0:T(8,128)}), f32[36,2048]{1,0:T(8,128)}) %all-reduce.2.cloned.1.call-update) | async-done | bytes 294928 | tf_op jit(solution)/shard_map/psum | solution.py:70
  336.8 1.4 fusion.31
  338.2 0.4 fusion.29
  338.7 2.0 convolution_subtract_fusion
  (35 shorter events, 0.7 us)
Async XLA Ops:
  6.5 69.2 %copy-start = (f32[3,2048]{1,0:T(4,128)S(1)}, f32[3,2048]{1,0:T(4,128)}, u32[]{:S(2)}) copy-start(f32[3,2048]{1,0:T(4,128)} %param.7) | copy-start | bytes 73732
  6.5 330.3 %all-reduce.2.cloned.1.call-start = ((), (), s32[]{:S(2)}) async-start(), calls=%async_computation | async-start | bytes 655360 | tf_op jit(solution)/shard_map/psum | solution.py:70
  7.4 13.0 %collective-permute-start = (f32[1,2048]{1,0:T(1,128)S(1)}, f32[1,2048]{1,0:T(1,128)S(1)}, u32[]{:S(2)}, u32[]{:S(2)}) collective-permute-start(f32[1,2048]{1,0:T(1,128)S(1)} %slice.120), channel_id=1, source_target_pairs={{15,0},{0,1},{1,2},{2,3},{3,4},{4,5},{5,6},{6,7},{7,8},{8,9},{9,10... | collective-permute-start | bytes 24584 | tf_op jit(solution)/shard_map/ppermute | solution.py:12
  20.4 9.5 %copy-start.1 = (s32[128,2048]{1,0:T(8,128)S(1)}, s32[128,2048]{1,0:T(8,128)}, u32[]{:S(2)}) copy-start(s32[128,2048]{1,0:T(8,128)} %param.5) | copy-start | bytes 3145732
  23.1 6.8 %collective-permute-start.1 = (f32[2,2048]{1,0:T(2,128)S(1)}, f32[2,2048]{1,0:T(2,128)S(1)}, u32[]{:S(2)}, u32[]{:S(2)}) collective-permute-start(f32[2,2048]{1,0:T(2,128)S(1)} %slice.154), channel_id=1, source_target_pairs={{15,0},{0,1},{1,2},{2,3},{3,4},{4,5},{5,6},{6,7},{7,8},{8,9},{9,10... | collective-permute-start | bytes 49160 | tf_op jit(solution)/shard_map/ppermute | solution.py:12
  31.2 7.0 %collective-permute-start.2 = (f32[4,2048]{1,0:T(4,128)S(1)}, f32[4,2048]{1,0:T(4,128)S(1)}, u32[]{:S(2)}, u32[]{:S(2)}) collective-permute-start(f32[4,2048]{1,0:T(4,128)S(1)} %slice.156), channel_id=1, source_target_pairs={{15,0},{0,1},{1,2},{2,3},{3,4},{4,5},{5,6},{6,7},{7,8},{8,9},{9,10... | collective-permute-start | bytes 98312 | tf_op jit(solution)/shard_map/ppermute | solution.py:12
  39.5 7.4 %collective-permute-start.3 = (f32[8,2048]{1,0:T(8,128)S(1)}, f32[8,2048]{1,0:T(8,128)S(1)}, u32[]{:S(2)}, u32[]{:S(2)}) collective-permute-start(f32[8,2048]{1,0:T(8,128)S(1)} %slice.158), channel_id=1, source_target_pairs={{15,0},{0,1},{1,2},{2,3},{3,4},{4,5},{5,6},{6,7},{7,8},{8,9},{9,10... | collective-permute-start | bytes 196616 | tf_op jit(solution)/shard_map/ppermute | solution.py:12
  48.1 7.6 %collective-permute-start.4 = (f32[2,8,2048]{2,1,0:T(8,128)S(1)}, f32[2,8,2048]{2,1,0:T(8,128)S(1)}, u32[]{:S(2)}, u32[]{:S(2)}) collective-permute-start(f32[2,8,2048]{2,1,0:T(8,128)S(1)} %pad_maximum_fusion.4), channel_id=1, source_target_pairs={{1,0},{2,1},{3,2},{4,3},{5,4},{6,5},{7,6},{8,7},{9,8},{10,9},{11,1... | collective-permute-start | bytes 393224 | tf_op jit(solution)/shard_map/ppermute | solution.py:12
  56.1 6.2 %collective-permute-start.5 = (f32[2,4,2048]{2,1,0:T(4,128)S(1)}, f32[2,4,2048]{2,1,0:T(4,128)S(1)}, u32[]{:S(2)}, u32[]{:S(2)}) collective-permute-start(f32[2,4,2048]{2,1,0:T(4,128)S(1)} %pad_maximum_fusion.5), channel_id=1, source_target_pairs={{1,0},{2,1},{3,2},{4,3},{5,4},{6,5},{7,6},{8,7},{9,8},{10,9},{11,1... | collective-permute-start | bytes 196616 | tf_op jit(solution)/shard_map/ppermute | solution.py:12
  62.6 5.8 %collective-permute-start.6 = (f32[2,2,2048]{2,1,0:T(2,128)S(1)}, f32[2,2,2048]{2,1,0:T(2,128)S(1)}, u32[]{:S(2)}, u32[]{:S(2)}) collective-permute-start(f32[2,2,2048]{2,1,0:T(2,128)S(1)} %pad_maximum_fusion.6), channel_id=1, source_target_pairs={{1,0},{2,1},{3,2},{4,3},{5,4},{6,5},{7,6},{8,7},{9,8},{10,9},{11,1... | collective-permute-start | bytes 98312 | tf_op jit(solution)/shard_map/ppermute | solution.py:12
  68.8 6.6 %collective-permute-start.7 = (f32[2,1,2048]{2,1,0:T(1,128)S(1)}, f32[2,1,2048]{2,1,0:T(1,128)S(1)}, u32[]{:S(2)}, u32[]{:S(2)}) collective-permute-start(f32[2,1,2048]{2,1,0:T(1,128)S(1)} %pad_maximum_fusion.7), channel_id=1, source_target_pairs={{1,0},{2,1},{3,2},{4,3},{5,4},{6,5},{7,6},{8,7},{9,8},{10,9},{11,1... | collective-permute-start | bytes 49160 | tf_op jit(solution)/shard_map/ppermute | solution.py:12
  76.7 52.6 %copy-start.2 = (f32[128,6]{0,1:T(8,128)S(1)}, f32[128,6]{0,1:T(8,128)}, u32[]{:S(2)}) copy-start(f32[128,6]{0,1:T(8,128)} %param.6) | copy-start | bytes 9220
  129.4 2.6 collective-permute-start.8
Sparse Core Ops, SparseCore 0:
  196.6 140.1 all-reduce.1
where the time goes:
time: 348 us
  waiting for transfers between devices  174 us (50%)
  blocking collectives  111 us (32%)
  starting transfers between devices  24.4 us (7%)
  other arithmetic  15.3 us (4%)
  between operations  13.7 us (4%)
  matrix products  6.32 us (2%)
    psum x1, waiting for transfers between devices, local(): gram_matrix, cross_products = lax.psum((gram_matrix, cross_products), 'tm')  136 us
    psum x1, blocking collectives, local(): gram_matrix, cross_products = lax.psum((gram_matrix, cross_products), 'tm')  58.9 us
    psum x1, blocking collectives, local(): numer = lax.psum(numer, 'vox')  52.6 us
    ppermute x8, waiting for transfers between devices, from_behind(): return lax.ppermute(block, axis, route)  36.3 us
    ppermute x8, starting transfers between devices, from_behind(): return lax.ppermute(block, axis, route)  23.1 us
  transfers between devices with their start and end apart: 10, of which 10 were waited for; matrix products, arithmetic and copies ran while one was open for 1% of the time, Pallas kernels for 0%

commit v1 on v0

v1 whole, which is shorter than its diff:
```python
import jax
import jax.numpy as jnp
from jax import lax
from jax.sharding import PartitionSpec as P

LEVELS = 4
HALO = 16


def from_behind(block, axis, distance):
    devices = range(lax.axis_size(axis))
    route = [((i - distance) % len(devices), i) for i in devices]
    return lax.ppermute(block, axis, route)


def precise_product(left, right):
    return jnp.dot(left, right, precision=lax.Precision.HIGHEST, preferred_element_type=jnp.float32)


def keep_level(spikes, level):
    return 1.0 - (spikes // 2**level % 2).astype(jnp.float32)


def despike_window(window, flags):
    approx = window
    kept_list = []
    for level in range(LEVELS):
        shift_rows = 2**level
        lagged = jnp.roll(approx, shift_rows, axis=0)
        detail = (approx - lagged) * 0.5
        kept_list.append(detail * keep_level(flags, level))
        approx = (approx + lagged) * 0.5
    for level in range(LEVELS - 1, -1, -1):
        shift_rows = 2**level
        kept = kept_list[level]
        lead_approx = jnp.roll(approx, -shift_rows, axis=0)
        lead_kept = jnp.roll(kept, -shift_rows, axis=0)
        approx = (approx + lead_approx) * 0.5 + (kept - lead_kept) * 0.5
    return approx


def sum_over_vox(block):
    n = lax.axis_size("vox")
    copies = jnp.broadcast_to(block, (n,) + block.shape)
    return lax.all_to_all(copies, "vox", 0, 0, tiled=False).sum(axis=0)


def sum_over_tm(block):
    n = lax.axis_size("tm")
    rows, cols = block.shape
    parts = block.reshape(rows, n, cols // n).transpose(1, 0, 2)
    owned = lax.all_to_all(parts, "tm", 0, 0, tiled=False).sum(axis=0)
    copies = jnp.broadcast_to(owned, (n,) + owned.shape)
    gathered = lax.all_to_all(copies, "tm", 0, 0, tiled=False)
    return gathered.transpose(1, 0, 2).reshape(rows, cols)


def local(series, spikes, motion, tissue):
    frames = series.shape[0]
    flags = spikes.astype(jnp.float32)
    tail = jnp.stack([series[frames - HALO :], flags[frames - HALO :]])
    head = jnp.stack([series[:HALO], flags[:HALO]])
    before = from_behind(tail, "tm", 1)
    after = from_behind(head, "tm", -1)
    motion_before = from_behind(motion[frames - 1 :], "tm", 1)
    window = jnp.concatenate([before[0], series, after[0]], axis=0)
    window_flags = jnp.concatenate([before[1], flags, after[1]], axis=0).astype(jnp.int32)
    despiked_window = despike_window(window, window_flags)
    spike_free_series = despiked_window[HALO : HALO + frames]

    rows = despiked_window[HALO - 8 : HALO + frames]
    numer = sum_over_vox(precise_product(rows, tissue.T))
    voxel_signals = numer / float(tissue.shape[1] * lax.axis_size("vox"))

    first = lax.axis_index("tm") == 0
    base_before = jnp.concatenate([motion_before, voxel_signals[7:8]], axis=1)
    base_before = jnp.where(first, jnp.zeros_like(base_before), base_before)
    base_regressors = jnp.concatenate([motion, voxel_signals[8:]], axis=1)
    previous = jnp.concatenate([base_before, base_regressors[:-1]], axis=0)
    temporal_derivative = base_regressors - previous
    nuisance_matrix = jnp.concatenate(
        [
            base_regressors,
            temporal_derivative,
            base_regressors * base_regressors,
            temporal_derivative * temporal_derivative,
        ],
        axis=1,
    )
    terms = nuisance_matrix.shape[1]
    voxels = series.shape[1]
    gram_matrix = precise_product(nuisance_matrix.T, nuisance_matrix)
    cross_products = precise_product(nuisance_matrix.T, spike_free_series)
    gram_rows = -(-terms * terms // voxels)
    gram_flat = jnp.pad(gram_matrix.reshape(terms * terms), (0, gram_rows * voxels - terms * terms))
    packed = jnp.concatenate([cross_products, gram_flat.reshape(gram_rows, voxels)], axis=0)
    summed = sum_over_tm(packed)
    cross_products = summed[:terms]
    gram_matrix = summed[terms:].reshape(-1)[: terms * terms].reshape(terms, terms)
    factor = jnp.linalg.cholesky(gram_matrix)
    beta_estimates = jax.scipy.linalg.cho_solve((factor, True), cross_products)
    return spike_free_series - precise_product(nuisance_matrix, beta_estimates)


def solution(mesh):
    return jax.shard_map(
        local,
        mesh=mesh,
        in_specs=(P("tm", "vox"), P("tm", "vox"), P("tm", None), P(None, "vox")),
        out_specs=P("tm", "vox"),
        check_vma=False,
    )
```

time: 348 us -> 124 us (0.36)
  the two profiles are of different devices: /device:TPU:4 before, /device:TPU:64 now
where the time goes in v1:
time: 124 us; the launch traced here: 123 us
  blocking collectives  61.4 us (50%)
  other arithmetic  17.8 us (14%)
  starting transfers between devices  15.9 us (13%)
  waiting for transfers between devices  12.7 us (10%)
  local copies, waits for them, and re-layouts  10.5 us (8%)
  matrix products  4.68 us (4%)
    all_to_all x1, blocking collectives, sum_over_tm(): owned = lax.all_to_all(parts, 'tm', 0, 0, tiled=False).sum(axis=0)  33.8 us
    all_to_all x1, blocking collectives, sum_over_tm(): gathered = lax.all_to_all(copies, 'tm', 0, 0, tiled=False)  27.6 us
    ppermute x3, starting transfers between devices, from_behind(): return lax.ppermute(block, axis, route)  10.5 us
    ppermute x3, waiting for transfers between devices, from_behind(): return lax.ppermute(block, axis, route)  9.95 us
    unnamed x24, local copies, waits for them, and re-layouts  7.7 us
    mul x4, other arithmetic, despike_window(): kept_list.append(detail * keep_level(flags, level))  5.84 us
    all_to_all x1, starting transfers between devices, sum_over_vox(): return lax.all_to_all(copies, 'vox', 0, 0, tiled=False).sum(axis=0)  5.46 us
    another operation x3, other arithmetic, local(): factor = jnp.linalg.cholesky(gram_matrix)  3.96 us
  transfers between devices with their start and end apart: 4, of which 4 were waited for; matrix products, arithmetic and copies ran while one was open for 1% of the time, Pallas kernels for 0%

profile of v1, /device:TPU:64, one launch (start us, length us, event | category | flops | bytes accessed | tf_op | source)
XLA Modules:
  0.0 123.5 jit_solution(17562749450203980161)
XLA Ops:
  0.0 1.4 %convert_element_type.20 = f32[128,2048]{1,0:T(8,128)S(1)} convert(s32[128,2048]{1,0:T(8,128)} %param.5) | non-fusion elementwise | flops 262144 | bytes 2097152 | tf_op jit(solution)/shard_map/convert_element_type | solution.py:60
  1.4 0.1 copy-done.7
  1.6 2.0 %collective-permute-start.1 = (f32[2,16,2048]{2,1,0:T(8,128)S(1)}, f32[2,16,2048]{2,1,0:T(8,128)S(1)}, u32[]{:S(2)}, u32[]{:S(2)}) collective-permute-start(f32[2,16,2048]{2,1,0:T(8,128)S(1)} %pad_maximum_fusion.6), channel_id=1, source_target_pairs={{1,0},{2,1},{3,2},{4,3},{5,4},{6,5},{7,6},{8,7},{9,8},{10,9},{11,1... | collective-permute-start | bytes 786440 | tf_op jit(solution)/shard_map/ppermute | solution.py:13
  3.7 3.8 %collective-permute-start = (f32[2,16,2048]{2,1,0:T(8,128)S(1)}, f32[2,16,2048]{2,1,0:T(8,128)S(1)}, u32[]{:S(2)}, u32[]{:S(2)}) collective-permute-start(f32[2,16,2048]{2,1,0:T(8,128)S(1)} %pad_maximum_fusion.5), channel_id=1, source_target_pairs={{15,0},{0,1},{1,2},{2,3},{3,4},{4,5},{5,6},{6,7},{7,8},{8,9},{9,10... | collective-permute-start | bytes 786440 | tf_op jit(solution)/shard_map/ppermute | solution.py:13
  7.5 4.2 %collective-permute-done.1 = f32[2,16,2048]{2,1,0:T(8,128)S(1)} collective-permute-done((f32[2,16,2048]{2,1,0:T(8,128)S(1)}, f32[2,16,2048]{2,1,0:T(8,128)S(1)}, u32[]{:S(2)}, u32[]{:S(2)}) %collective-permute-start.1) | collective-permute-done | bytes 262176 | tf_op jit(solution)/shard_map/ppermute | solution.py:13
  11.8 3.6 %collective-permute-done = f32[2,16,2048]{2,1,0:T(8,128)S(1)} collective-permute-done((f32[2,16,2048]{2,1,0:T(8,128)S(1)}, f32[2,16,2048]{2,1,0:T(8,128)S(1)}, u32[]{:S(2)}, u32[]{:S(2)}) %collective-permute-start) | collective-permute-done | bytes 262176 | tf_op jit(solution)/shard_map/ppermute | solution.py:13
  15.4 0.1 pad_maximum_fusion
  15.5 0.9 fusion.16
  16.5 1.7 %fusion.13 = (f32[160,2048]{1,0:T(8,128)S(1)}, f32[160,2048]{1,0:T(8,128)S(1)}) fusion(f32[160,2048]{1,0:T(8,128)S(1)} %get-tuple-element.12, f32[158,2048]{1,0:T(8,128)S(1)} %bitcast.58, f32[2,2048]{1,0:T(2,128)S(1)} %slice.215, f32[16,2048]{1,0:T(8,128)S(1)} %get-tuple-element.21, f32[128,2048]{1,0:T(8,128)S(1)} %convert_element_type.20, ...), kind=kLoop, calls=%fused_computation.34 | loop fusion | flops 12124160 | bytes 6553600 | tf_op jit(solution)/shard_map/mul | solution.py:31
  18.2 1.7 %fusion.9 = (f32[160,2048]{1,0:T(8,128)S(1)}, f32[160,2048]{1,0:T(8,128)S(1)}) fusion(f32[160,2048]{1,0:T(8,128)S(1)} %get-tuple-element.10, f32[156,2048]{1,0:T(8,128)S(1)} %bitcast.57, f32[4,2048]{1,0:T(4,128)S(1)} %slice.217, f32[16,2048]{1,0:T(8,128)S(1)} %get-tuple-element.21, f32[128,2048]{1,0:T(8,128)S(1)} %convert_element_type.20, ...), kind=kLoop, calls=%fused_computation.30 | loop fusion | flops 12124160 | bytes 6553600 | tf_op jit(solution)/shard_map/mul | solution.py:31
  20.0 1.6 %fusion.4 = (f32[160,2048]{1,0:T(8,128)S(1)}, f32[160,2048]{1,0:T(8,128)S(1)}) fusion(f32[160,2048]{1,0:T(8,128)S(1)} %get-tuple-element.8, f32[152,2048]{1,0:T(8,128)S(1)} %slice.220, f32[8,2048]{1,0:T(8,128)S(1)} %slice.219, f32[16,2048]{1,0:T(8,128)S(1)} %get-tuple-element.21, f32[128,2048]{1,0:T(8,128)S(1)} %convert_element_type.20, ...), kind=kLoop, calls=%fused_computation.25 | loop fusion | flops 12124160 | bytes 6553600 | tf_op jit(solution)/shard_map/mul | solution.py:31
  21.8 0.5 fusion.18
  22.4 1.0 copy-done.1
  23.3 0.1 slice.229
  23.5 1.2 copy-done.2
  24.7 0.5 fusion.20
  25.2 0.1 slice.231
  25.3 0.9 copy-done.3
  26.3 0.1 slice.233
  26.4 1.1 copy-done.4
  27.6 0.5 fusion.22
  28.1 0.1 slice.235
  28.3 1.0 copy-done.5
  29.2 0.1 slice.237
  29.3 1.2 copy-done.6
  30.5 0.5 fusion.24
  31.1 1.0 fusion.27
  32.1 0.8 reshape.63
  32.9 5.5 %all-to-all-start = ((f32[32,1,408]{2,1,0:T(1,128)}), f32[32,1,408]{2,1,0:T(1,128)S(1)}, u32[]{:S(2)}, u32[]{:S(2)}) async-start(f32[32,1,408]{2,1,0:T(1,128)} %reshape.63), calls=%async_computation | async-start | bytes 131072 | tf_op jit(solution)/shard_map/all_to_all | solution.py:45
  38.5 4.6 %collective-permute-start.2 = (f32[1,6]{0,1:T(8,128)S(1)}, f32[1,6]{0,1:T(8,128)S(1)}, u32[]{:S(2)}, u32[]{:S(2)}) collective-permute-start(f32[1,6]{0,1:T(8,128)S(1)} %slice.202), channel_id=1, source_target_pairs={{15,0},{0,1},{1,2},{2,3},{3,4},{4,5},{5,6},{6,7},{7,8},{8,9},{9,10... | collective-permute-start | bytes 80 | tf_op jit(solution)/shard_map/ppermute | solution.py:13
  43.1 2.7 %all-to-all-done = f32[32,1,408]{2,1,0:T(1,128)S(1)} async-done(((f32[32,1,408]{2,1,0:T(1,128)}), f32[32,1,408]{2,1,0:T(1,128)S(1)}, u32[]{:S(2)}, u32[]{:S(2)}) %all-to-all-start) | async-done | bytes 52256 | tf_op jit(solution)/shard_map/all_to_all | solution.py:45
  45.9 0.5 broadcast.159
  46.4 0.8 reduce.6
  47.2 0.1 reshape.64
  47.5 2.1 %collective-permute-done.2 = f32[1,6]{0,1:T(8,128)S(1)} collective-permute-done((f32[1,6]{0,1:T(8,128)S(1)}, f32[1,6]{0,1:T(8,128)S(1)}, u32[]{:S(2)}, u32[]{:S(2)}) %collective-permute-start.2) | collective-permute-done | bytes 56 | tf_op jit(solution)/shard_map/ppermute | solution.py:13
  49.7 0.4 concatenate.96
  50.2 0.7 fusion.29
  50.8 0.2 fusion.41
  51.4 33.8 %all_to_all.15 = f32[16,37,128]{2,1,0:T(8,128)S(1)} all-to-all(f32[16,37,128]{2,1,0:T(8,128)S(1)} %maximum_bitcast_fusion), channel_id=1, replica_groups=mesh['vox'=32,'tm'=16] {'tm'}, dimensions={0} | all-to-all | bytes 606208 | tf_op jit(solution)/shard_map/all_to_all | solution.py:52
  85.2 27.6 %all_to_all.16 = f32[16,37,128]{2,1,0:T(8,128)S(1)} all-to-all(f32[16,37,128]{2,1,0:T(8,128)S(1)} %broadcast_in_dim.9), channel_id=1, replica_groups=mesh['vox'=32,'tm'=16] {'tm'}, dimensions={0} | all-to-all | bytes 606208 | tf_op jit(solution)/shard_map/all_to_all | solution.py:54
  113.0 3.3 %cholesky.16 = f32[36,36]{1,0:T(8,128)S(1)} custom-call(f32[36,36]{1,0:T(8,128)S(1)} %fusion.37), custom_call_target="Cholesky" | custom-call | tf_op jit(solution)/shard_map/jit(cholesky)/cholesky | solution.py:100
  116.3 0.6 compare_reduce_fusion
  117.0 0.7 fusion.32
  117.6 2.8 %custom-call.10 = f32[1,36,36]{1,2,0:T(8,128)S(1)} custom-call(f32[1,36,36]{2,1,0:T(8,128)S(1)} %fusion.32), custom_call_target="InvertDiagBlocksLowerTriangular" | custom-call | tf_op jit(solution)/shard_map/jit(_cho_solve)/triangular_solve | solution.py:101
  120.5 0.1 copy.13
  120.6 0.5 fusion.35
  121.1 0.4 fusion.33
  121.5 2.0 %convolution_subtract_fusion = f32[128,2048]{1,0:T(8,128)} fusion(f32[128,36]{0,1:T(8,128)S(1)} %concatenate.96, f32[36,2048]{1,0:T(8,128)S(1)} %fusion.33, f32[160,2048]{1,0:T(8,128)S(1)} %fusion.24), kind=kOutput, calls=%fused_computation | convolution fusion | flops 113508352 | bytes 2410496 | tf_op jit(solution)/shard_map/dot_general | solution.py:17
  (59 shorter events, 1.7 us)
Async XLA Ops:
  0.0 31.1 %copy-start = (f32[3,2048]{1,0:T(4,128)S(1)}, f32[3,2048]{1,0:T(4,128)}, u32[]{:S(2)}) copy-start(f32[3,2048]{1,0:T(4,128)} %param.7) | copy-start | bytes 73732
  0.0 1.5 %copy-start.7 = (f32[128,2048]{1,0:T(8,128)S(1)}, f32[128,2048]{1,0:T(8,128)}, u32[]{:S(2)}) copy-start(f32[128,2048]{1,0:T(8,128)} %param.4) | copy-start | bytes 3145732
  1.6 10.1 %collective-permute-start.1 = (f32[2,16,2048]{2,1,0:T(8,128)S(1)}, f32[2,16,2048]{2,1,0:T(8,128)S(1)}, u32[]{:S(2)}, u32[]{:S(2)}) collective-permute-start(f32[2,16,2048]{2,1,0:T(8,128)S(1)} %pad_maximum_fusion.6), channel_id=1, source_target_pairs={{1,0},{2,1},{3,2},{4,3},{5,4},{6,5},{7,6},{8,7},{9,8},{10,9},{11,1... | collective-permute-start | bytes 786440 | tf_op jit(solution)/shard_map/ppermute | solution.py:13
  3.7 11.7 %collective-permute-start = (f32[2,16,2048]{2,1,0:T(8,128)S(1)}, f32[2,16,2048]{2,1,0:T(8,128)S(1)}, u32[]{:S(2)}, u32[]{:S(2)}) collective-permute-start(f32[2,16,2048]{2,1,0:T(8,128)S(1)} %pad_maximum_fusion.5), channel_id=1, source_target_pairs={{15,0},{0,1},{1,2},{2,3},{3,4},{4,5},{5,6},{6,7},{7,8},{8,9},{9,10... | collective-permute-start | bytes 786440 | tf_op jit(solution)/shard_map/ppermute | solution.py:13
  22.3 1.1 copy-start.1
  23.3 1.3 %copy-start.2 = (f32[160,2048]{1,0:T(8,128)S(1)}, f32[160,2048]{1,0:T(8,128)}, u32[]{:S(2)}) copy-start(f32[160,2048]{1,0:T(8,128)} %copy-done.1) | copy-start | bytes 3932164
  23.3 1.3 %slice-start = ((f32[160,2048]{1,0:T(8,128)}), f32[4,2048]{1,0:T(4,128)S(1)}, s32[]{:S(2)}) async-start(f32[160,2048]{1,0:T(8,128)} %copy-done.1), calls=%async_computation.3 | async-start | bytes 65536 | tf_op jit(solution)/shard_map/jit(_roll_static)/slice | solution.py:36
  25.2 1.1 copy-start.3
  26.3 1.3 %copy-start.4 = (f32[160,2048]{1,0:T(8,128)S(1)}, f32[160,2048]{1,0:T(8,128)}, u32[]{:S(2)}) copy-start(f32[160,2048]{1,0:T(8,128)} %copy-done.3) | copy-start | bytes 3932164
  26.3 1.3 %slice-start.1 = ((f32[160,2048]{1,0:T(8,128)}), f32[2,2048]{1,0:T(2,128)S(1)}, s32[]{:S(2)}) async-start(f32[160,2048]{1,0:T(8,128)} %copy-done.3), calls=%async_computation.4 | async-start | bytes 32768 | tf_op jit(solution)/shard_map/jit(_roll_static)/slice | solution.py:36
  28.1 1.1 copy-start.5
  29.2 1.3 %copy-start.6 = (f32[160,2048]{1,0:T(8,128)S(1)}, f32[160,2048]{1,0:T(8,128)}, u32[]{:S(2)}) copy-start(f32[160,2048]{1,0:T(8,128)} %copy-done.5) | copy-start | bytes 3932164
  29.2 1.3 %slice-start.2 = ((f32[160,2048]{1,0:T(8,128)}), f32[1,2048]{1,0:T(1,128)S(1)}, s32[]{:S(2)}) async-start(f32[160,2048]{1,0:T(8,128)} %copy-done.5), calls=%async_computation.5 | async-start | bytes 16384 | tf_op jit(solution)/shard_map/jit(_roll_static)/slice | solution.py:36
  31.1 7.3 %copy-start.8 = (f32[128,6]{0,1:T(8,128)S(1)}, f32[128,6]{0,1:T(8,128)}, u32[]{:S(2)}) copy-start(f32[128,6]{0,1:T(8,128)} %param.6) | copy-start | bytes 9220
  32.9 12.9 %all-to-all-start = ((f32[32,1,408]{2,1,0:T(1,128)}), f32[32,1,408]{2,1,0:T(1,128)S(1)}, u32[]{:S(2)}, u32[]{:S(2)}) async-start(f32[32,1,408]{2,1,0:T(1,128)} %reshape.63), calls=%async_computation | async-start | bytes 131072 | tf_op jit(solution)/shard_map/all_to_all | solution.py:45
  38.5 11.2 %collective-permute-start.2 = (f32[1,6]{0,1:T(8,128)S(1)}, f32[1,6]{0,1:T(8,128)S(1)}, u32[]{:S(2)}, u32[]{:S(2)}) collective-permute-start(f32[1,6]{0,1:T(8,128)S(1)} %slice.202), channel_id=1, source_target_pairs={{15,0},{0,1},{1,2},{2,3},{3,4},{4,5},{5,6},{6,7},{7,8},{8,9},{9,10... | collective-permute-start | bytes 80 | tf_op jit(solution)/shard_map/ppermute | solution.py:13

commit v2 on v1

--- a/solution.py
+++ b/solution.py
@@ -57,16 +57,25 @@
 
 def local(series, spikes, motion, tissue):
     frames = series.shape[0]
-    flags = spikes.astype(jnp.float32)
-    tail = jnp.stack([series[frames - HALO :], flags[frames - HALO :]])
-    head = jnp.stack([series[:HALO], flags[:HALO]])
+    tail = jnp.stack([series[frames - HALO :], spikes[frames - HALO :].astype(jnp.float32)])
+    head = jnp.stack([series[:HALO], spikes[:HALO].astype(jnp.float32)])
     before = from_behind(tail, "tm", 1)
     after = from_behind(head, "tm", -1)
     motion_before = from_behind(motion[frames - 1 :], "tm", 1)
-    window = jnp.concatenate([before[0], series, after[0]], axis=0)
-    window_flags = jnp.concatenate([before[1], flags, after[1]], axis=0).astype(jnp.int32)
-    despiked_window = despike_window(window, window_flags)
-    spike_free_series = despiked_window[HALO : HALO + frames]
+    inner = despike_window(series, spikes)
+    edge = 2 * HALO
+    head_window = despike_window(
+        jnp.concatenate([before[0], series[:edge]], axis=0),
+        jnp.concatenate([before[1].astype(jnp.int32), spikes[:edge]], axis=0),
+    )
+    tail_window = despike_window(
+        jnp.concatenate([series[frames - edge :], after[0]], axis=0),
+        jnp.concatenate([spikes[frames - edge :], after[1].astype(jnp.int32)], axis=0),
+    )
+    spike_free_series = jnp.concatenate(
+        [head_window[HALO:edge], inner[HALO : frames - HALO], tail_window[HALO:edge]], axis=0
+    )
+    despiked_window = jnp.concatenate([head_window[:HALO], spike_free_series], axis=0)
 
     rows = despiked_window[HALO - 8 : HALO + frames]
     numer = sum_over_vox(precise_product(rows, tissue.T))

time: 124 us -> 121 us (0.976)
  waiting for transfers between devices: 12.7 us -> 2.35 us
  local copies, waits for them, and re-layouts: 10.5 us -> 13 us
  starting transfers between devices: 15.9 us -> 18.3 us
  other arithmetic: 17.8 us -> 19.4 us
    ppermute x3, waiting for transfers between devices: 9.95 us -> 0.01 us  [from_behind(): return lax.ppermute(block, axis, route)]
    all_to_all x1, starting transfers between devices: 5.46 us -> 7.32 us  [sum_over_vox(): return lax.all_to_all(copies, 'vox', 0, 0, tiled=False).sum(axis=0)]
    convert_element_type x1 -> x2, other arithmetic: 1.4 us -> 0.04 us  [the longest x1 0.02 us: local(): after[1].astype(jnp.int32)]
    mul x4 -> x10, other arithmetic: 5.84 us -> 6.85 us  [despike_window(): kept_list.append(detail * keep_level(flags, level))]
    unnamed x24 -> x30, local copies, waits for them, and re-layouts: 7.7 us -> 8.63 us
  transfers between devices with their start and end apart: 4 -> 4, of which waited for: 4 -> 1; matrix products, arithmetic and copies ran while one was open for 1% -> 7% of each run, Pallas kernels for 0% -> 0%
where the time goes in v2:
time: 121 us
  blocking collectives  62.2 us (51%)
  other arithmetic  19.4 us (16%)
  starting transfers between devices  18.3 us (15%)
  local copies, waits for them, and re-layouts  13 us (11%)
  matrix products  4.67 us (4%)
  waiting for transfers between devices  2.35 us (2%)
    all_to_all x1, blocking collectives, sum_over_tm(): owned = lax.all_to_all(parts, 'tm', 0, 0, tiled=False).sum(axis=0)  34.6 us
    all_to_all x1, blocking collectives, sum_over_tm(): gathered = lax.all_to_all(copies, 'tm', 0, 0, tiled=False)  27.6 us
    ppermute x3, starting transfers between devices, from_behind(): return lax.ppermute(block, axis, route)  11 us
    unnamed x30, local copies, waits for them, and re-layouts  8.63 us
    all_to_all x1, starting transfers between devices, sum_over_vox(): return lax.all_to_all(copies, 'vox', 0, 0, tiled=False).sum(axis=0)  7.32 us
    mul x10, other arithmetic, despike_window(): kept_list.append(detail * keep_level(flags, level))  6.85 us
    another operation x3, other arithmetic, local(): factor = jnp.linalg.cholesky(gram_matrix)  3.96 us
    dot_general x4, matrix products, precise_product(): jnp.dot(left, right, precision=lax.Precision.HIGHEST, preferred_element_t...  3.79 us
  transfers between devices with their start and end apart: 4, of which 1 were waited for; matrix products, arithmetic and copies ran while one was open for 7% of the time, Pallas kernels for 0%

profile of v2, /device:TPU:64, one launch (start us, length us, event | category | flops | bytes accessed | tf_op | source)
XLA Modules:
  0.0 121.0 jit_solution(12521373604104037749)
XLA Ops:
  0.0 1.1 slice_bitcast_fusion.3
  1.1 1.0 convert_bitcast_fusion.1
  2.1 2.1 %collective-permute-start.1 = (f32[2,16,2048]{2,1,0:T(8,128)S(1)}, f32[2,16,2048]{2,1,0:T(8,128)S(1)}, u32[]{:S(2)}, u32[]{:S(2)}) collective-permute-start(f32[2,16,2048]{2,1,0:T(8,128)S(1)} %pad_maximum_fusion.23), channel_id=1, source_target_pairs={{1,0},{2,1},{3,2},{4,3},{5,4},{6,5},{7,6},{8,7},{9,8},{10,9},{11,1... | collective-permute-start | bytes 786440 | tf_op jit(solution)/shard_map/ppermute | solution.py:13
  4.3 3.8 %collective-permute-start = (f32[2,16,2048]{2,1,0:T(8,128)S(1)}, f32[2,16,2048]{2,1,0:T(8,128)S(1)}, u32[]{:S(2)}, u32[]{:S(2)}) collective-permute-start(f32[2,16,2048]{2,1,0:T(8,128)S(1)} %pad_maximum_fusion.22), channel_id=1, source_target_pairs={{15,0},{0,1},{1,2},{2,3},{3,4},{4,5},{5,6},{6,7},{7,8},{8,9},{9,10... | collective-permute-start | bytes 786440 | tf_op jit(solution)/shard_map/ppermute | solution.py:13
  8.2 0.7 add_multiply_fusion.3
  8.9 1.3 %fusion.15 = (f32[128,2048]{1,0:T(8,128)S(1)}, f32[128,2048]{1,0:T(8,128)S(1)}) fusion(f32[128,2048]{1,0:T(8,128)S(1)} %get-tuple-element.11, f32[126,2048]{1,0:T(8,128)S(1)} %bitcast.62, f32[2,2048]{1,0:T(2,128)S(1)} %slice.475, s32[128,2048]{1,0:T(8,128)S(1)} %copy-done.1), kind=kLoop, calls=%fused_computation.38 | loop fusion | flops 8912896 | bytes 5242880 | tf_op jit(solution)/shard_map/mul | solution.py:31
  10.2 1.3 %fusion.11 = (f32[128,2048]{1,0:T(8,128)S(1)}, f32[128,2048]{1,0:T(8,128)S(1)}) fusion(f32[128,2048]{1,0:T(8,128)S(1)} %get-tuple-element.10, f32[124,2048]{1,0:T(8,128)S(1)} %bitcast.61, f32[4,2048]{1,0:T(4,128)S(1)} %slice.477, s32[128,2048]{1,0:T(8,128)S(1)} %copy-done.1), kind=kLoop, calls=%fused_computation.34 | loop fusion | flops 8912896 | bytes 5242880 | tf_op jit(solution)/shard_map/mul | solution.py:31
  11.6 1.2 fusion.6
  13.0 0.3 fusion.20
  13.5 0.9 copy-done.2
  14.4 1.1 copy-done.3
  15.6 0.3 fusion.22
  16.0 0.9 copy-done.4
  17.0 1.1 copy-done.5
  18.1 0.3 fusion.24
  18.6 0.9 copy-done.7
  19.5 1.1 copy-done.8
  20.7 0.2 fusion.28
  21.1 0.3 add_multiply_fusion.7
  21.4 0.5 fusion.63
  21.9 0.5 fusion.59
  22.5 0.5 fusion.54
  23.0 0.3 fusion.49
  23.3 0.5 fusion.46
  23.8 0.5 fusion.42
  24.4 0.5 fusion.37
  25.6 0.6 copy-done.9
  26.7 0.9 copy-done.10
  27.6 0.3 fusion.74
  28.0 1.0 fusion
  29.0 0.8 reshape.65
  29.8 7.3 %all-to-all-start = ((f32[32,1,408]{2,1,0:T(1,128)}), f32[32,1,408]{2,1,0:T(1,128)S(1)}, u32[]{:S(2)}, u32[]{:S(2)}) async-start(f32[32,1,408]{2,1,0:T(1,128)} %reshape.65), calls=%async_computation | async-start | bytes 131072 | tf_op jit(solution)/shard_map/all_to_all | solution.py:45
  37.2 5.0 %collective-permute-start.2 = (f32[1,6]{0,1:T(8,128)S(1)}, f32[1,6]{0,1:T(8,128)S(1)}, u32[]{:S(2)}, u32[]{:S(2)}) collective-permute-start(f32[1,6]{0,1:T(8,128)S(1)} %slice.441), channel_id=1, source_target_pairs={{15,0},{0,1},{1,2},{2,3},{3,4},{4,5},{5,6},{6,7},{7,8},{8,9},{9,10... | collective-permute-start | bytes 80 | tf_op jit(solution)/shard_map/ppermute | solution.py:13
  42.3 2.3 %all-to-all-done = f32[32,1,408]{2,1,0:T(1,128)S(1)} async-done(((f32[32,1,408]{2,1,0:T(1,128)}), f32[32,1,408]{2,1,0:T(1,128)S(1)}, u32[]{:S(2)}, u32[]{:S(2)}) %all-to-all-start) | async-done | bytes 52256 | tf_op jit(solution)/shard_map/all_to_all | solution.py:45
  44.6 0.5 broadcast.277
  45.1 0.8 reduce.6
  46.4 0.4 concatenate.218
  46.8 0.2 fusion.105
  47.1 0.7 fusion.29
  48.0 34.6 %all_to_all.15 = f32[16,37,128]{2,1,0:T(8,128)S(1)} all-to-all(f32[16,37,128]{2,1,0:T(8,128)S(1)} %maximum_bitcast_fusion), channel_id=1, replica_groups=mesh['vox'=32,'tm'=16] {'tm'}, dimensions={0} | all-to-all | bytes 606208 | tf_op jit(solution)/shard_map/all_to_all | solution.py:52
  82.7 27.6 %all_to_all.16 = f32[16,37,128]{2,1,0:T(8,128)S(1)} all-to-all(f32[16,37,128]{2,1,0:T(8,128)S(1)} %broadcast_in_dim.9), channel_id=1, replica_groups=mesh['vox'=32,'tm'=16] {'tm'}, dimensions={0} | all-to-all | bytes 606208 | tf_op jit(solution)/shard_map/all_to_all | solution.py:54
  110.5 3.3 %cholesky.16 = f32[36,36]{1,0:T(8,128)S(1)} custom-call(f32[36,36]{1,0:T(8,128)S(1)} %fusion.96), custom_call_target="Cholesky" | custom-call | tf_op jit(solution)/shard_map/jit(cholesky)/cholesky | solution.py:109
  113.8 0.6 compare_reduce_fusion
  114.5 0.7 fusion.91
  115.1 2.8 %custom-call.10 = f32[1,36,36]{1,2,0:T(8,128)S(1)} custom-call(f32[1,36,36]{2,1,0:T(8,128)S(1)} %fusion.91), custom_call_target="InvertDiagBlocksLowerTriangular" | custom-call | tf_op jit(solution)/shard_map/jit(_cho_solve)/triangular_solve | solution.py:110
  118.1 0.5 fusion.94
  118.6 0.4 fusion.92
  119.0 2.0 %convolution_subtract_fusion = f32[128,2048]{1,0:T(8,128)} fusion(f32[128,36]{0,1:T(8,128)S(1)} %concatenate.218, f32[36,2048]{1,0:T(8,128)S(1)} %fusion.92, f32[16,2048]{1,0:T(8,128)S(1)} %fusion.88, f32[96,2048]{1,0:T(8,128)S(1)} %fusion.28, f32[16,2048]{1,0:T(8,128)S(1)} %slice.474), kind=kOutput, calls=%fused_computation | convolution fusion | flops 114032640 | bytes 2410496 | tf_op jit(solution)/shard_map/dot_general | solution.py:17
  (127 shorter events, 3.8 us)
Async XLA Ops:
  0.0 27.9 %copy-start = (f32[3,2048]{1,0:T(4,128)S(1)}, f32[3,2048]{1,0:T(4,128)}, u32[]{:S(2)}) copy-start(f32[3,2048]{1,0:T(4,128)} %param.7) | copy-start | bytes 73732
  0.0 8.1 %copy-start.6 = (f32[128,2048]{1,0:T(8,128)S(1)}, f32[128,2048]{1,0:T(8,128)}, u32[]{:S(2)}) copy-start(f32[128,2048]{1,0:T(8,128)} %param.4) | copy-start | bytes 3145732
  2.1 6.1 %copy-start.1 = (s32[128,2048]{1,0:T(8,128)S(1)}, s32[128,2048]{1,0:T(8,128)}, u32[]{:S(2)}) copy-start(s32[128,2048]{1,0:T(8,128)} %param.5) | copy-start | bytes 3145732
  2.1 18.9 %collective-permute-start.1 = (f32[2,16,2048]{2,1,0:T(8,128)S(1)}, f32[2,16,2048]{2,1,0:T(8,128)S(1)}, u32[]{:S(2)}, u32[]{:S(2)}) collective-permute-start(f32[2,16,2048]{2,1,0:T(8,128)S(1)} %pad_maximum_fusion.23), channel_id=1, source_target_pairs={{1,0},{2,1},{3,2},{4,3},{5,4},{6,5},{7,6},{8,7},{9,8},{10,9},{11,1... | collective-permute-start | bytes 786440 | tf_op jit(solution)/shard_map/ppermute | solution.py:13
  4.3 16.7 %collective-permute-start = (f32[2,16,2048]{2,1,0:T(8,128)S(1)}, f32[2,16,2048]{2,1,0:T(8,128)S(1)}, u32[]{:S(2)}, u32[]{:S(2)}) collective-permute-start(f32[2,16,2048]{2,1,0:T(8,128)S(1)} %pad_maximum_fusion.22), channel_id=1, source_target_pairs={{15,0},{0,1},{1,2},{2,3},{3,4},{4,5},{5,6},{6,7},{7,8},{8,9},{9,10... | collective-permute-start | bytes 786440 | tf_op jit(solution)/shard_map/ppermute | solution.py:13
  13.4 1.0 copy-start.2
  14.3 1.2 %copy-start.3 = (f32[128,2048]{1,0:T(8,128)S(1)}, f32[128,2048]{1,0:T(8,128)}, u32[]{:S(2)}) copy-start(f32[128,2048]{1,0:T(8,128)} %copy-done.2) | copy-start | bytes 3145732
  14.3 1.2 %slice-start = ((f32[128,2048]{1,0:T(8,128)}), f32[4,2048]{1,0:T(4,128)S(1)}, s32[]{:S(2)}) async-start(f32[128,2048]{1,0:T(8,128)} %copy-done.2), calls=%async_computation.3 | async-start | bytes 65536 | tf_op jit(solution)/shard_map/jit(_roll_static)/slice | solution.py:36
  15.9 1.0 copy-start.4
  16.9 1.2 %copy-start.5 = (f32[128,2048]{1,0:T(8,128)S(1)}, f32[128,2048]{1,0:T(8,128)}, u32[]{:S(2)}) copy-start(f32[128,2048]{1,0:T(8,128)} %copy-done.4) | copy-start | bytes 3145732
  16.9 1.2 %slice-start.1 = ((f32[128,2048]{1,0:T(8,128)}), f32[2,2048]{1,0:T(2,128)S(1)}, s32[]{:S(2)}) async-start(f32[128,2048]{1,0:T(8,128)} %copy-done.4), calls=%async_computation.4 | async-start | bytes 32768 | tf_op jit(solution)/shard_map/jit(_roll_static)/slice | solution.py:36
  18.5 1.0 copy-start.7
  19.4 1.2 %copy-start.8 = (f32[128,2048]{1,0:T(8,128)S(1)}, f32[128,2048]{1,0:T(8,128)}, u32[]{:S(2)}) copy-start(f32[128,2048]{1,0:T(8,128)} %copy-done.7) | copy-start | bytes 3145732
  19.4 1.2 %slice-start.2 = ((f32[128,2048]{1,0:T(8,128)}), f32[1,2048]{1,0:T(1,128)S(1)}, s32[]{:S(2)}) async-start(f32[128,2048]{1,0:T(8,128)} %copy-done.7), calls=%async_computation.5 | async-start | bytes 16384 | tf_op jit(solution)/shard_map/jit(_roll_static)/slice | solution.py:36
  25.4 0.7 copy-start.9
  26.6 1.0 copy-start.10
  26.6 1.0 slice-start.3
  27.9 9.2 %copy-start.11 = (f32[128,6]{0,1:T(8,128)S(1)}, f32[128,6]{0,1:T(8,128)}, u32[]{:S(2)}) copy-start(f32[128,6]{0,1:T(8,128)} %param.6) | copy-start | bytes 9220
  29.8 14.8 %all-to-all-start = ((f32[32,1,408]{2,1,0:T(1,128)}), f32[32,1,408]{2,1,0:T(1,128)S(1)}, u32[]{:S(2)}, u32[]{:S(2)}) async-start(f32[32,1,408]{2,1,0:T(1,128)} %reshape.65), calls=%async_computation | async-start | bytes 131072 | tf_op jit(solution)/shard_map/all_to_all | solution.py:45
  37.2 9.1 %collective-permute-start.2 = (f32[1,6]{0,1:T(8,128)S(1)}, f32[1,6]{0,1:T(8,128)S(1)}, u32[]{:S(2)}, u32[]{:S(2)}) collective-permute-start(f32[1,6]{0,1:T(8,128)S(1)} %slice.441), channel_id=1, source_target_pairs={{15,0},{0,1},{1,2},{2,3},{3,4},{4,5},{5,6},{6,7},{7,8},{8,9},{9,10... | collective-permute-start | bytes 80 | tf_op jit(solution)/shard_map/ppermute | solution.py:13

commit v3 on v2

--- a/solution.py
+++ b/solution.py
@@ -45,14 +45,20 @@
     return lax.all_to_all(copies, "vox", 0, 0, tiled=False).sum(axis=0)
 
 
-def sum_over_tm(block):
+def sum_over_tm(block, pieces=4):
     n = lax.axis_size("tm")
     rows, cols = block.shape
-    parts = block.reshape(rows, n, cols // n).transpose(1, 0, 2)
-    owned = lax.all_to_all(parts, "tm", 0, 0, tiled=False).sum(axis=0)
-    copies = jnp.broadcast_to(owned, (n,) + owned.shape)
-    gathered = lax.all_to_all(copies, "tm", 0, 0, tiled=False)
-    return gathered.transpose(1, 0, 2).reshape(rows, cols)
+    width = cols // n
+    parts = block.reshape(rows, n, width).transpose(1, 0, 2)
+    step = width // pieces
+    owned = [
+        lax.all_to_all(parts[:, :, q * step : (q + 1) * step], "tm", 0, 0, tiled=False).sum(axis=0)
+        for q in range(pieces)
+    ]
+    gathered = [
+        lax.all_to_all(jnp.broadcast_to(o, (n,) + o.shape), "tm", 0, 0, tiled=False) for o in owned
+    ]
+    return jnp.concatenate(gathered, axis=2).transpose(1, 0, 2).reshape(rows, cols)
 
 
 def local(series, spikes, motion, tissue):

time: 121 us -> 205 us (1.69)
  the two profiles are of different devices: /device:TPU:64 before, /device:TPU:32 now
where the time goes in v3:
time: 205 us; the launch traced here: 204 us
  waiting for transfers between devices  88.6 us (43%)
  starting transfers between devices  59.6 us (29%)
  other arithmetic  25.7 us (13%)
  local copies, waits for them, and re-layouts  24 us (12%)
  matrix products  4.68 us (2%)
    all_to_all x4, waiting for transfers between devices, sum_over_tm(): lax.all_to_all(parts[:, :, q * step:(q + 1) * step], 'tm', 0, 0, tiled=Fa...  43.2 us
    all_to_all x4, waiting for transfers between devices, sum_over_tm(): lax.all_to_all(jnp.broadcast_to(o, (n,) + o.shape), 'tm', 0, 0, tiled=False)  39.8 us
    all_to_all x4, starting transfers between devices, sum_over_tm(): lax.all_to_all(parts[:, :, q * step:(q + 1) * step], 'tm', 0, 0, tiled=Fa...  25.9 us
    unnamed x50, local copies, waits for them, and re-layouts  18.5 us
    all_to_all x4, starting transfers between devices, sum_over_tm(): lax.all_to_all(jnp.broadcast_to(o, (n,) + o.shape), 'tm', 0, 0, tiled=False)  16.6 us
    ppermute x3, starting transfers between devices, from_behind(): return lax.ppermute(block, axis, route)  12.5 us
    mul x10, other arithmetic, despike_window(): kept_list.append(detail * keep_level(flags, level))  6.85 us
    all_to_all x1, starting transfers between devices, sum_over_vox(): return lax.all_to_all(copies, 'vox', 0, 0, tiled=False).sum(axis=0)  4.57 us
  transfers between devices with their start and end apart: 12, of which 10 were waited for; matrix products, arithmetic and copies ran while one was open for 11% of the time, Pallas kernels for 0%

profile of v3, /device:TPU:32, one launch (start us, length us, event | category | flops | bytes accessed | tf_op | source)
XLA Modules:
  0.0 203.9 jit_solution(1649628889549687635)
XLA Ops:
  0.0 1.1 slice_bitcast_fusion.3
  1.1 1.0 convert_bitcast_fusion.1
  2.1 7.5 %collective-permute-start.1 = (f32[2,16,2048]{2,1,0:T(8,128)S(1)}, f32[2,16,2048]{2,1,0:T(8,128)S(1)}, u32[]{:S(2)}, u32[]{:S(2)}) collective-permute-start(f32[2,16,2048]{2,1,0:T(8,128)S(1)} %pad_maximum_fusion.24), channel_id=1, source_target_pairs={{1,0},{2,1},{3,2},{4,3},{5,4},{6,5},{7,6},{8,7},{9,8},{10,9},{11,1... | collective-permute-start | bytes 786440 | tf_op jit(solution)/shard_map/ppermute | solution.py:13
  9.6 1.9 collective-permute-start
  12.4 1.3 fusion.15
  13.7 1.3 fusion.11
  15.0 1.2 fusion.6
  16.9 0.9 copy-done.2
  17.9 1.1 copy-done.3
  19.5 0.9 copy-done.4
  20.4 1.1 copy-done.5
  22.0 0.9 copy-done.7
  23.0 1.1 copy-done.8
  30.1 0.9 copy-done.10
  31.4 1.0 fusion
  32.4 0.8 reshape.65
  33.2 4.6 %all-to-all-start = ((f32[32,1,408]{2,1,0:T(1,128)}), f32[32,1,408]{2,1,0:T(1,128)S(1)}, u32[]{:S(2)}, u32[]{:S(2)}) async-start(f32[32,1,408]{2,1,0:T(1,128)} %reshape.65), calls=%async_computation | async-start | bytes 131072 | tf_op jit(solution)/shard_map/all_to_all | solution.py:45
  37.9 3.1 %collective-permute-start.2 = (f32[1,6]{0,1:T(8,128)S(1)}, f32[1,6]{0,1:T(8,128)S(1)}, u32[]{:S(2)}, u32[]{:S(2)}) collective-permute-start(f32[1,6]{0,1:T(8,128)S(1)} %slice.453), channel_id=1, source_target_pairs={{15,0},{0,1},{1,2},{2,3},{3,4},{4,5},{5,6},{6,7},{7,8},{8,9},{9,10... | collective-permute-start | bytes 80 | tf_op jit(solution)/shard_map/ppermute | solution.py:13
  41.1 4.2 %all-to-all-done = f32[32,1,408]{2,1,0:T(1,128)S(1)} async-done(((f32[32,1,408]{2,1,0:T(1,128)}), f32[32,1,408]{2,1,0:T(1,128)S(1)}, u32[]{:S(2)}, u32[]{:S(2)}) %all-to-all-start) | async-done | bytes 52256 | tf_op jit(solution)/shard_map/all_to_all | solution.py:45
  46.9 1.4 collective-permute-done.2
  50.3 0.9 reshape.67
  51.3 13.1 %all-to-all-start.7 = ((f32[16,1,1184]{2,1,0:T(1,128)}), f32[16,1,1184]{2,1,0:T(1,128)S(1)}, u32[]{:S(2)}, u32[]{:S(2)}) async-start(f32[16,1,1184]{2,1,0:T(1,128)} %reshape.67), calls=%async_computation.7 | async-start | bytes 163840 | tf_op jit(solution)/shard_map/all_to_all | solution.py:55
  64.4 0.9 reshape.79
  65.3 11.7 %all-to-all-done.7 = f32[16,1,1184]{2,1,0:T(1,128)S(1)} async-done(((f32[16,1,1184]{2,1,0:T(1,128)}), f32[16,1,1184]{2,1,0:T(1,128)S(1)}, u32[]{:S(2)}, u32[]{:S(2)}) %all-to-all-start.7) | async-done | bytes 75808 | tf_op jit(solution)/shard_map/all_to_all | solution.py:55
  77.0 4.3 %all-to-all-start.1 = ((f32[16,1,1184]{2,1,0:T(1,128)}), f32[16,1,1184]{2,1,0:T(1,128)S(1)}, u32[]{:S(2)}, u32[]{:S(2)}) async-start(f32[16,1,1184]{2,1,0:T(1,128)} %reshape.79), calls=%async_computation.1 | async-start | bytes 163840 | tf_op jit(solution)/shard_map/all_to_all | solution.py:55
  81.3 0.9 reshape.71
  82.2 11.1 %all-to-all-done.1 = f32[16,1,1184]{2,1,0:T(1,128)S(1)} async-done(((f32[16,1,1184]{2,1,0:T(1,128)}), f32[16,1,1184]{2,1,0:T(1,128)S(1)}, u32[]{:S(2)}, u32[]{:S(2)}) %all-to-all-start.1) | async-done | bytes 75808 | tf_op jit(solution)/shard_map/all_to_all | solution.py:55
  93.4 4.3 %all-to-all-start.5 = ((f32[16,1,1184]{2,1,0:T(1,128)}), f32[16,1,1184]{2,1,0:T(1,128)S(1)}, u32[]{:S(2)}, u32[]{:S(2)}) async-start(f32[16,1,1184]{2,1,0:T(1,128)} %reshape.71), calls=%async_computation.5 | async-start | bytes 163840 | tf_op jit(solution)/shard_map/all_to_all | solution.py:55
  97.7 0.9 reshape.75
  99.6 10.2 %all-to-all-done.5 = f32[16,1,1184]{2,1,0:T(1,128)S(1)} async-done(((f32[16,1,1184]{2,1,0:T(1,128)}), f32[16,1,1184]{2,1,0:T(1,128)S(1)}, u32[]{:S(2)}, u32[]{:S(2)}) %all-to-all-start.5) | async-done | bytes 75808 | tf_op jit(solution)/shard_map/all_to_all | solution.py:55
  109.8 4.2 %all-to-all-start.3 = ((f32[16,1,1184]{2,1,0:T(1,128)}), f32[16,1,1184]{2,1,0:T(1,128)S(1)}, u32[]{:S(2)}, u32[]{:S(2)}) async-start(f32[16,1,1184]{2,1,0:T(1,128)} %reshape.75), calls=%async_computation.3 | async-start | bytes 163840 | tf_op jit(solution)/shard_map/all_to_all | solution.py:55
  115.2 0.9 reshape.69
  116.1 10.1 %all-to-all-done.3 = f32[16,1,1184]{2,1,0:T(1,128)S(1)} async-done(((f32[16,1,1184]{2,1,0:T(1,128)}), f32[16,1,1184]{2,1,0:T(1,128)S(1)}, u32[]{:S(2)}, u32[]{:S(2)}) %all-to-all-start.3) | async-done | bytes 75808 | tf_op jit(solution)/shard_map/all_to_all | solution.py:55
  126.3 4.2 %all-to-all-start.8 = ((f32[16,1,1184]{2,1,0:T(1,128)}), f32[16,1,1184]{2,1,0:T(1,128)S(1)}, u32[]{:S(2)}, u32[]{:S(2)}) async-start(f32[16,1,1184]{2,1,0:T(1,128)} %reshape.69), calls=%async_computation.8 | async-start | bytes 163840 | tf_op jit(solution)/shard_map/all_to_all | solution.py:59
  131.6 0.9 reshape.81
  132.5 10.1 %all-to-all-done.8 = f32[16,1,1184]{2,1,0:T(1,128)S(1)} async-done(((f32[16,1,1184]{2,1,0:T(1,128)}), f32[16,1,1184]{2,1,0:T(1,128)S(1)}, u32[]{:S(2)}, u32[]{:S(2)}) %all-to-all-start.8) | async-done | bytes 75808 | tf_op jit(solution)/shard_map/all_to_all | solution.py:59
  142.6 4.1 %all-to-all-start.2 = ((f32[16,1,1184]{2,1,0:T(1,128)}), f32[16,1,1184]{2,1,0:T(1,128)S(1)}, u32[]{:S(2)}, u32[]{:S(2)}) async-start(f32[16,1,1184]{2,1,0:T(1,128)} %reshape.81), calls=%async_computation.2 | async-start | bytes 163840 | tf_op jit(solution)/shard_map/all_to_all | solution.py:59
  147.9 0.9 reshape.73
  148.8 10.1 %all-to-all-done.2 = f32[16,1,1184]{2,1,0:T(1,128)S(1)} async-done(((f32[16,1,1184]{2,1,0:T(1,128)}), f32[16,1,1184]{2,1,0:T(1,128)S(1)}, u32[]{:S(2)}, u32[]{:S(2)}) %all-to-all-start.2) | async-done | bytes 75808 | tf_op jit(solution)/shard_map/all_to_all | solution.py:59
  158.9 4.1 %all-to-all-start.6 = ((f32[16,1,1184]{2,1,0:T(1,128)}), f32[16,1,1184]{2,1,0:T(1,128)S(1)}, u32[]{:S(2)}, u32[]{:S(2)}) async-start(f32[16,1,1184]{2,1,0:T(1,128)} %reshape.73), calls=%async_computation.6 | async-start | bytes 163840 | tf_op jit(solution)/shard_map/all_to_all | solution.py:59
  163.1 0.9 reshape.77
  164.1 11.2 %all-to-all-done.6 = f32[16,1,1184]{2,1,0:T(1,128)S(1)} async-done(((f32[16,1,1184]{2,1,0:T(1,128)}), f32[16,1,1184]{2,1,0:T(1,128)S(1)}, u32[]{:S(2)}, u32[]{:S(2)}) %all-to-all-start.6) | async-done | bytes 75808 | tf_op jit(solution)/shard_map/all_to_all | solution.py:59
  175.3 4.1 %all-to-all-start.4 = ((f32[16,1,1184]{2,1,0:T(1,128)}), f32[16,1,1184]{2,1,0:T(1,128)S(1)}, u32[]{:S(2)}, u32[]{:S(2)}) async-start(f32[16,1,1184]{2,1,0:T(1,128)} %reshape.77), calls=%async_computation.4 | async-start | bytes 163840 | tf_op jit(solution)/shard_map/all_to_all | solution.py:59
  180.7 0.8 reduce.14
  183.3 8.3 %all-to-all-done.4 = f32[16,1,1184]{2,1,0:T(1,128)S(1)} async-done(((f32[16,1,1184]{2,1,0:T(1,128)}), f32[16,1,1184]{2,1,0:T(1,128)S(1)}, u32[]{:S(2)}, u32[]{:S(2)}) %all-to-all-start.4) | async-done | bytes 75808 | tf_op jit(solution)/shard_map/all_to_all | solution.py:59
  193.4 3.3 %cholesky.16 = f32[36,36]{1,0:T(8,128)S(1)} custom-call(f32[36,36]{1,0:T(8,128)S(1)} %fusion.96), custom_call_target="Cholesky" | custom-call | tf_op jit(solution)/shard_map/jit(cholesky)/cholesky | solution.py:115
  198.0 2.8 %custom-call.10 = f32[1,36,36]{1,2,0:T(8,128)S(1)} custom-call(f32[1,36,36]{2,1,0:T(8,128)S(1)} %fusion.91), custom_call_target="InvertDiagBlocksLowerTriangular" | custom-call | tf_op jit(solution)/shard_map/jit(_cho_solve)/triangular_solve | solution.py:116
  201.8 2.0 convolution_subtract_fusion
  (177 shorter events, 23.8 us)
Async XLA Ops:
  0.0 31.4 %copy-start = (f32[3,2048]{1,0:T(4,128)S(1)}, f32[3,2048]{1,0:T(4,128)}, u32[]{:S(2)}) copy-start(f32[3,2048]{1,0:T(4,128)} %param.7) | copy-start | bytes 73732
  0.0 11.6 %copy-start.6 = (f32[128,2048]{1,0:T(8,128)S(1)}, f32[128,2048]{1,0:T(8,128)}, u32[]{:S(2)}) copy-start(f32[128,2048]{1,0:T(8,128)} %param.4) | copy-start | bytes 3145732
  2.1 9.6 %copy-start.1 = (s32[128,2048]{1,0:T(8,128)S(1)}, s32[128,2048]{1,0:T(8,128)}, u32[]{:S(2)}) copy-start(s32[128,2048]{1,0:T(8,128)} %param.5) | copy-start | bytes 3145732
  2.1 22.3 %collective-permute-start.1 = (f32[2,16,2048]{2,1,0:T(8,128)S(1)}, f32[2,16,2048]{2,1,0:T(8,128)S(1)}, u32[]{:S(2)}, u32[]{:S(2)}) collective-permute-start(f32[2,16,2048]{2,1,0:T(8,128)S(1)} %pad_maximum_fusion.24), channel_id=1, source_target_pairs={{1,0},{2,1},{3,2},{4,3},{5,4},{6,5},{7,6},{8,7},{9,8},{10,9},{11,1... | collective-permute-start | bytes 786440 | tf_op jit(solution)/shard_map/ppermute | solution.py:13
  9.6 14.8 %collective-permute-start = (f32[2,16,2048]{2,1,0:T(8,128)S(1)}, f32[2,16,2048]{2,1,0:T(8,128)S(1)}, u32[]{:S(2)}, u32[]{:S(2)}) collective-permute-start(f32[2,16,2048]{2,1,0:T(8,128)S(1)} %pad_maximum_fusion.23), channel_id=1, source_target_pairs={{15,0},{0,1},{1,2},{2,3},{3,4},{4,5},{5,6},{6,7},{7,8},{8,9},{9,10... | collective-permute-start | bytes 786440 | tf_op jit(solution)/shard_map/ppermute | solution.py:13
  16.8 1.0 copy-start.2
  17.8 1.2 copy-start.3
  17.8 1.2 slice-start
  19.4 1.0 copy-start.4
  20.3 1.2 copy-start.5
  20.3 1.2 slice-start.1
  21.9 1.0 copy-start.7
  22.9 1.2 copy-start.8
  22.9 1.2 slice-start.2
  28.9 0.7 copy-start.9
  30.0 1.0 copy-start.10
  30.0 1.0 slice-start.3
  31.4 6.5 %copy-start.11 = (f32[128,6]{0,1:T(8,128)S(1)}, f32[128,6]{0,1:T(8,128)}, u32[]{:S(2)}) copy-start(f32[128,6]{0,1:T(8,128)} %param.6) | copy-start | bytes 9220
  33.2 12.1 %all-to-all-start = ((f32[32,1,408]{2,1,0:T(1,128)}), f32[32,1,408]{2,1,0:T(1,128)S(1)}, u32[]{:S(2)}, u32[]{:S(2)}) async-start(f32[32,1,408]{2,1,0:T(1,128)} %reshape.65), calls=%async_computation | async-start | bytes 131072 | tf_op jit(solution)/shard_map/all_to_all | solution.py:45
  37.9 10.4 %collective-permute-start.2 = (f32[1,6]{0,1:T(8,128)S(1)}, f32[1,6]{0,1:T(8,128)S(1)}, u32[]{:S(2)}, u32[]{:S(2)}) collective-permute-start(f32[1,6]{0,1:T(8,128)S(1)} %slice.453), channel_id=1, source_target_pairs={{15,0},{0,1},{1,2},{2,3},{3,4},{4,5},{5,6},{6,7},{7,8},{8,9},{9,10... | collective-permute-start | bytes 80 | tf_op jit(solution)/shard_map/ppermute | solution.py:13
  51.3 25.7 %all-to-all-start.7 = ((f32[16,1,1184]{2,1,0:T(1,128)}), f32[16,1,1184]{2,1,0:T(1,128)S(1)}, u32[]{:S(2)}, u32[]{:S(2)}) async-start(f32[16,1,1184]{2,1,0:T(1,128)} %reshape.67), calls=%async_computation.7 | async-start | bytes 163840 | tf_op jit(solution)/shard_map/all_to_all | solution.py:55
  77.0 16.3 %all-to-all-start.1 = ((f32[16,1,1184]{2,1,0:T(1,128)}), f32[16,1,1184]{2,1,0:T(1,128)S(1)}, u32[]{:S(2)}, u32[]{:S(2)}) async-start(f32[16,1,1184]{2,1,0:T(1,128)} %reshape.79), calls=%async_computation.1 | async-start | bytes 163840 | tf_op jit(solution)/shard_map/all_to_all | solution.py:55
  93.4 16.5 %all-to-all-start.5 = ((f32[16,1,1184]{2,1,0:T(1,128)}), f32[16,1,1184]{2,1,0:T(1,128)S(1)}, u32[]{:S(2)}, u32[]{:S(2)}) async-start(f32[16,1,1184]{2,1,0:T(1,128)} %reshape.71), calls=%async_computation.5 | async-start | bytes 163840 | tf_op jit(solution)/shard_map/all_to_all | solution.py:55
  109.8 16.4 %all-to-all-start.3 = ((f32[16,1,1184]{2,1,0:T(1,128)}), f32[16,1,1184]{2,1,0:T(1,128)S(1)}, u32[]{:S(2)}, u32[]{:S(2)}) async-start(f32[16,1,1184]{2,1,0:T(1,128)} %reshape.75), calls=%async_computation.3 | async-start | bytes 163840 | tf_op jit(solution)/shard_map/all_to_all | solution.py:55
  126.3 16.4 %all-to-all-start.8 = ((f32[16,1,1184]{2,1,0:T(1,128)}), f32[16,1,1184]{2,1,0:T(1,128)S(1)}, u32[]{:S(2)}, u32[]{:S(2)}) async-start(f32[16,1,1184]{2,1,0:T(1,128)} %reshape.69), calls=%async_computation.8 | async-start | bytes 163840 | tf_op jit(solution)/shard_map/all_to_all | solution.py:59
  142.6 16.3 %all-to-all-start.2 = ((f32[16,1,1184]{2,1,0:T(1,128)}), f32[16,1,1184]{2,1,0:T(1,128)S(1)}, u32[]{:S(2)}, u32[]{:S(2)}) async-start(f32[16,1,1184]{2,1,0:T(1,128)} %reshape.81), calls=%async_computation.2 | async-start | bytes 163840 | tf_op jit(solution)/shard_map/all_to_all | solution.py:59
  158.9 16.3 %all-to-all-start.6 = ((f32[16,1,1184]{2,1,0:T(1,128)}), f32[16,1,1184]{2,1,0:T(1,128)S(1)}, u32[]{:S(2)}, u32[]{:S(2)}) async-start(f32[16,1,1184]{2,1,0:T(1,128)} %reshape.73), calls=%async_computation.6 | async-start | bytes 163840 | tf_op jit(solution)/shard_map/all_to_all | solution.py:59
  175.3 16.3 %all-to-all-start.4 = ((f32[16,1,1184]{2,1,0:T(1,128)}), f32[16,1,1184]{2,1,0:T(1,128)S(1)}, u32[]{:S(2)}, u32[]{:S(2)}) async-start(f32[16,1,1184]{2,1,0:T(1,128)} %reshape.77), calls=%async_computation.4 | async-start | bytes 163840 | tf_op jit(solution)/shard_map/all_to_all | solution.py:59

commit v4 on v1

--- a/solution.py
+++ b/solution.py
@@ -21,21 +21,23 @@
     return 1.0 - (spikes // 2**level % 2).astype(jnp.float32)
 
 
-def despike_window(window, flags):
+def despike_trimmed(window, flags):
+    length = window.shape[0]
     approx = window
+    start = 0
     kept_list = []
     for level in range(LEVELS):
         shift_rows = 2**level
-        lagged = jnp.roll(approx, shift_rows, axis=0)
-        detail = (approx - lagged) * 0.5
-        kept_list.append(detail * keep_level(flags, level))
-        approx = (approx + lagged) * 0.5
+        current, lagged = approx[shift_rows:], approx[:-shift_rows]
+        start += shift_rows
+        keep = keep_level(flags[start:], level)
+        kept_list.append((start, (current - lagged) * 0.5 * keep))
+        approx = (current + lagged) * 0.5
     for level in range(LEVELS - 1, -1, -1):
         shift_rows = 2**level
-        kept = kept_list[level]
-        lead_approx = jnp.roll(approx, -shift_rows, axis=0)
-        lead_kept = jnp.roll(kept, -shift_rows, axis=0)
-        approx = (approx + lead_approx) * 0.5 + (kept - lead_kept) * 0.5
+        kept_start, kept = kept_list[level]
+        kept = kept[start - kept_start : start - kept_start + approx.shape[0]]
+        approx = (approx[:-shift_rows] + approx[shift_rows:]) * 0.5 + (kept[:-shift_rows] - kept[shift_rows:]) * 0.5
     return approx
 
 
@@ -57,16 +59,25 @@
 
 def local(series, spikes, motion, tissue):
     frames = series.shape[0]
-    flags = spikes.astype(jnp.float32)
-    tail = jnp.stack([series[frames - HALO :], flags[frames - HALO :]])
-    head = jnp.stack([series[:HALO], flags[:HALO]])
+    voxels = series.shape[1]
+    motion_row = jnp.pad(motion[frames - 1 :], ((0, 7), (0, voxels - motion.shape[1])))
+    tail = jnp.concatenate([series[frames - HALO :], spikes[frames - HALO :].astype(jnp.float32), motion_row], axis=0)
+    head = jnp.concatenate([series[:HALO], spikes[:HALO].astype(jnp.float32)], axis=0)
     before = from_behind(tail, "tm", 1)
     after = from_behind(head, "tm", -1)
-    motion_before = from_behind(motion[frames - 1 :], "tm", 1)
-    window = jnp.concatenate([before[0], series, after[0]], axis=0)
-    window_flags = jnp.concatenate([before[1], flags, after[1]], axis=0).astype(jnp.int32)
-    despiked_window = despike_window(window, window_flags)
-    spike_free_series = despiked_window[HALO : HALO + frames]
+    motion_before = before[2 * HALO : 2 * HALO + 1, : motion.shape[1]]
+    inner = despike_trimmed(series, spikes)
+    edge = 2 * HALO
+    head_window = despike_trimmed(
+        jnp.concatenate([before[:HALO], series[:edge]], axis=0),
+        jnp.concatenate([before[HALO : 2 * HALO].astype(jnp.int32), spikes[:edge]], axis=0),
+    )
+    tail_window = despike_trimmed(
+        jnp.concatenate([series[frames - edge :], after[:HALO]], axis=0),
+        jnp.concatenate([spikes[frames - edge :], after[HALO:].astype(jnp.int32)], axis=0),
+    )
+    spike_free_series = jnp.concatenate([head_window[1 : HALO + 1], inner[1 : frames - 31], tail_window[1 : HALO + 1]], axis=0)
+    despiked_window = jnp.concatenate([jnp.zeros((HALO - 1, voxels), jnp.float32), head_window[:1], spike_free_series], axis=0)
 
     rows = despiked_window[HALO - 8 : HALO + frames]
     numer = sum_over_vox(precise_product(rows, tissue.T))
@@ -88,7 +99,6 @@
         axis=1,
     )
     terms = nuisance_matrix.shape[1]
-    voxels = series.shape[1]
     gram_matrix = precise_product(nuisance_matrix.T, nuisance_matrix)
     cross_products = precise_product(nuisance_matrix.T, spike_free_series)
     gram_rows = -(-terms * terms // voxels)

time: 124 us -> 114 us (0.919)
  local copies, waits for them, and re-layouts: 10.5 us -> 4.77 us
  waiting for transfers between devices: 12.7 us -> 8.98 us
  starting transfers between devices: 15.9 us -> 12.3 us
  blocking collectives: 61.4 us -> 63.5 us
    ppermute x3 -> x2, waiting for transfers between devices: 9.95 us -> 1.54 us  [from_behind(): return lax.ppermute(block, axis, route)]
    unnamed x24 -> x15, local copies, waits for them, and re-layouts: 7.7 us -> 1.31 us
    all_to_all x1, waiting for transfers between devices: 2.74 us -> 7.44 us  [sum_over_vox(): return lax.all_to_all(copies, 'vox', 0, 0, tiled=False).sum(axis=0)]
    ppermute x3 -> x2, starting transfers between devices: 10.5 us -> 5.97 us  [from_behind(): return lax.ppermute(block, axis, route)]
    mul x4 -> x11, other arithmetic: 5.84 us -> 8.04 us  [despike_trimmed(): approx = (current + lagged) * 0.5]
    all_to_all x1, blocking collectives: 33.8 us -> 35.9 us  [sum_over_tm(): owned = lax.all_to_all(parts, 'tm', 0, 0, tiled=False).sum(axis=0)]
  transfers between devices with their start and end apart: 4 -> 3, of which waited for: 4 -> 2; matrix products, arithmetic and copies ran while one was open for 1% -> 6% of each run, Pallas kernels for 0% -> 0%
where the time goes in v4:
time: 114 us
  blocking collectives  63.5 us (56%)
  other arithmetic  19 us (17%)
  starting transfers between devices  12.3 us (11%)
  waiting for transfers between devices  8.98 us (8%)
  local copies, waits for them, and re-layouts  4.77 us (4%)
  matrix products  4.75 us (4%)
    all_to_all x1, blocking collectives, sum_over_tm(): owned = lax.all_to_all(parts, 'tm', 0, 0, tiled=False).sum(axis=0)  35.9 us
    all_to_all x1, blocking collectives, sum_over_tm(): gathered = lax.all_to_all(copies, 'tm', 0, 0, tiled=False)  27.6 us
    mul x11, other arithmetic, despike_trimmed(): approx = (current + lagged) * 0.5  8.04 us
    all_to_all x1, waiting for transfers between devices, sum_over_vox(): return lax.all_to_all(copies, 'vox', 0, 0, tiled=False).sum(axis=0)  7.44 us
    all_to_all x1, starting transfers between devices, sum_over_vox(): return lax.all_to_all(copies, 'vox', 0, 0, tiled=False).sum(axis=0)  6.34 us
    ppermute x2, starting transfers between devices, from_behind(): return lax.ppermute(block, axis, route)  5.97 us
    another operation x3, other arithmetic, local(): factor = jnp.linalg.cholesky(gram_matrix)  3.96 us
    dot_general x4, matrix products, precise_product(): jnp.dot(left, right, precision=lax.Precision.HIGHEST, preferred_element_t...  3.87 us
  transfers between devices with their start and end apart: 3, of which 2 were waited for; matrix products, arithmetic and copies ran while one was open for 6% of the time, Pallas kernels for 0%

profile of v4, /device:TPU:64, one launch (start us, length us, event | category | flops | bytes accessed | tf_op | source)
XLA Modules:
  0.0 113.8 jit_solution(9565860759172957868)
XLA Ops:
  0.0 1.1 fusion.111
  1.1 1.0 slice_convert_fusion.3
  2.1 2.1 %collective-permute-start.1 = (f32[32,2048]{1,0:T(8,128)S(1)}, f32[32,2048]{1,0:T(8,128)S(1)}, u32[]{:S(2)}, u32[]{:S(2)}) collective-permute-start(f32[32,2048]{1,0:T(8,128)S(1)} %pad_maximum_fusion.10), channel_id=1, source_target_pairs={{1,0},{2,1},{3,2},{4,3},{5,4},{6,5},{7,6},{8,7},{9,8},{10,9},{11,1... | collective-permute-start | bytes 786440 | tf_op jit(solution)/shard_map/ppermute | solution.py:13
  4.4 0.1 copy.32
  4.5 3.8 %collective-permute-start = (f32[40,2048]{1,0:T(8,128)S(1)}, f32[40,2048]{1,0:T(8,128)S(1)}, u32[]{:S(2)}, u32[]{:S(2)}) collective-permute-start(f32[40,2048]{1,0:T(8,128)S(1)} %select_maximum_fusion), channel_id=1, source_target_pairs={{15,0},{0,1},{1,2},{2,3},{3,4},{4,5},{5,6},{6,7},{7,8},{8,9},{9,10... | collective-permute-start | bytes 983048 | tf_op jit(solution)/shard_map/ppermute | solution.py:13
  8.4 0.8 add_multiply_fusion.2
  9.2 1.3 %add_multiply_fusion.1 = (f32[125,2048]{1,0:T(8,128)S(1)}, f32[125,2048]{1,0:T(8,128)S(1)}) fusion(f32[127,2048]{1,0:T(8,128)S(1)} %get-tuple-element.21, s32[128,2048]{1,0:T(8,128)S(1)} %copy-done.1), kind=kLoop, calls=%fused_computation.47 | loop fusion | flops 8448000 | bytes 5120000 | tf_op jit(solution)/shard_map/mul | solution.py:35
  10.5 1.3 %add_multiply_fusion = (f32[121,2048]{1,0:T(8,128)S(1)}, f32[121,2048]{1,0:T(8,128)S(1)}) fusion(f32[125,2048]{1,0:T(8,128)S(1)} %get-tuple-element.19, s32[128,2048]{1,0:T(8,128)S(1)} %copy-done.1), kind=kLoop, calls=%fused_computation.46 | loop fusion | flops 8177664 | bytes 4956160 | tf_op jit(solution)/shard_map/mul | solution.py:35
  11.8 1.2 %add_multiply_fusion.3 = (f32[113,2048]{1,0:T(8,128)S(1)}, f32[113,2048]{1,0:T(8,128)S(1)}) fusion(f32[121,2048]{1,0:T(8,128)S(1)} %get-tuple-element.17, s32[128,2048]{1,0:T(8,128)S(1)} %copy-done.1), kind=kLoop, calls=%fused_computation.57 | loop fusion | flops 7636992 | bytes 4628480 | tf_op jit(solution)/shard_map/mul | solution.py:35
  13.0 0.1 fusion.24
  13.1 0.2 fusion.28
  13.4 0.3 fusion.26
  13.7 0.4 fusion.113
  14.0 0.3 fusion.30
  14.5 0.3 add_multiply_fusion.6
  14.8 0.5 add_multiply_fusion.5
  15.4 1.5 %collective-permute-done = f32[40,2048]{1,0:T(8,128)S(1)} collective-permute-done((f32[40,2048]{1,0:T(8,128)S(1)}, f32[40,2048]{1,0:T(8,128)S(1)}, u32[]{:S(2)}, u32[]{:S(2)}) %collective-permute-start) | collective-permute-done | bytes 327712 | tf_op jit(solution)/shard_map/ppermute | solution.py:13
  16.9 0.3 add_multiply_fusion.9
  17.2 0.5 add_multiply_fusion.8
  17.8 1.0 add_multiply_fusion.4
  18.8 0.4 add_multiply_fusion.10
  19.4 0.4 add_multiply_fusion.11
  20.2 1.0 fusion
  21.3 0.8 reshape.62
  22.1 6.3 %all-to-all-start = ((f32[32,1,408]{2,1,0:T(1,128)}), f32[32,1,408]{2,1,0:T(1,128)S(1)}, u32[]{:S(2)}, u32[]{:S(2)}) async-start(f32[32,1,408]{2,1,0:T(1,128)} %reshape.62), calls=%async_computation | async-start | bytes 131072 | tf_op jit(solution)/shard_map/all_to_all | solution.py:47
  28.5 7.4 %all-to-all-done = f32[32,1,408]{2,1,0:T(1,128)S(1)} async-done(((f32[32,1,408]{2,1,0:T(1,128)}), f32[32,1,408]{2,1,0:T(1,128)S(1)}, u32[]{:S(2)}, u32[]{:S(2)}) %all-to-all-start) | async-done | bytes 52256 | tf_op jit(solution)/shard_map/all_to_all | solution.py:47
  35.9 0.5 broadcast.403
  36.4 0.8 reduce.6
  37.3 0.1 reshape.63
  37.4 0.1 copy.25
  37.7 0.1 copy.27
  37.9 0.4 concatenate.66
  38.4 0.2 fusion.119
  38.5 0.1 reshape.59
  38.6 0.7 fusion.31
  39.4 0.1 copy.29
  39.5 35.9 %all_to_all.15 = f32[16,37,128]{2,1,0:T(8,128)S(1)} all-to-all(f32[16,37,128]{2,1,0:T(8,128)S(1)} %maximum_bitcast_fusion), channel_id=1, replica_groups=mesh['vox'=32,'tm'=16] {'tm'}, dimensions={0} | all-to-all | bytes 606208 | tf_op jit(solution)/shard_map/all_to_all | solution.py:54
  75.5 27.6 %all_to_all.16 = f32[16,37,128]{2,1,0:T(8,128)S(1)} all-to-all(f32[16,37,128]{2,1,0:T(8,128)S(1)} %broadcast_in_dim.13), channel_id=1, replica_groups=mesh['vox'=32,'tm'=16] {'tm'}, dimensions={0} | all-to-all | bytes 606208 | tf_op jit(solution)/shard_map/all_to_all | solution.py:56
  103.1 0.1 reshape.61
  103.2 0.1 copy.30
  103.3 3.3 %cholesky.16 = f32[36,36]{1,0:T(8,128)S(1)} custom-call(f32[36,36]{1,0:T(8,128)S(1)} %fusion.104), custom_call_target="Cholesky" | custom-call | tf_op jit(solution)/shard_map/jit(cholesky)/cholesky | solution.py:110
  106.6 0.6 compare_reduce_fusion
  107.2 0.7 fusion.99
  107.9 2.8 %custom-call.10 = f32[1,36,36]{1,2,0:T(8,128)S(1)} custom-call(f32[1,36,36]{2,1,0:T(8,128)S(1)} %fusion.99), custom_call_target="InvertDiagBlocksLowerTriangular" | custom-call | tf_op jit(solution)/shard_map/jit(_cho_solve)/triangular_solve | solution.py:111
  110.8 0.1 copy.34
  110.9 0.5 fusion.102
  111.4 0.4 fusion.100
  111.8 2.0 %convolution_subtract_fusion = f32[128,2048]{1,0:T(8,128)} fusion(f32[128,36]{0,1:T(8,128)S(1)} %concatenate.66, f32[36,2048]{1,0:T(8,128)S(1)} %fusion.100, f32[16,2048]{1,0:T(8,128)S(1)} %fusion.98, f32[96,2048]{1,0:T(8,128)S(1)} %fusion.30, f32[16,2048]{1,0:T(8,128)S(1)} %slice.519), kind=kOutput, calls=%fused_computation | convolution fusion | flops 114032640 | bytes 2410496 | tf_op jit(solution)/shard_map/dot_general | solution.py:17
  (50 shorter events, 1.5 us)
Async XLA Ops:
  0.0 20.2 %copy-start = (f32[3,2048]{1,0:T(4,128)S(1)}, f32[3,2048]{1,0:T(4,128)}, u32[]{:S(2)}) copy-start(f32[3,2048]{1,0:T(4,128)} %param.7) | copy-start | bytes 73732
  0.0 8.3 %copy-start.2 = (f32[128,2048]{1,0:T(8,128)S(1)}, f32[128,2048]{1,0:T(8,128)}, u32[]{:S(2)}) copy-start(f32[128,2048]{1,0:T(8,128)} %param.4) | copy-start | bytes 3145732
  0.0 4.3 %copy-start.3 = (f32[128,6]{0,1:T(8,128)S(1)}, f32[128,6]{0,1:T(8,128)}, u32[]{:S(2)}) copy-start(f32[128,6]{0,1:T(8,128)} %param.6) | copy-start | bytes 9220
  2.1 6.3 %copy-start.1 = (s32[128,2048]{1,0:T(8,128)S(1)}, s32[128,2048]{1,0:T(8,128)}, u32[]{:S(2)}) copy-start(s32[128,2048]{1,0:T(8,128)} %param.5) | copy-start | bytes 3145732
  2.1 12.3 %collective-permute-start.1 = (f32[32,2048]{1,0:T(8,128)S(1)}, f32[32,2048]{1,0:T(8,128)S(1)}, u32[]{:S(2)}, u32[]{:S(2)}) collective-permute-start(f32[32,2048]{1,0:T(8,128)S(1)} %pad_maximum_fusion.10), channel_id=1, source_target_pairs={{1,0},{2,1},{3,2},{4,3},{5,4},{6,5},{7,6},{8,7},{9,8},{10,9},{11,1... | collective-permute-start | bytes 786440 | tf_op jit(solution)/shard_map/ppermute | solution.py:13
  4.5 12.4 %collective-permute-start = (f32[40,2048]{1,0:T(8,128)S(1)}, f32[40,2048]{1,0:T(8,128)S(1)}, u32[]{:S(2)}, u32[]{:S(2)}) collective-permute-start(f32[40,2048]{1,0:T(8,128)S(1)} %select_maximum_fusion), channel_id=1, source_target_pairs={{15,0},{0,1},{1,2},{2,3},{3,4},{4,5},{5,6},{6,7},{7,8},{8,9},{9,10... | collective-permute-start | bytes 983048 | tf_op jit(solution)/shard_map/ppermute | solution.py:13
  22.1 13.8 %all-to-all-start = ((f32[32,1,408]{2,1,0:T(1,128)}), f32[32,1,408]{2,1,0:T(1,128)S(1)}, u32[]{:S(2)}, u32[]{:S(2)}) async-start(f32[32,1,408]{2,1,0:T(1,128)} %reshape.62), calls=%async_computation | async-start | bytes 131072 | tf_op jit(solution)/shard_map/all_to_all | solution.py:47

commit v5 on v4

--- a/solution.py
+++ b/solution.py
@@ -108,8 +108,8 @@
     cross_products = summed[:terms]
     gram_matrix = summed[terms:].reshape(-1)[: terms * terms].reshape(terms, terms)
     factor = jnp.linalg.cholesky(gram_matrix)
-    beta_estimates = jax.scipy.linalg.cho_solve((factor, True), cross_products)
-    return spike_free_series - precise_product(nuisance_matrix, beta_estimates)
+    weights = jax.scipy.linalg.cho_solve((factor, True), nuisance_matrix.T)
+    return spike_free_series - precise_product(weights.T, cross_products)
 
 
 def solution(mesh):

time: 114 us -> 114 us (level)
  no operation moved by 1% of the time
where the time goes in v5:
time: 114 us; the launch traced here: 113 us
  blocking collectives  63.5 us (56%)
  other arithmetic  19 us (17%)
  starting transfers between devices  12.3 us (11%)
  waiting for transfers between devices  8.98 us (8%)
  local copies, waits for them, and re-layouts  4.75 us (4%)
  matrix products  4.27 us (4%)
    all_to_all x1, blocking collectives, sum_over_tm(): owned = lax.all_to_all(parts, 'tm', 0, 0, tiled=False).sum(axis=0)  35.9 us
    all_to_all x1, blocking collectives, sum_over_tm(): gathered = lax.all_to_all(copies, 'tm', 0, 0, tiled=False)  27.6 us
    mul x11, other arithmetic, despike_trimmed(): approx = (current + lagged) * 0.5  8.04 us
    all_to_all x1, waiting for transfers between devices, sum_over_vox(): return lax.all_to_all(copies, 'vox', 0, 0, tiled=False).sum(axis=0)  7.44 us
    all_to_all x1, starting transfers between devices, sum_over_vox(): return lax.all_to_all(copies, 'vox', 0, 0, tiled=False).sum(axis=0)  6.34 us
    ppermute x2, starting transfers between devices, from_behind(): return lax.ppermute(block, axis, route)  5.97 us
    another operation x3, other arithmetic, local(): factor = jnp.linalg.cholesky(gram_matrix)  3.96 us
    dot_general x4, matrix products, precise_product(): jnp.dot(left, right, precision=lax.Precision.HIGHEST, preferred_element_t...  3.87 us
  transfers between devices with their start and end apart: 3, of which 2 were waited for; matrix products, arithmetic and copies ran while one was open for 6% of the time, Pallas kernels for 0%

profile of v5, /device:TPU:64, one launch (start us, length us, event | category | flops | bytes accessed | tf_op | source)
XLA Modules:
  0.0 113.3 jit_solution(11467206076007348485)
XLA Ops:
  0.0 1.1 fusion.111
  1.1 1.0 slice_convert_fusion.3
  2.1 2.1 %collective-permute-start.1 = (f32[32,2048]{1,0:T(8,128)S(1)}, f32[32,2048]{1,0:T(8,128)S(1)}, u32[]{:S(2)}, u32[]{:S(2)}) collective-permute-start(f32[32,2048]{1,0:T(8,128)S(1)} %pad_maximum_fusion.10), channel_id=1, source_target_pairs={{1,0},{2,1},{3,2},{4,3},{5,4},{6,5},{7,6},{8,7},{9,8},{10,9},{11,1... | collective-permute-start | bytes 786440 | tf_op jit(solution)/shard_map/ppermute | solution.py:13
  4.4 0.1 copy.32
  4.5 3.8 %collective-permute-start = (f32[40,2048]{1,0:T(8,128)S(1)}, f32[40,2048]{1,0:T(8,128)S(1)}, u32[]{:S(2)}, u32[]{:S(2)}) collective-permute-start(f32[40,2048]{1,0:T(8,128)S(1)} %select_maximum_fusion), channel_id=1, source_target_pairs={{15,0},{0,1},{1,2},{2,3},{3,4},{4,5},{5,6},{6,7},{7,8},{8,9},{9,10... | collective-permute-start | bytes 983048 | tf_op jit(solution)/shard_map/ppermute | solution.py:13
  8.4 0.8 add_multiply_fusion.2
  9.2 1.3 %add_multiply_fusion.1 = (f32[125,2048]{1,0:T(8,128)S(1)}, f32[125,2048]{1,0:T(8,128)S(1)}) fusion(f32[127,2048]{1,0:T(8,128)S(1)} %get-tuple-element.21, s32[128,2048]{1,0:T(8,128)S(1)} %copy-done.1), kind=kLoop, calls=%fused_computation.47 | loop fusion | flops 8448000 | bytes 5120000 | tf_op jit(solution)/shard_map/mul | solution.py:35
  10.5 1.3 %add_multiply_fusion = (f32[121,2048]{1,0:T(8,128)S(1)}, f32[121,2048]{1,0:T(8,128)S(1)}) fusion(f32[125,2048]{1,0:T(8,128)S(1)} %get-tuple-element.19, s32[128,2048]{1,0:T(8,128)S(1)} %copy-done.1), kind=kLoop, calls=%fused_computation.46 | loop fusion | flops 8177664 | bytes 4956160 | tf_op jit(solution)/shard_map/mul | solution.py:35
  11.8 1.2 %add_multiply_fusion.3 = (f32[113,2048]{1,0:T(8,128)S(1)}, f32[113,2048]{1,0:T(8,128)S(1)}) fusion(f32[121,2048]{1,0:T(8,128)S(1)} %get-tuple-element.17, s32[128,2048]{1,0:T(8,128)S(1)} %copy-done.1), kind=kLoop, calls=%fused_computation.57 | loop fusion | flops 7636992 | bytes 4628480 | tf_op jit(solution)/shard_map/mul | solution.py:35
  13.0 0.1 fusion.24
  13.1 0.2 fusion.28
  13.4 0.3 fusion.26
  13.7 0.4 fusion.113
  14.0 0.3 fusion.30
  14.5 0.3 add_multiply_fusion.6
  14.8 0.5 add_multiply_fusion.5
  15.4 1.5 %collective-permute-done = f32[40,2048]{1,0:T(8,128)S(1)} collective-permute-done((f32[40,2048]{1,0:T(8,128)S(1)}, f32[40,2048]{1,0:T(8,128)S(1)}, u32[]{:S(2)}, u32[]{:S(2)}) %collective-permute-start) | collective-permute-done | bytes 327712 | tf_op jit(solution)/shard_map/ppermute | solution.py:13
  16.9 0.3 add_multiply_fusion.9
  17.2 0.5 add_multiply_fusion.8
  17.8 1.0 add_multiply_fusion.4
  18.8 0.4 add_multiply_fusion.10
  19.4 0.4 add_multiply_fusion.11
  20.2 1.0 fusion
  21.3 0.8 reshape.62
  22.1 6.3 %all-to-all-start = ((f32[32,1,408]{2,1,0:T(1,128)}), f32[32,1,408]{2,1,0:T(1,128)S(1)}, u32[]{:S(2)}, u32[]{:S(2)}) async-start(f32[32,1,408]{2,1,0:T(1,128)} %reshape.62), calls=%async_computation | async-start | bytes 131072 | tf_op jit(solution)/shard_map/all_to_all | solution.py:47
  28.5 7.4 %all-to-all-done = f32[32,1,408]{2,1,0:T(1,128)S(1)} async-done(((f32[32,1,408]{2,1,0:T(1,128)}), f32[32,1,408]{2,1,0:T(1,128)S(1)}, u32[]{:S(2)}, u32[]{:S(2)}) %all-to-all-start) | async-done | bytes 52256 | tf_op jit(solution)/shard_map/all_to_all | solution.py:47
  35.9 0.5 broadcast.403
  36.4 0.8 reduce.6
  37.3 0.1 reshape.63
  37.4 0.1 copy.25
  37.7 0.1 copy.27
  37.9 0.4 concatenate.66
  38.4 0.2 fusion.119
  38.5 0.1 reshape.59
  38.6 0.7 fusion.31
  39.4 0.1 copy.29
  39.5 35.9 %all_to_all.15 = f32[16,37,128]{2,1,0:T(8,128)S(1)} all-to-all(f32[16,37,128]{2,1,0:T(8,128)S(1)} %maximum_bitcast_fusion), channel_id=1, replica_groups=mesh['vox'=32,'tm'=16] {'tm'}, dimensions={0} | all-to-all | bytes 606208 | tf_op jit(solution)/shard_map/all_to_all | solution.py:54
  75.5 27.6 %all_to_all.16 = f32[16,37,128]{2,1,0:T(8,128)S(1)} all-to-all(f32[16,37,128]{2,1,0:T(8,128)S(1)} %broadcast_in_dim.13), channel_id=1, replica_groups=mesh['vox'=32,'tm'=16] {'tm'}, dimensions={0} | all-to-all | bytes 606208 | tf_op jit(solution)/shard_map/all_to_all | solution.py:56
  103.1 0.1 reshape.61
  103.2 0.1 copy.30
  103.3 3.3 %cholesky.16 = f32[36,36]{1,0:T(8,128)S(1)} custom-call(f32[36,36]{1,0:T(8,128)S(1)} %fusion.104), custom_call_target="Cholesky" | custom-call | tf_op jit(solution)/shard_map/jit(cholesky)/cholesky | solution.py:110
  106.6 0.6 compare_reduce_fusion
  107.2 0.7 fusion.99
  107.9 2.8 %custom-call.10 = f32[1,36,36]{1,2,0:T(8,128)S(1)} custom-call(f32[1,36,36]{2,1,0:T(8,128)S(1)} %fusion.99), custom_call_target="InvertDiagBlocksLowerTriangular" | custom-call | tf_op jit(solution)/shard_map/jit(_cho_solve)/triangular_solve | solution.py:111
  110.7 0.2 fusion.102
  110.9 0.2 fusion.100
  111.2 0.1 copy.34
  111.3 2.0 %convolution_subtract_fusion = f32[128,2048]{1,0:T(8,128)} fusion(f32[36,128]{1,0:T(8,128)S(1)} %fusion.100, f32[36,2048]{1,0:T(8,128)S(1)} %bitcast.39, f32[16,2048]{1,0:T(8,128)S(1)} %fusion.98, f32[96,2048]{1,0:T(8,128)S(1)} %fusion.30, f32[16,2048]{1,0:T(8,128)S(1)} %slice.519), kind=kOutput, calls=%fused_computation | convolution fusion | flops 114032640 | bytes 2410496 | tf_op jit(solution)/shard_map/dot_general | solution.py:17
  (50 shorter events, 1.5 us)
Async XLA Ops:
  0.0 20.2 %copy-start = (f32[3,2048]{1,0:T(4,128)S(1)}, f32[3,2048]{1,0:T(4,128)}, u32[]{:S(2)}) copy-start(f32[3,2048]{1,0:T(4,128)} %param.7) | copy-start | bytes 73732
  0.0 8.3 %copy-start.2 = (f32[128,2048]{1,0:T(8,128)S(1)}, f32[128,2048]{1,0:T(8,128)}, u32[]{:S(2)}) copy-start(f32[128,2048]{1,0:T(8,128)} %param.4) | copy-start | bytes 3145732
  0.0 4.3 %copy-start.3 = (f32[128,6]{0,1:T(8,128)S(1)}, f32[128,6]{0,1:T(8,128)}, u32[]{:S(2)}) copy-start(f32[128,6]{0,1:T(8,128)} %param.6) | copy-start | bytes 9220
  2.1 6.3 %copy-start.1 = (s32[128,2048]{1,0:T(8,128)S(1)}, s32[128,2048]{1,0:T(8,128)}, u32[]{:S(2)}) copy-start(s32[128,2048]{1,0:T(8,128)} %param.5) | copy-start | bytes 3145732
  2.1 12.3 %collective-permute-start.1 = (f32[32,2048]{1,0:T(8,128)S(1)}, f32[32,2048]{1,0:T(8,128)S(1)}, u32[]{:S(2)}, u32[]{:S(2)}) collective-permute-start(f32[32,2048]{1,0:T(8,128)S(1)} %pad_maximum_fusion.10), channel_id=1, source_target_pairs={{1,0},{2,1},{3,2},{4,3},{5,4},{6,5},{7,6},{8,7},{9,8},{10,9},{11,1... | collective-permute-start | bytes 786440 | tf_op jit(solution)/shard_map/ppermute | solution.py:13
  4.5 12.4 %collective-permute-start = (f32[40,2048]{1,0:T(8,128)S(1)}, f32[40,2048]{1,0:T(8,128)S(1)}, u32[]{:S(2)}, u32[]{:S(2)}) collective-permute-start(f32[40,2048]{1,0:T(8,128)S(1)} %select_maximum_fusion), channel_id=1, source_target_pairs={{15,0},{0,1},{1,2},{2,3},{3,4},{4,5},{5,6},{6,7},{7,8},{8,9},{9,10... | collective-permute-start | bytes 983048 | tf_op jit(solution)/shard_map/ppermute | solution.py:13
  22.1 13.8 %all-to-all-start = ((f32[32,1,408]{2,1,0:T(1,128)}), f32[32,1,408]{2,1,0:T(1,128)S(1)}, u32[]{:S(2)}, u32[]{:S(2)}) async-start(f32[32,1,408]{2,1,0:T(1,128)} %reshape.62), calls=%async_computation | async-start | bytes 131072 | tf_op jit(solution)/shard_map/all_to_all | solution.py:47

commit v6 on v5

--- a/solution.py
+++ b/solution.py
@@ -47,14 +47,31 @@
     return lax.all_to_all(copies, "vox", 0, 0, tiled=False).sum(axis=0)
 
 
-def sum_over_tm(block):
+def scatter_over_tm(block):
     n = lax.axis_size("tm")
     rows, cols = block.shape
     parts = block.reshape(rows, n, cols // n).transpose(1, 0, 2)
-    owned = lax.all_to_all(parts, "tm", 0, 0, tiled=False).sum(axis=0)
+    return lax.all_to_all(parts, "tm", 0, 0, tiled=False).sum(axis=0)
+
+
+def gather_over_tm(owned):
+    n = lax.axis_size("tm")
+    rows, width = owned.shape
     copies = jnp.broadcast_to(owned, (n,) + owned.shape)
     gathered = lax.all_to_all(copies, "tm", 0, 0, tiled=False)
-    return gathered.transpose(1, 0, 2).reshape(rows, cols)
+    return gathered.transpose(1, 0, 2).reshape(rows, n * width)
+
+
+def with_flat(block, small, voxels):
+    size = small.size
+    rows = -(-size // voxels)
+    flat = jnp.pad(small.reshape(size), (0, rows * voxels - size))
+    return jnp.concatenate([block, flat.reshape(rows, voxels)], axis=0)
+
+
+def flat_part(summed, first_row, shape):
+    size = shape[0] * shape[1]
+    return summed[first_row:].reshape(-1)[:size].reshape(shape)
 
 
 def local(series, spikes, motion, tissue):
@@ -80,33 +97,36 @@
     despiked_window = jnp.concatenate([jnp.zeros((HALO - 1, voxels), jnp.float32), head_window[:1], spike_free_series], axis=0)
 
     rows = despiked_window[HALO - 8 : HALO + frames]
+    first = lax.axis_index("tm") == 0
+    motion_before = jnp.where(first, jnp.zeros_like(motion_before), motion_before)
+    motion_derivative = motion - jnp.concatenate([motion_before, motion[:-1]], axis=0)
+    motion_terms = jnp.concatenate(
+        [motion, motion_derivative, motion * motion, motion_derivative * motion_derivative], axis=1
+    )
+    motion_cross = precise_product(motion_terms.T, spike_free_series)
+    motion_gram = precise_product(motion_terms.T, motion_terms)
+    owned_motion = scatter_over_tm(with_flat(motion_cross, motion_gram, voxels))
+
     numer = sum_over_vox(precise_product(rows, tissue.T))
     voxel_signals = numer / float(tissue.shape[1] * lax.axis_size("vox"))
+    signals_before = jnp.where(first, jnp.zeros_like(voxel_signals[7:8]), voxel_signals[7:8])
+    signals = voxel_signals[8:]
+    signal_derivative = signals - jnp.concatenate([signals_before, signals[:-1]], axis=0)
+    signal_terms = jnp.concatenate(
+        [signals, signal_derivative, signals * signals, signal_derivative * signal_derivative], axis=1
+    )
+    nuisance_matrix = jnp.concatenate([motion_terms, signal_terms], axis=1)
+    signal_cross = precise_product(signal_terms.T, spike_free_series)
+    signal_gram = precise_product(signal_terms.T, nuisance_matrix)
+    owned_signal = scatter_over_tm(with_flat(signal_cross, signal_gram, voxels))
 
-    first = lax.axis_index("tm") == 0
-    base_before = jnp.concatenate([motion_before, voxel_signals[7:8]], axis=1)
-    base_before = jnp.where(first, jnp.zeros_like(base_before), base_before)
-    base_regressors = jnp.concatenate([motion, voxel_signals[8:]], axis=1)
-    previous = jnp.concatenate([base_before, base_regressors[:-1]], axis=0)
-    temporal_derivative = base_regressors - previous
-    nuisance_matrix = jnp.concatenate(
-        [
-            base_regressors,
-            temporal_derivative,
-            base_regressors * base_regressors,
-            temporal_derivative * temporal_derivative,
-        ],
-        axis=1,
-    )
-    terms = nuisance_matrix.shape[1]
-    gram_matrix = precise_product(nuisance_matrix.T, nuisance_matrix)
-    cross_products = precise_product(nuisance_matrix.T, spike_free_series)
-    gram_rows = -(-terms * terms // voxels)
-    gram_flat = jnp.pad(gram_matrix.reshape(terms * terms), (0, gram_rows * voxels - terms * terms))
-    packed = jnp.concatenate([cross_products, gram_flat.reshape(gram_rows, voxels)], axis=0)
-    summed = sum_over_tm(packed)
-    cross_products = summed[:terms]
-    gram_matrix = summed[terms:].reshape(-1)[: terms * terms].reshape(terms, terms)
+    moving, signaled = motion_terms.shape[1], signal_terms.shape[1]
+    summed = gather_over_tm(jnp.concatenate([owned_motion, owned_signal], axis=0))
+    split = owned_motion.shape[0]
+    cross_products = jnp.concatenate([summed[:moving], summed[split : split + signaled]], axis=0)
+    gram_mm = flat_part(summed, moving, (moving, moving))
+    gram_s = flat_part(summed, split + signaled, (signaled, moving + signaled))
+    gram_matrix = jnp.concatenate([jnp.concatenate([gram_mm, gram_s[:, :moving].T], axis=1), gram_s], axis=0)
     factor = jnp.linalg.cholesky(gram_matrix)
     weights = jax.scipy.linalg.cho_solve((factor, True), nuisance_matrix.T)
     return spike_free_series - precise_product(weights.T, cross_products)

time: 114 us -> 133 us (1.17)
  blocking collectives: 63.5 us -> 26.4 us
  waiting for transfers between devices: 8.98 us -> 39.8 us
  starting transfers between devices: 12.3 us -> 32.8 us
  other arithmetic: 19 us -> 23.7 us
    all_to_all x2 -> x1, blocking collectives: 63.5 us -> 26.4 us  [gather_over_tm(): gathered = lax.all_to_all(copies, 'tm', 0, 0, tiled=False)]
    all_to_all x0 -> x2, waiting for transfers between devices: none -> 30.6 us  [scatter_over_tm(): return lax.all_to_all(parts, 'tm', 0, 0, tiled=False).sum(axis=0)]
    all_to_all x0 -> x2, starting transfers between devices: none -> 20.7 us  [scatter_over_tm(): return lax.all_to_all(parts, 'tm', 0, 0, tiled=False).sum(axis=0)]
    transpose x1 -> x2, other arithmetic: 0.03 us -> 1.41 us  [scatter_over_tm(): parts = block.reshape(rows, n, cols // n).transpose(1, 0, 2)]
    dot_general x4 -> x6, matrix products: 3.87 us -> 4.54 us  [precise_product(): jnp.dot(left, right, precision=lax.Precision.HIGHEST, preferred_element_t...]
  transfers between devices with their start and end apart: 3 -> 5, of which waited for: 2 -> 4; matrix products, arithmetic and copies ran while one was open for 6% -> 7% of each run, Pallas kernels for 0% -> 0%
where the time goes in v6:
time: 133 us
  waiting for transfers between devices  39.8 us (30%)
  starting transfers between devices  32.8 us (25%)
  blocking collectives  26.4 us (20%)
  other arithmetic  23.7 us (18%)
  matrix products  4.94 us (4%)
  local copies, waits for them, and re-layouts  4.75 us (4%)
    all_to_all x2, waiting for transfers between devices, scatter_over_tm(): return lax.all_to_all(parts, 'tm', 0, 0, tiled=False).sum(axis=0)  30.6 us
    all_to_all x1, blocking collectives, gather_over_tm(): gathered = lax.all_to_all(copies, 'tm', 0, 0, tiled=False)  26.4 us
    all_to_all x2, starting transfers between devices, scatter_over_tm(): return lax.all_to_all(parts, 'tm', 0, 0, tiled=False).sum(axis=0)  20.7 us
    mul x11, other arithmetic, despike_trimmed(): approx = (current + lagged) * 0.5  8.04 us
    all_to_all x1, waiting for transfers between devices, sum_over_vox(): return lax.all_to_all(copies, 'vox', 0, 0, tiled=False).sum(axis=0)  7.38 us
    all_to_all x1, starting transfers between devices, sum_over_vox(): return lax.all_to_all(copies, 'vox', 0, 0, tiled=False).sum(axis=0)  6.34 us
    ppermute x2, starting transfers between devices, from_behind(): return lax.ppermute(block, axis, route)  5.82 us
    dot_general x6, matrix products, precise_product(): jnp.dot(left, right, precision=lax.Precision.HIGHEST, preferred_element_t...  4.54 us
  transfers between devices with their start and end apart: 5, of which 4 were waited for; matrix products, arithmetic and copies ran while one was open for 7% of the time, Pallas kernels for 0%

profile of v6, /device:TPU:64, one launch (start us, length us, event | category | flops | bytes accessed | tf_op | source)
XLA Modules:
  0.0 133.0 jit_solution(13155601971023451141)
XLA Ops:
  0.0 1.1 fusion.121
  1.1 1.0 slice_convert_fusion.2
  2.1 0.7 pad_maximum_fusion.11
  2.8 2.0 %collective-permute-start.1 = (f32[32,2048]{1,0:T(8,128)}, f32[32,2048]{1,0:T(8,128)S(1)}, u32[]{:S(2)}, u32[]{:S(2)}) collective-permute-start(f32[32,2048]{1,0:T(8,128)} %pad_maximum_fusion.11), channel_id=1, source_target_pairs={{1,0},{2,1},{3,2},{4,3},{5,4},{6,5},{7,6},{8,7},{9,8},{10,9},{11,1... | collective-permute-start | bytes 786440 | tf_op jit(solution)/shard_map/ppermute | solution.py:13
  5.0 0.7 select_maximum_fusion
  5.8 3.8 %collective-permute-start = (f32[40,2048]{1,0:T(8,128)}, f32[40,2048]{1,0:T(8,128)}, u32[]{:S(2)}, u32[]{:S(2)}) collective-permute-start(f32[40,2048]{1,0:T(8,128)} %select_maximum_fusion), channel_id=1, source_target_pairs={{15,0},{0,1},{1,2},{2,3},{3,4},{4,5},{5,6},{6,7},{7,8},{8,9},{9,10... | collective-permute-start | bytes 983048 | tf_op jit(solution)/shard_map/ppermute | solution.py:13
  9.6 0.8 add_multiply_fusion.2
  10.4 1.3 add_multiply_fusion.1
  11.7 1.3 add_multiply_fusion
  13.1 1.2 add_multiply_fusion.3
  14.4 0.2 fusion.28
  14.6 0.3 fusion.26
  14.9 0.4 fusion.120
  15.3 0.3 fusion.30
  15.8 0.3 add_multiply_fusion.6
  16.1 0.5 add_multiply_fusion.5
  16.6 1.8 %collective-permute-done = f32[40,2048]{1,0:T(8,128)} collective-permute-done((f32[40,2048]{1,0:T(8,128)}, f32[40,2048]{1,0:T(8,128)}, u32[]{:S(2)}, u32[]{:S(2)}) %collective-permute-start) | collective-permute-done | bytes 327712 | tf_op jit(solution)/shard_map/ppermute | solution.py:13
  18.5 0.7 broadcast_select_fusion
  19.2 1.0 fusion.124
  20.2 0.3 add_multiply_fusion.9
  20.5 0.5 add_multiply_fusion.8
  21.1 1.0 add_multiply_fusion.4
  22.1 0.4 add_multiply_fusion.10
  22.7 0.4 add_multiply_fusion.11
  23.5 1.0 fusion
  24.6 0.8 reshape.54
  25.4 6.3 %all-to-all-start.1 = ((f32[32,1,408]{2,1,0:T(1,128)}), f32[32,1,408]{2,1,0:T(1,128)S(1)}, u32[]{:S(2)}, u32[]{:S(2)}) async-start(f32[32,1,408]{2,1,0:T(1,128)} %reshape.54), calls=%async_computation.1 | async-start | bytes 131072 | tf_op jit(solution)/shard_map/all_to_all | solution.py:47
  31.8 7.4 %all-to-all-done.1 = f32[32,1,408]{2,1,0:T(1,128)S(1)} async-done(((f32[32,1,408]{2,1,0:T(1,128)}), f32[32,1,408]{2,1,0:T(1,128)S(1)}, u32[]{:S(2)}, u32[]{:S(2)}) %all-to-all-start.1) | async-done | bytes 52256 | tf_op jit(solution)/shard_map/all_to_all | solution.py:47
  39.2 0.5 broadcast.394
  39.7 0.8 reduce.6
  41.0 0.3 concatenate.86
  41.5 0.6 fusion.32
  42.2 0.7 maximum_bitcast_fusion.1
  42.9 16.0 %all-to-all-start.2 = ((f32[16,13,128]{2,1,0:T(8,128)}), f32[16,13,128]{2,1,0:T(8,128)S(1)}, u32[]{:S(2)}, u32[]{:S(2)}) async-start(f32[16,13,128]{2,1,0:T(8,128)} %maximum_bitcast_fusion.1), calls=%async_computation.2 | async-start | bytes 262144 | tf_op jit(solution)/shard_map/all_to_all | solution.py:54
  58.8 0.1 fusion.108
  59.1 0.6 convolution_bitcast_fusion
  59.7 0.7 maximum_bitcast_fusion
  60.5 12.5 %all-to-all-done.2 = f32[16,13,128]{2,1,0:T(8,128)S(1)} async-done(((f32[16,13,128]{2,1,0:T(8,128)}), f32[16,13,128]{2,1,0:T(8,128)S(1)}, u32[]{:S(2)}, u32[]{:S(2)}) %all-to-all-start.2) | async-done | bytes 106528 | tf_op jit(solution)/shard_map/all_to_all | solution.py:54
  73.0 4.7 %all-to-all-start = ((f32[16,25,128]{2,1,0:T(8,128)}), f32[16,25,128]{2,1,0:T(8,128)S(1)}, u32[]{:S(2)}, u32[]{:S(2)}) async-start(f32[16,25,128]{2,1,0:T(8,128)} %maximum_bitcast_fusion), calls=%async_computation | async-start | bytes 524288 | tf_op jit(solution)/shard_map/all_to_all | solution.py:54
  77.7 18.1 %all-to-all-done = f32[16,25,128]{2,1,0:T(8,128)S(1)} async-done(((f32[16,25,128]{2,1,0:T(8,128)}), f32[16,25,128]{2,1,0:T(8,128)S(1)}, u32[]{:S(2)}, u32[]{:S(2)}) %all-to-all-start) | async-done | bytes 204832 | tf_op jit(solution)/shard_map/all_to_all | solution.py:54
  95.9 26.4 %all_to_all.20 = f32[16,38,128]{2,1,0:T(8,128)S(1)} all-to-all(f32[16,38,128]{2,1,0:T(8,128)S(1)} %broadcast_in_dim.13), channel_id=1, replica_groups=mesh['vox'=32,'tm'=16] {'tm'}, dimensions={0} | all-to-all | bytes 622592 | tf_op jit(solution)/shard_map/all_to_all | solution.py:61
  123.2 3.3 %cholesky.16 = f32[36,36]{1,0:T(8,128)S(1)} custom-call(f32[36,36]{1,0:T(8,128)S(1)} %fusion.107), custom_call_target="Cholesky" | custom-call | tf_op jit(solution)/shard_map/jit(cholesky)/cholesky | solution.py:130
  126.5 0.6 compare_reduce_fusion
  127.1 0.7 fusion.102
  127.8 2.8 %custom-call.10 = f32[1,36,36]{1,2,0:T(8,128)S(1)} custom-call(f32[1,36,36]{2,1,0:T(8,128)S(1)} %fusion.102), custom_call_target="InvertDiagBlocksLowerTriangular" | custom-call | tf_op jit(solution)/shard_map/jit(_cho_solve)/triangular_solve | solution.py:131
  130.5 0.2 fusion.105
  130.8 0.2 fusion.103
  131.0 2.0 %convolution_subtract_fusion = f32[128,2048]{1,0:T(8,128)} fusion(f32[36,128]{1,0:T(8,128)S(1)} %fusion.103, f32[16,2048]{1,0:T(8,128)S(1)} %fusion.101, f32[96,2048]{1,0:T(8,128)S(1)} %fusion.30, f32[16,2048]{1,0:T(8,128)S(1)} %slice.545, f32[12,2048]{1,0:T(8,128)S(1)} %bitcast.59, f32[24,2048]{1,0:T(8,128)S(1)} %bitcast.55), kind=kOutput, calls=%fused_computation | convolution fusion | flops 114106368 | bytes 2410496 | tf_op jit(solution)/shard_map/dot_general | solution.py:17
  (69 shorter events, 3.0 us)
Async XLA Ops:
  0.0 23.5 %copy-start = (f32[3,2048]{1,0:T(4,128)S(1)}, f32[3,2048]{1,0:T(4,128)}, u32[]{:S(2)}) copy-start(f32[3,2048]{1,0:T(4,128)} %param.7) | copy-start | bytes 73732
  0.0 9.6 %copy-start.2 = (f32[128,2048]{1,0:T(8,128)S(1)}, f32[128,2048]{1,0:T(8,128)}, u32[]{:S(2)}) copy-start(f32[128,2048]{1,0:T(8,128)} %param.4) | copy-start | bytes 3145732
  0.0 4.8 %copy-start.3 = (f32[128,6]{0,1:T(8,128)S(1)}, f32[128,6]{0,1:T(8,128)}, u32[]{:S(2)}) copy-start(f32[128,6]{0,1:T(8,128)} %param.6) | copy-start | bytes 9220
  2.1 7.5 %copy-start.1 = (s32[128,2048]{1,0:T(8,128)S(1)}, s32[128,2048]{1,0:T(8,128)}, u32[]{:S(2)}) copy-start(s32[128,2048]{1,0:T(8,128)} %param.5) | copy-start | bytes 3145732
  2.8 12.9 %collective-permute-start.1 = (f32[32,2048]{1,0:T(8,128)}, f32[32,2048]{1,0:T(8,128)S(1)}, u32[]{:S(2)}, u32[]{:S(2)}) collective-permute-start(f32[32,2048]{1,0:T(8,128)} %pad_maximum_fusion.11), channel_id=1, source_target_pairs={{1,0},{2,1},{3,2},{4,3},{5,4},{6,5},{7,6},{8,7},{9,8},{10,9},{11,1... | collective-permute-start | bytes 786440 | tf_op jit(solution)/shard_map/ppermute | solution.py:13
  5.8 12.7 %collective-permute-start = (f32[40,2048]{1,0:T(8,128)}, f32[40,2048]{1,0:T(8,128)}, u32[]{:S(2)}, u32[]{:S(2)}) collective-permute-start(f32[40,2048]{1,0:T(8,128)} %select_maximum_fusion), channel_id=1, source_target_pairs={{15,0},{0,1},{1,2},{2,3},{3,4},{4,5},{5,6},{6,7},{7,8},{8,9},{9,10... | collective-permute-start | bytes 983048 | tf_op jit(solution)/shard_map/ppermute | solution.py:13
  25.4 13.8 %all-to-all-start.1 = ((f32[32,1,408]{2,1,0:T(1,128)}), f32[32,1,408]{2,1,0:T(1,128)S(1)}, u32[]{:S(2)}, u32[]{:S(2)}) async-start(f32[32,1,408]{2,1,0:T(1,128)} %reshape.54), calls=%async_computation.1 | async-start | bytes 131072 | tf_op jit(solution)/shard_map/all_to_all | solution.py:47
  42.9 30.1 %all-to-all-start.2 = ((f32[16,13,128]{2,1,0:T(8,128)}), f32[16,13,128]{2,1,0:T(8,128)S(1)}, u32[]{:S(2)}, u32[]{:S(2)}) async-start(f32[16,13,128]{2,1,0:T(8,128)} %maximum_bitcast_fusion.1), calls=%async_computation.2 | async-start | bytes 262144 | tf_op jit(solution)/shard_map/all_to_all | solution.py:54
  73.0 22.8 %all-to-all-start = ((f32[16,25,128]{2,1,0:T(8,128)}), f32[16,25,128]{2,1,0:T(8,128)S(1)}, u32[]{:S(2)}, u32[]{:S(2)}) async-start(f32[16,25,128]{2,1,0:T(8,128)} %maximum_bitcast_fusion), calls=%async_computation | async-start | bytes 524288 | tf_op jit(solution)/shard_map/all_to_all | solution.py:54

commit v7 on v5

--- a/solution.py
+++ b/solution.py
@@ -60,17 +60,23 @@
 def local(series, spikes, motion, tissue):
     frames = series.shape[0]
     voxels = series.shape[1]
-    motion_row = jnp.pad(motion[frames - 1 :], ((0, 7), (0, voxels - motion.shape[1])))
-    tail = jnp.concatenate([series[frames - HALO :], spikes[frames - HALO :].astype(jnp.float32), motion_row], axis=0)
+    last_rows = jnp.concatenate(
+        [spikes[frames - 1 :].astype(jnp.float32), jnp.pad(motion[frames - 1 :], ((0, 0), (0, voxels - motion.shape[1])))],
+        axis=0,
+    )
+    tail = jnp.concatenate([series[frames - HALO :], jnp.pad(last_rows, ((0, 6), (0, 0)))], axis=0)
     head = jnp.concatenate([series[:HALO], spikes[:HALO].astype(jnp.float32)], axis=0)
     before = from_behind(tail, "tm", 1)
     after = from_behind(head, "tm", -1)
-    motion_before = before[2 * HALO : 2 * HALO + 1, : motion.shape[1]]
+    motion_before = before[HALO + 1 : HALO + 2, : motion.shape[1]]
+    flags_before = jnp.concatenate(
+        [jnp.zeros((HALO - 1, voxels), jnp.int32), before[HALO : HALO + 1].astype(jnp.int32)], axis=0
+    )
     inner = despike_trimmed(series, spikes)
     edge = 2 * HALO
     head_window = despike_trimmed(
         jnp.concatenate([before[:HALO], series[:edge]], axis=0),
-        jnp.concatenate([before[HALO : 2 * HALO].astype(jnp.int32), spikes[:edge]], axis=0),
+        jnp.concatenate([flags_before, spikes[:edge]], axis=0),
     )
     tail_window = despike_trimmed(
         jnp.concatenate([series[frames - edge :], after[:HALO]], axis=0),

time: 114 us -> 115 us (level)
  blocking collectives: 63.5 us -> 60.7 us
  waiting for transfers between devices: 8.98 us -> 10.2 us
  starting transfers between devices: 12.3 us -> 13.5 us
    all_to_all x1, blocking collectives: 35.9 us -> 33.1 us  [sum_over_tm(): owned = lax.all_to_all(parts, 'tm', 0, 0, tiled=False).sum(axis=0)]
    ppermute x2, waiting for transfers between devices: 1.54 us -> 2.72 us  [from_behind(): return lax.ppermute(block, axis, route)]
    all_to_all x1, starting transfers between devices: 6.34 us -> 7.5 us  [sum_over_vox(): return lax.all_to_all(copies, 'vox', 0, 0, tiled=False).sum(axis=0)]
where the time goes in v7:
time: 115 us; the launch traced here: 114 us
  blocking collectives  60.7 us (53%)
  other arithmetic  19.9 us (17%)
  starting transfers between devices  13.5 us (12%)
  waiting for transfers between devices  10.2 us (9%)
  local copies, waits for them, and re-layouts  5.44 us (5%)
  matrix products  4.27 us (4%)
    all_to_all x1, blocking collectives, sum_over_tm(): owned = lax.all_to_all(parts, 'tm', 0, 0, tiled=False).sum(axis=0)  33.1 us
    all_to_all x1, blocking collectives, sum_over_tm(): gathered = lax.all_to_all(copies, 'tm', 0, 0, tiled=False)  27.6 us
    mul x11, other arithmetic, despike_trimmed(): approx = (current + lagged) * 0.5  8.02 us
    all_to_all x1, starting transfers between devices, sum_over_vox(): return lax.all_to_all(copies, 'vox', 0, 0, tiled=False).sum(axis=0)  7.5 us
    all_to_all x1, waiting for transfers between devices, sum_over_vox(): return lax.all_to_all(copies, 'vox', 0, 0, tiled=False).sum(axis=0)  7.44 us
    ppermute x2, starting transfers between devices, from_behind(): return lax.ppermute(block, axis, route)  5.97 us
    another operation x3, other arithmetic, local(): factor = jnp.linalg.cholesky(gram_matrix)  3.96 us
    dot_general x4, matrix products, precise_product(): jnp.dot(left, right, precision=lax.Precision.HIGHEST, preferred_element_t...  3.86 us
  transfers between devices with their start and end apart: 3, of which 2 were waited for; matrix products, arithmetic and copies ran while one was open for 6% of the time, Pallas kernels for 0%

profile of v7, /device:TPU:64, one launch (start us, length us, event | category | flops | bytes accessed | tf_op | source)
XLA Modules:
  0.0 114.5 jit_solution(14323404871645494734)
XLA Ops:
  0.0 0.8 slice.378
  0.9 0.8 slice_convert_fusion.3
  1.8 1.0 fusion.109
  2.8 4.0 %collective-permute-start = (f32[24,2048]{1,0:T(8,128)S(1)}, f32[24,2048]{1,0:T(8,128)S(1)}, u32[]{:S(2)}, u32[]{:S(2)}) collective-permute-start(f32[24,2048]{1,0:T(8,128)S(1)} %select_maximum_fusion), channel_id=1, source_target_pairs={{15,0},{0,1},{1,2},{2,3},{3,4},{4,5},{5,6},{6,7},{7,8},{8,9},{9,10... | collective-permute-start | bytes 589832 | tf_op jit(solution)/shard_map/ppermute | solution.py:13
  6.8 0.9 slice_convert_fusion.1
  7.8 2.0 %collective-permute-start.1 = (f32[32,2048]{1,0:T(8,128)S(1)}, f32[32,2048]{1,0:T(8,128)S(1)}, u32[]{:S(2)}, u32[]{:S(2)}) collective-permute-start(f32[32,2048]{1,0:T(8,128)S(1)} %pad_maximum_fusion.10), channel_id=1, source_target_pairs={{1,0},{2,1},{3,2},{4,3},{5,4},{6,5},{7,6},{8,7},{9,8},{10,9},{11,1... | collective-permute-start | bytes 786440 | tf_op jit(solution)/shard_map/ppermute | solution.py:13
  9.8 0.8 add_multiply_fusion.2
  10.6 1.3 %add_multiply_fusion.1 = (f32[125,2048]{1,0:T(8,128)S(1)}, f32[125,2048]{1,0:T(8,128)S(1)}) fusion(f32[127,2048]{1,0:T(8,128)S(1)} %get-tuple-element.19, s32[128,2048]{1,0:T(8,128)S(1)} %copy-done.1), kind=kLoop, calls=%fused_computation.47 | loop fusion | flops 8448000 | bytes 5120000 | tf_op jit(solution)/shard_map/mul | solution.py:35
  11.9 1.3 %add_multiply_fusion = (f32[121,2048]{1,0:T(8,128)S(1)}, f32[121,2048]{1,0:T(8,128)S(1)}) fusion(f32[125,2048]{1,0:T(8,128)S(1)} %get-tuple-element.17, s32[128,2048]{1,0:T(8,128)S(1)} %copy-done.1), kind=kLoop, calls=%fused_computation.46 | loop fusion | flops 8177664 | bytes 4956160 | tf_op jit(solution)/shard_map/mul | solution.py:35
  13.3 1.2 %add_multiply_fusion.3 = (f32[113,2048]{1,0:T(8,128)S(1)}, f32[113,2048]{1,0:T(8,128)S(1)}) fusion(f32[121,2048]{1,0:T(8,128)S(1)} %get-tuple-element.15, s32[128,2048]{1,0:T(8,128)S(1)} %copy-done.1), kind=kLoop, calls=%fused_computation.57 | loop fusion | flops 7636992 | bytes 4628480 | tf_op jit(solution)/shard_map/mul | solution.py:35
  14.5 0.1 fusion.24
  14.6 0.2 fusion.28
  14.8 0.3 fusion.26
  15.1 0.4 fusion.111
  15.5 0.3 fusion.30
  16.0 0.1 pad_add_fusion.1
  16.1 2.7 %collective-permute-done.1 = f32[32,2048]{1,0:T(8,128)S(1)} collective-permute-done((f32[32,2048]{1,0:T(8,128)S(1)}, f32[32,2048]{1,0:T(8,128)S(1)}, u32[]{:S(2)}, u32[]{:S(2)}) %collective-permute-start.1) | collective-permute-done | bytes 262176 | tf_op jit(solution)/shard_map/ppermute | solution.py:13
  18.8 0.6 add_multiply_fusion.6
  19.4 0.5 add_multiply_fusion.5
  20.0 0.5 add_multiply_fusion.4
  20.5 0.4 add_multiply_fusion.10
  21.1 0.5 add_multiply_fusion.8
  21.7 0.5 add_multiply_fusion.7
  22.2 0.4 add_multiply_fusion.11
  22.9 1.0 fusion
  24.0 0.8 reshape.62
  24.9 7.5 %all-to-all-start = ((f32[32,1,408]{2,1,0:T(1,128)}), f32[32,1,408]{2,1,0:T(1,128)S(1)}, u32[]{:S(2)}, u32[]{:S(2)}) async-start(f32[32,1,408]{2,1,0:T(1,128)} %reshape.62), calls=%async_computation | async-start | bytes 131072 | tf_op jit(solution)/shard_map/all_to_all | solution.py:47
  32.4 7.4 %all-to-all-done = f32[32,1,408]{2,1,0:T(1,128)S(1)} async-done(((f32[32,1,408]{2,1,0:T(1,128)}), f32[32,1,408]{2,1,0:T(1,128)S(1)}, u32[]{:S(2)}, u32[]{:S(2)}) %all-to-all-start) | async-done | bytes 52256 | tf_op jit(solution)/shard_map/all_to_all | solution.py:47
  39.8 0.5 broadcast.411
  40.4 0.8 reduce.6
  41.2 0.1 reshape.63
  41.3 0.1 copy.25
  41.6 0.1 copy.27
  41.8 0.4 concatenate.74
  42.3 0.2 fusion.116
  42.6 0.7 fusion.31
  43.3 0.1 copy.29
  43.5 33.1 %all_to_all.15 = f32[16,37,128]{2,1,0:T(8,128)S(1)} all-to-all(f32[16,37,128]{2,1,0:T(8,128)S(1)} %maximum_bitcast_fusion), channel_id=1, replica_groups=mesh['vox'=32,'tm'=16] {'tm'}, dimensions={0} | all-to-all | bytes 606208 | tf_op jit(solution)/shard_map/all_to_all | solution.py:54
  76.7 27.6 %all_to_all.16 = f32[16,37,128]{2,1,0:T(8,128)S(1)} all-to-all(f32[16,37,128]{2,1,0:T(8,128)S(1)} %broadcast_in_dim.17), channel_id=1, replica_groups=mesh['vox'=32,'tm'=16] {'tm'}, dimensions={0} | all-to-all | bytes 606208 | tf_op jit(solution)/shard_map/all_to_all | solution.py:56
  104.3 0.1 reshape.61
  104.5 3.3 %cholesky.16 = f32[36,36]{1,0:T(8,128)S(1)} custom-call(f32[36,36]{1,0:T(8,128)S(1)} %fusion.101), custom_call_target="Cholesky" | custom-call | tf_op jit(solution)/shard_map/jit(cholesky)/cholesky | solution.py:116
  107.8 0.6 compare_reduce_fusion
  108.4 0.7 fusion.96
  109.1 2.8 %custom-call.10 = f32[1,36,36]{1,2,0:T(8,128)S(1)} custom-call(f32[1,36,36]{2,1,0:T(8,128)S(1)} %fusion.96), custom_call_target="InvertDiagBlocksLowerTriangular" | custom-call | tf_op jit(solution)/shard_map/jit(_cho_solve)/triangular_solve | solution.py:117
  111.9 0.2 fusion.99
  112.1 0.2 fusion.97
  112.4 0.1 copy.34
  112.5 2.0 %convolution_subtract_fusion = f32[128,2048]{1,0:T(8,128)} fusion(f32[36,128]{1,0:T(8,128)S(1)} %fusion.97, f32[36,2048]{1,0:T(8,128)S(1)} %bitcast.39, f32[16,2048]{1,0:T(8,128)S(1)} %fusion.95, f32[96,2048]{1,0:T(8,128)S(1)} %fusion.30, f32[16,2048]{1,0:T(8,128)S(1)} %slice.514), kind=kOutput, calls=%fused_computation | convolution fusion | flops 114032640 | bytes 2410496 | tf_op jit(solution)/shard_map/dot_general | solution.py:17
  (56 shorter events, 1.7 us)
Async XLA Ops:
  0.0 22.9 %copy-start = (f32[3,2048]{1,0:T(4,128)S(1)}, f32[3,2048]{1,0:T(4,128)}, u32[]{:S(2)}) copy-start(f32[3,2048]{1,0:T(4,128)} %param.7) | copy-start | bytes 73732
  0.0 9.8 %copy-start.2 = (f32[128,2048]{1,0:T(8,128)S(1)}, f32[128,2048]{1,0:T(8,128)}, u32[]{:S(2)}) copy-start(f32[128,2048]{1,0:T(8,128)} %param.4) | copy-start | bytes 3145732
  2.8 7.0 %copy-start.1 = (s32[128,2048]{1,0:T(8,128)S(1)}, s32[128,2048]{1,0:T(8,128)}, u32[]{:S(2)}) copy-start(s32[128,2048]{1,0:T(8,128)} %param.5) | copy-start | bytes 3145732
  2.8 13.1 %collective-permute-start = (f32[24,2048]{1,0:T(8,128)S(1)}, f32[24,2048]{1,0:T(8,128)S(1)}, u32[]{:S(2)}, u32[]{:S(2)}) collective-permute-start(f32[24,2048]{1,0:T(8,128)S(1)} %select_maximum_fusion), channel_id=1, source_target_pairs={{15,0},{0,1},{1,2},{2,3},{3,4},{4,5},{5,6},{6,7},{7,8},{8,9},{9,10... | collective-permute-start | bytes 589832 | tf_op jit(solution)/shard_map/ppermute | solution.py:13
  7.8 11.1 %collective-permute-start.1 = (f32[32,2048]{1,0:T(8,128)S(1)}, f32[32,2048]{1,0:T(8,128)S(1)}, u32[]{:S(2)}, u32[]{:S(2)}) collective-permute-start(f32[32,2048]{1,0:T(8,128)S(1)} %pad_maximum_fusion.10), channel_id=1, source_target_pairs={{1,0},{2,1},{3,2},{4,3},{5,4},{6,5},{7,6},{8,7},{9,8},{10,9},{11,1... | collective-permute-start | bytes 786440 | tf_op jit(solution)/shard_map/ppermute | solution.py:13
  24.0 17.8 %copy-start.3 = (f32[128,6]{0,1:T(8,128)S(1)}, f32[128,6]{0,1:T(8,128)}, u32[]{:S(2)}) copy-start(f32[128,6]{0,1:T(8,128)} %param.6) | copy-start | bytes 9220
  24.9 15.0 %all-to-all-start = ((f32[32,1,408]{2,1,0:T(1,128)}), f32[32,1,408]{2,1,0:T(1,128)S(1)}, u32[]{:S(2)}, u32[]{:S(2)}) async-start(f32[32,1,408]{2,1,0:T(1,128)} %reshape.62), calls=%async_computation | async-start | bytes 131072 | tf_op jit(solution)/shard_map/all_to_all | solution.py:47

commit v8 on v5

--- a/solution.py
+++ b/solution.py
@@ -76,31 +76,51 @@
         jnp.concatenate([series[frames - edge :], after[:HALO]], axis=0),
         jnp.concatenate([spikes[frames - edge :], after[HALO:].astype(jnp.int32)], axis=0),
     )
-    spike_free_series = jnp.concatenate([head_window[1 : HALO + 1], inner[1 : frames - 31], tail_window[1 : HALO + 1]], axis=0)
-    despiked_window = jnp.concatenate([jnp.zeros((HALO - 1, voxels), jnp.float32), head_window[:1], spike_free_series], axis=0)
-
-    rows = despiked_window[HALO - 8 : HALO + frames]
-    numer = sum_over_vox(precise_product(rows, tissue.T))
+    middle = inner[1 : frames - 31]
+    head_rows, tail_rows = head_window[: HALO + 1], tail_window[1 : HALO + 1]
+    spike_free_series = jnp.concatenate([head_rows[1:], middle, tail_rows], axis=0)
+    weights_t = tissue.T
+    numer = jnp.concatenate(
+        [
+            jnp.zeros((7, tissue.shape[0]), jnp.float32),
+            precise_product(head_rows, weights_t),
+            precise_product(middle, weights_t),
+            precise_product(tail_rows, weights_t),
+        ],
+        axis=0,
+    )
+    numer = sum_over_vox(numer)
     voxel_signals = numer / float(tissue.shape[1] * lax.axis_size("vox"))
 
     first = lax.axis_index("tm") == 0
-    base_before = jnp.concatenate([motion_before, voxel_signals[7:8]], axis=1)
-    base_before = jnp.where(first, jnp.zeros_like(base_before), base_before)
-    base_regressors = jnp.concatenate([motion, voxel_signals[8:]], axis=1)
-    previous = jnp.concatenate([base_before, base_regressors[:-1]], axis=0)
-    temporal_derivative = base_regressors - previous
-    nuisance_matrix = jnp.concatenate(
-        [
-            base_regressors,
-            temporal_derivative,
-            base_regressors * base_regressors,
-            temporal_derivative * temporal_derivative,
-        ],
-        axis=1,
+    motion_before = jnp.where(first, jnp.zeros_like(motion_before), motion_before)
+    motion_derivative = motion - jnp.concatenate([motion_before, motion[:-1]], axis=0)
+    motion_terms = jnp.concatenate(
+        [motion, motion_derivative, motion * motion, motion_derivative * motion_derivative], axis=1
     )
-    terms = nuisance_matrix.shape[1]
-    gram_matrix = precise_product(nuisance_matrix.T, nuisance_matrix)
-    cross_products = precise_product(nuisance_matrix.T, spike_free_series)
+    inner_rows = slice(HALO, frames - HALO)
+    motion_cross = (
+        precise_product(motion_terms[inner_rows].T, middle)
+        + precise_product(motion_terms[:HALO].T, head_rows[1:])
+        + precise_product(motion_terms[frames - HALO :].T, tail_rows)
+    )
+    motion_gram = precise_product(motion_terms.T, motion_terms)
+
+    signals_before = jnp.where(first, jnp.zeros_like(voxel_signals[7:8]), voxel_signals[7:8])
+    signals = voxel_signals[8:]
+    signal_derivative = signals - jnp.concatenate([signals_before, signals[:-1]], axis=0)
+    signal_terms = jnp.concatenate(
+        [signals, signal_derivative, signals * signals, signal_derivative * signal_derivative], axis=1
+    )
+    nuisance_matrix = jnp.concatenate([motion_terms, signal_terms], axis=1)
+    signal_cross = precise_product(signal_terms.T, spike_free_series)
+    signal_gram = precise_product(signal_terms.T, nuisance_matrix)
+    moving, signaled = motion_terms.shape[1], signal_terms.shape[1]
+    terms = moving + signaled
+    gram_matrix = jnp.concatenate(
+        [jnp.concatenate([motion_gram, signal_gram[:, :moving].T], axis=1), signal_gram], axis=0
+    )
+    cross_products = jnp.concatenate([motion_cross, signal_cross], axis=0)
     gram_rows = -(-terms * terms // voxels)
     gram_flat = jnp.pad(gram_matrix.reshape(terms * terms), (0, gram_rows * voxels - terms * terms))
     packed = jnp.concatenate([cross_products, gram_flat.reshape(gram_rows, voxels)], axis=0)

time: 114 us -> 118 us (1.035)
  other arithmetic: 19 us -> 22.4 us
  waiting for transfers between devices: 8.98 us -> 7.26 us
  local copies, waits for them, and re-layouts: 4.75 us -> 6.13 us
  matrix products: 4.27 us -> 5.63 us
    dot_general x4 -> x10, matrix products: 3.87 us -> 5.22 us  [precise_product(): jnp.dot(left, right, precision=lax.Precision.HIGHEST, preferred_element_t...]
    unnamed x15 -> x18, local copies, waits for them, and re-layouts: 1.31 us -> 2.41 us
  transfers between devices with their start and end apart: 3 -> 3, of which waited for: 2 -> 2; matrix products, arithmetic and copies ran while one was open for 6% -> 8% of each run, Pallas kernels for 0% -> 0%
where the time goes in v8:
time: 118 us; the launch traced here: 117 us
  blocking collectives  62.8 us (53%)
  other arithmetic  22.4 us (19%)
  starting transfers between devices  12.6 us (11%)
  waiting for transfers between devices  7.26 us (6%)
  local copies, waits for them, and re-layouts  6.13 us (5%)
  matrix products  5.63 us (5%)
    all_to_all x1, blocking collectives, sum_over_tm(): owned = lax.all_to_all(parts, 'tm', 0, 0, tiled=False).sum(axis=0)  35.2 us
    all_to_all x1, blocking collectives, sum_over_tm(): gathered = lax.all_to_all(copies, 'tm', 0, 0, tiled=False)  27.6 us
    mul x11, other arithmetic, despike_trimmed(): approx = (current + lagged) * 0.5  8.1 us
    all_to_all x1, starting transfers between devices, sum_over_vox(): return lax.all_to_all(copies, 'vox', 0, 0, tiled=False).sum(axis=0)  6.82 us
    all_to_all x1, waiting for transfers between devices, sum_over_vox(): return lax.all_to_all(copies, 'vox', 0, 0, tiled=False).sum(axis=0)  6.75 us
    ppermute x2, starting transfers between devices, from_behind(): return lax.ppermute(block, axis, route)  5.82 us
    dot_general x10, matrix products, precise_product(): jnp.dot(left, right, precision=lax.Precision.HIGHEST, preferred_element_t...  5.22 us
    another operation x3, other arithmetic, local(): factor = jnp.linalg.cholesky(gram_matrix)  3.96 us
  transfers between devices with their start and end apart: 3, of which 2 were waited for; matrix products, arithmetic and copies ran while one was open for 8% of the time, Pallas kernels for 0%

profile of v8, /device:TPU:64, one launch (start us, length us, event | category | flops | bytes accessed | tf_op | source)
XLA Modules:
  0.0 117.4 jit_solution(2470468229891792941)
XLA Ops:
  0.0 1.1 fusion.119
  1.1 1.0 slice_convert_fusion.2
  2.1 0.7 pad_maximum_fusion.4
  2.8 2.0 %collective-permute-start.1 = (f32[32,2048]{1,0:T(8,128)}, f32[32,2048]{1,0:T(8,128)S(1)}, u32[]{:S(2)}, u32[]{:S(2)}) collective-permute-start(f32[32,2048]{1,0:T(8,128)} %pad_maximum_fusion.4), channel_id=1, source_target_pairs={{1,0},{2,1},{3,2},{4,3},{5,4},{6,5},{7,6},{8,7},{9,8},{10,9},{11,1... | collective-permute-start | bytes 786440 | tf_op jit(solution)/shard_map/ppermute | solution.py:13
  5.0 0.7 select_maximum_fusion
  5.8 3.8 %collective-permute-start = (f32[40,2048]{1,0:T(8,128)}, f32[40,2048]{1,0:T(8,128)}, u32[]{:S(2)}, u32[]{:S(2)}) collective-permute-start(f32[40,2048]{1,0:T(8,128)} %select_maximum_fusion), channel_id=1, source_target_pairs={{15,0},{0,1},{1,2},{2,3},{3,4},{4,5},{5,6},{6,7},{7,8},{8,9},{9,10... | collective-permute-start | bytes 983048 | tf_op jit(solution)/shard_map/ppermute | solution.py:13
  9.6 0.8 add_multiply_fusion.2
  10.4 1.3 %add_multiply_fusion.1 = (f32[125,2048]{1,0:T(8,128)S(1)}, f32[125,2048]{1,0:T(8,128)S(1)}) fusion(f32[127,2048]{1,0:T(8,128)S(1)} %get-tuple-element.19, s32[128,2048]{1,0:T(8,128)S(1)} %copy-done.1), kind=kLoop, calls=%fused_computation.46 | loop fusion | flops 8448000 | bytes 5120000 | tf_op jit(solution)/shard_map/mul | solution.py:35
  11.7 1.3 %add_multiply_fusion = (f32[121,2048]{1,0:T(8,128)S(1)}, f32[121,2048]{1,0:T(8,128)S(1)}) fusion(f32[125,2048]{1,0:T(8,128)S(1)} %get-tuple-element.17, s32[128,2048]{1,0:T(8,128)S(1)} %copy-done.1), kind=kLoop, calls=%fused_computation.45 | loop fusion | flops 8177664 | bytes 4956160 | tf_op jit(solution)/shard_map/mul | solution.py:35
  13.1 1.2 %add_multiply_fusion.3 = (f32[113,2048]{1,0:T(8,128)S(1)}, f32[113,2048]{1,0:T(8,128)S(1)}) fusion(f32[121,2048]{1,0:T(8,128)S(1)} %get-tuple-element.15, s32[128,2048]{1,0:T(8,128)S(1)} %copy-done.1), kind=kLoop, calls=%fused_computation.56 | loop fusion | flops 7636992 | bytes 4628480 | tf_op jit(solution)/shard_map/mul | solution.py:35
  14.4 0.2 fusion.28
  14.6 0.3 fusion.26
  14.9 0.4 fusion.118
  15.3 0.3 fusion.30
  15.7 0.7 fusion.125
  16.4 0.3 add_multiply_fusion.6
  16.7 0.5 add_multiply_fusion.5
  17.3 0.7 fusion.121
  18.0 0.5 collective-permute-done
  18.5 0.7 broadcast_select_fusion
  19.5 0.5 fusion.108
  20.0 1.0 fusion.122
  21.0 0.3 add_multiply_fusion.9
  21.3 0.5 add_multiply_fusion.8
  21.8 1.0 add_multiply_fusion.4
  22.8 0.4 add_multiply_fusion.10
  23.5 0.9 copy-done.3
  24.4 0.2 fusion.126
  24.6 0.5 add_multiply_fusion.11
  25.4 0.2 fusion.86
  25.8 1.0 reshape.35
  26.8 6.8 %all-to-all-start = ((f32[32,1,408]{2,1,0:T(1,128)}), f32[32,1,408]{2,1,0:T(1,128)S(1)}, u32[]{:S(2)}, u32[]{:S(2)}) async-start(f32[32,1,408]{2,1,0:T(1,128)} %reshape.35), calls=%async_computation | async-start | bytes 131072 | tf_op jit(solution)/shard_map/all_to_all | solution.py:47
  33.6 0.3 convolution_add_fusion.1
  33.9 0.4 fusion
  34.4 6.8 %all-to-all-done = f32[32,1,408]{2,1,0:T(1,128)S(1)} async-done(((f32[32,1,408]{2,1,0:T(1,128)}), f32[32,1,408]{2,1,0:T(1,128)S(1)}, u32[]{:S(2)}, u32[]{:S(2)}) %all-to-all-start) | async-done | bytes 52256 | tf_op jit(solution)/shard_map/all_to_all | solution.py:47
  41.1 0.5 broadcast.392
  41.6 0.8 reduce.6
  42.8 0.3 concatenate.70
  43.5 0.6 fusion.31
  44.3 35.2 %all_to_all.15 = f32[16,37,128]{2,1,0:T(8,128)S(1)} all-to-all(f32[16,37,128]{2,1,0:T(8,128)S(1)} %maximum_bitcast_fusion), channel_id=1, replica_groups=mesh['vox'=32,'tm'=16] {'tm'}, dimensions={0} | all-to-all | bytes 606208 | tf_op jit(solution)/shard_map/all_to_all | solution.py:54
  79.5 27.6 %all_to_all.16 = f32[16,37,128]{2,1,0:T(8,128)S(1)} all-to-all(f32[16,37,128]{2,1,0:T(8,128)S(1)} %broadcast_in_dim.9), channel_id=1, replica_groups=mesh['vox'=32,'tm'=16] {'tm'}, dimensions={0} | all-to-all | bytes 606208 | tf_op jit(solution)/shard_map/all_to_all | solution.py:56
  107.4 3.3 %cholesky.16 = f32[36,36]{1,0:T(8,128)S(1)} custom-call(f32[36,36]{1,0:T(8,128)S(1)} %fusion.105), custom_call_target="Cholesky" | custom-call | tf_op jit(solution)/shard_map/jit(cholesky)/cholesky | solution.py:130
  110.7 0.6 compare_reduce_fusion
  111.3 0.7 fusion.100
  112.0 2.8 %custom-call.10 = f32[1,36,36]{1,2,0:T(8,128)S(1)} custom-call(f32[1,36,36]{2,1,0:T(8,128)S(1)} %fusion.100), custom_call_target="InvertDiagBlocksLowerTriangular" | custom-call | tf_op jit(solution)/shard_map/jit(_cho_solve)/triangular_solve | solution.py:131
  114.7 0.2 fusion.103
  115.0 0.2 fusion.101
  115.4 2.0 %convolution_subtract_fusion = f32[128,2048]{1,0:T(8,128)} fusion(f32[36,128]{1,0:T(8,128)S(1)} %fusion.101, f32[36,2048]{1,0:T(8,128)S(1)} %bitcast.52, f32[16,2048]{1,0:T(8,128)S(1)} %fusion.99, f32[96,2048]{1,0:T(8,128)S(1)} %fusion.30, f32[16,2048]{1,0:T(8,128)S(1)} %slice.537), kind=kOutput, calls=%fused_computation | convolution fusion | flops 114032640 | bytes 2410496 | tf_op jit(solution)/shard_map/dot_general | solution.py:17
  (60 shorter events, 2.9 us)
Async XLA Ops:
  0.0 15.7 %copy-start = (f32[3,2048]{1,0:T(4,128)S(1)}, f32[3,2048]{1,0:T(4,128)}, u32[]{:S(2)}) copy-start(f32[3,2048]{1,0:T(4,128)} %param.7) | copy-start | bytes 73732
  0.0 9.6 %copy-start.2 = (f32[128,2048]{1,0:T(8,128)S(1)}, f32[128,2048]{1,0:T(8,128)}, u32[]{:S(2)}) copy-start(f32[128,2048]{1,0:T(8,128)} %param.4) | copy-start | bytes 3145732
  1.1 3.7 %copy-start.4 = (f32[128,6]{0,1:T(8,128)S(1)}, f32[128,6]{0,1:T(8,128)}, u32[]{:S(2)}) copy-start(f32[128,6]{0,1:T(8,128)} %param.6) | copy-start | bytes 9220
  2.1 7.5 %copy-start.1 = (s32[128,2048]{1,0:T(8,128)S(1)}, s32[128,2048]{1,0:T(8,128)}, u32[]{:S(2)}) copy-start(s32[128,2048]{1,0:T(8,128)} %param.5) | copy-start | bytes 3145732
  2.8 13.6 %collective-permute-start.1 = (f32[32,2048]{1,0:T(8,128)}, f32[32,2048]{1,0:T(8,128)S(1)}, u32[]{:S(2)}, u32[]{:S(2)}) collective-permute-start(f32[32,2048]{1,0:T(8,128)} %pad_maximum_fusion.4), channel_id=1, source_target_pairs={{1,0},{2,1},{3,2},{4,3},{5,4},{6,5},{7,6},{8,7},{9,8},{10,9},{11,1... | collective-permute-start | bytes 786440 | tf_op jit(solution)/shard_map/ppermute | solution.py:13
  5.8 12.7 %collective-permute-start = (f32[40,2048]{1,0:T(8,128)}, f32[40,2048]{1,0:T(8,128)}, u32[]{:S(2)}, u32[]{:S(2)}) collective-permute-start(f32[40,2048]{1,0:T(8,128)} %select_maximum_fusion), channel_id=1, source_target_pairs={{15,0},{0,1},{1,2},{2,3},{3,4},{4,5},{5,6},{6,7},{7,8},{8,9},{9,10... | collective-permute-start | bytes 983048 | tf_op jit(solution)/shard_map/ppermute | solution.py:13
  23.4 0.9 copy-start.3
  26.8 14.3 %all-to-all-start = ((f32[32,1,408]{2,1,0:T(1,128)}), f32[32,1,408]{2,1,0:T(1,128)S(1)}, u32[]{:S(2)}, u32[]{:S(2)}) async-start(f32[32,1,408]{2,1,0:T(1,128)} %reshape.35), calls=%async_computation | async-start | bytes 131072 | tf_op jit(solution)/shard_map/all_to_all | solution.py:47

commit v9 on v5

--- a/solution.py
+++ b/solution.py
@@ -43,8 +43,9 @@
 
 def sum_over_vox(block):
     n = lax.axis_size("vox")
-    copies = jnp.broadcast_to(block, (n,) + block.shape)
-    return lax.all_to_all(copies, "vox", 0, 0, tiled=False).sum(axis=0)
+    flat = block.reshape(1, block.size)
+    copies = jnp.broadcast_to(flat, (n,) + flat.shape)
+    return lax.all_to_all(copies, "vox", 0, 0, tiled=False).sum(axis=0).reshape(block.shape)
 
 
 def sum_over_tm(block):

time: 114 us -> 112 us (0.982)
  no operation moved by 1% of the time
where the time goes in v9:
time: 112 us
  blocking collectives  63.5 us (57%)
  other arithmetic  18.2 us (16%)
  starting transfers between devices  12.1 us (11%)
  waiting for transfers between devices  8.98 us (8%)
  local copies, waits for them, and re-layouts  4.35 us (4%)
  matrix products  4.31 us (4%)
    all_to_all x1, blocking collectives, sum_over_tm(): owned = lax.all_to_all(parts, 'tm', 0, 0, tiled=False).sum(axis=0)  35.9 us
    all_to_all x1, blocking collectives, sum_over_tm(): gathered = lax.all_to_all(copies, 'tm', 0, 0, tiled=False)  27.6 us
    mul x11, other arithmetic, despike_trimmed(): approx = (current + lagged) * 0.5  8.04 us
    all_to_all x1, waiting for transfers between devices, sum_over_vox(): lax.all_to_all(copies, 'vox', 0, 0, tiled=False).sum(axis=0)  7.44 us
    all_to_all x1, starting transfers between devices, sum_over_vox(): lax.all_to_all(copies, 'vox', 0, 0, tiled=False).sum(axis=0)  6.16 us
    ppermute x2, starting transfers between devices, from_behind(): return lax.ppermute(block, axis, route)  5.97 us
    another operation x3, other arithmetic, local(): factor = jnp.linalg.cholesky(gram_matrix)  3.96 us
    dot_general x4, matrix products, precise_product(): jnp.dot(left, right, precision=lax.Precision.HIGHEST, preferred_element_t...  3.9 us
  transfers between devices with their start and end apart: 3, of which 2 were waited for; matrix products, arithmetic and copies ran while one was open for 6% of the time, Pallas kernels for 0%

profile of v9, /device:TPU:64, one launch (start us, length us, event | category | flops | bytes accessed | tf_op | source)
XLA Modules:
  0.0 111.9 jit_solution(1578215122739512203)
XLA Ops:
  0.0 1.1 fusion.111
  1.1 1.0 slice_convert_fusion.3
  2.1 2.1 %collective-permute-start.1 = (f32[32,2048]{1,0:T(8,128)S(1)}, f32[32,2048]{1,0:T(8,128)S(1)}, u32[]{:S(2)}, u32[]{:S(2)}) collective-permute-start(f32[32,2048]{1,0:T(8,128)S(1)} %pad_maximum_fusion.10), channel_id=1, source_target_pairs={{1,0},{2,1},{3,2},{4,3},{5,4},{6,5},{7,6},{8,7},{9,8},{10,9},{11,1... | collective-permute-start | bytes 786440 | tf_op jit(solution)/shard_map/ppermute | solution.py:13
  4.4 0.1 copy.41
  4.5 3.8 %collective-permute-start = (f32[40,2048]{1,0:T(8,128)S(1)}, f32[40,2048]{1,0:T(8,128)S(1)}, u32[]{:S(2)}, u32[]{:S(2)}) collective-permute-start(f32[40,2048]{1,0:T(8,128)S(1)} %select_maximum_fusion), channel_id=1, source_target_pairs={{15,0},{0,1},{1,2},{2,3},{3,4},{4,5},{5,6},{6,7},{7,8},{8,9},{9,10... | collective-permute-start | bytes 983048 | tf_op jit(solution)/shard_map/ppermute | solution.py:13
  8.4 0.8 add_multiply_fusion.2
  9.2 1.3 %add_multiply_fusion.1 = (f32[125,2048]{1,0:T(8,128)S(1)}, f32[125,2048]{1,0:T(8,128)S(1)}) fusion(f32[127,2048]{1,0:T(8,128)S(1)} %get-tuple-element.21, s32[128,2048]{1,0:T(8,128)S(1)} %copy-done.1), kind=kLoop, calls=%fused_computation.47 | loop fusion | flops 8448000 | bytes 5120000 | tf_op jit(solution)/shard_map/mul | solution.py:35
  10.5 1.3 %add_multiply_fusion = (f32[121,2048]{1,0:T(8,128)S(1)}, f32[121,2048]{1,0:T(8,128)S(1)}) fusion(f32[125,2048]{1,0:T(8,128)S(1)} %get-tuple-element.19, s32[128,2048]{1,0:T(8,128)S(1)} %copy-done.1), kind=kLoop, calls=%fused_computation.46 | loop fusion | flops 8177664 | bytes 4956160 | tf_op jit(solution)/shard_map/mul | solution.py:35
  11.8 1.2 %add_multiply_fusion.3 = (f32[113,2048]{1,0:T(8,128)S(1)}, f32[113,2048]{1,0:T(8,128)S(1)}) fusion(f32[121,2048]{1,0:T(8,128)S(1)} %get-tuple-element.17, s32[128,2048]{1,0:T(8,128)S(1)} %copy-done.1), kind=kLoop, calls=%fused_computation.57 | loop fusion | flops 7636992 | bytes 4628480 | tf_op jit(solution)/shard_map/mul | solution.py:35
  13.0 0.1 fusion.24
  13.1 0.2 fusion.28
  13.4 0.3 fusion.26
  13.7 0.4 fusion.113
  14.0 0.3 fusion.30
  14.5 0.3 add_multiply_fusion.6
  14.8 0.5 add_multiply_fusion.5
  15.4 1.5 %collective-permute-done = f32[40,2048]{1,0:T(8,128)S(1)} collective-permute-done((f32[40,2048]{1,0:T(8,128)S(1)}, f32[40,2048]{1,0:T(8,128)S(1)}, u32[]{:S(2)}, u32[]{:S(2)}) %collective-permute-start) | collective-permute-done | bytes 327712 | tf_op jit(solution)/shard_map/ppermute | solution.py:13
  16.9 0.3 add_multiply_fusion.9
  17.2 0.5 add_multiply_fusion.8
  17.8 1.0 add_multiply_fusion.4
  18.8 0.4 add_multiply_fusion.10
  19.4 0.4 add_multiply_fusion.11
  20.2 1.1 fusion
  21.3 0.2 reshape.71
  21.5 0.7 broadcast_in_dim.12
  22.1 6.2 %all-to-all-start = ((f32[32,1,408]{2,1,0:T(1,128)}), f32[32,1,408]{2,1,0:T(1,128)S(1)}, u32[]{:S(2)}, u32[]{:S(2)}) async-start(f32[32,1,408]{2,1,0:T(1,128)} %broadcast_in_dim.12), calls=%async_computation | async-start | bytes 131072 | tf_op jit(solution)/shard_map/all_to_all | solution.py:48
  28.3 7.4 %all-to-all-done = f32[32,1,408]{2,1,0:T(1,128)S(1)} async-done(((f32[32,1,408]{2,1,0:T(1,128)}), f32[32,1,408]{2,1,0:T(1,128)S(1)}, u32[]{:S(2)}, u32[]{:S(2)}) %all-to-all-start) | async-done | bytes 52256 | tf_op jit(solution)/shard_map/all_to_all | solution.py:48
  35.9 0.1 slice_bitcast_fusion
  36.1 0.1 copy.34
  36.2 0.2 slice.486
  36.5 0.1 fusion.109
  36.6 0.4 concatenate.66
  37.0 0.2 fusion.119
  37.2 0.1 reshape.72
  37.3 0.7 fusion.31
  38.0 0.1 copy.36
  38.2 35.9 %all_to_all.15 = f32[16,37,128]{2,1,0:T(8,128)S(1)} all-to-all(f32[16,37,128]{2,1,0:T(8,128)S(1)} %maximum_bitcast_fusion), channel_id=1, replica_groups=mesh['vox'=32,'tm'=16] {'tm'}, dimensions={0} | all-to-all | bytes 606208 | tf_op jit(solution)/shard_map/all_to_all | solution.py:55
  74.1 27.6 %all_to_all.16 = f32[16,37,128]{2,1,0:T(8,128)S(1)} all-to-all(f32[16,37,128]{2,1,0:T(8,128)S(1)} %broadcast_in_dim.13), channel_id=1, replica_groups=mesh['vox'=32,'tm'=16] {'tm'}, dimensions={0} | all-to-all | bytes 606208 | tf_op jit(solution)/shard_map/all_to_all | solution.py:57
  101.7 0.1 reshape.74
  101.8 0.1 copy.37
  101.9 3.3 %cholesky.16 = f32[36,36]{1,0:T(8,128)S(1)} custom-call(f32[36,36]{1,0:T(8,128)S(1)} %fusion.104), custom_call_target="Cholesky" | custom-call | tf_op jit(solution)/shard_map/jit(cholesky)/cholesky | solution.py:111
  105.2 0.6 compare_reduce_fusion
  105.9 0.7 fusion.99
  106.5 2.8 %custom-call.10 = f32[1,36,36]{1,2,0:T(8,128)S(1)} custom-call(f32[1,36,36]{2,1,0:T(8,128)S(1)} %fusion.99), custom_call_target="InvertDiagBlocksLowerTriangular" | custom-call | tf_op jit(solution)/shard_map/jit(_cho_solve)/triangular_solve | solution.py:112
  109.3 0.2 fusion.102
  109.5 0.2 fusion.100
  109.8 0.1 copy.43
  109.9 2.0 %convolution_subtract_fusion = f32[128,2048]{1,0:T(8,128)} fusion(f32[36,128]{1,0:T(8,128)S(1)} %fusion.100, f32[36,2048]{1,0:T(8,128)S(1)} %bitcast.37, f32[16,2048]{1,0:T(8,128)S(1)} %fusion.98, f32[96,2048]{1,0:T(8,128)S(1)} %fusion.30, f32[16,2048]{1,0:T(8,128)S(1)} %slice.527), kind=kOutput, calls=%fused_computation | convolution fusion | flops 114032640 | bytes 2410496 | tf_op jit(solution)/shard_map/dot_general | solution.py:17
  (47 shorter events, 1.5 us)
Async XLA Ops:
  0.0 20.2 %copy-start = (f32[3,2048]{1,0:T(4,128)S(1)}, f32[3,2048]{1,0:T(4,128)}, u32[]{:S(2)}) copy-start(f32[3,2048]{1,0:T(4,128)} %param.7) | copy-start | bytes 73732
  0.0 8.3 %copy-start.2 = (f32[128,2048]{1,0:T(8,128)S(1)}, f32[128,2048]{1,0:T(8,128)}, u32[]{:S(2)}) copy-start(f32[128,2048]{1,0:T(8,128)} %param.4) | copy-start | bytes 3145732
  0.0 4.3 %copy-start.3 = (f32[128,6]{0,1:T(8,128)S(1)}, f32[128,6]{0,1:T(8,128)}, u32[]{:S(2)}) copy-start(f32[128,6]{0,1:T(8,128)} %param.6) | copy-start | bytes 9220
  2.1 6.3 %copy-start.1 = (s32[128,2048]{1,0:T(8,128)S(1)}, s32[128,2048]{1,0:T(8,128)}, u32[]{:S(2)}) copy-start(s32[128,2048]{1,0:T(8,128)} %param.5) | copy-start | bytes 3145732
  2.1 12.3 %collective-permute-start.1 = (f32[32,2048]{1,0:T(8,128)S(1)}, f32[32,2048]{1,0:T(8,128)S(1)}, u32[]{:S(2)}, u32[]{:S(2)}) collective-permute-start(f32[32,2048]{1,0:T(8,128)S(1)} %pad_maximum_fusion.10), channel_id=1, source_target_pairs={{1,0},{2,1},{3,2},{4,3},{5,4},{6,5},{7,6},{8,7},{9,8},{10,9},{11,1... | collective-permute-start | bytes 786440 | tf_op jit(solution)/shard_map/ppermute | solution.py:13
  4.5 12.4 %collective-permute-start = (f32[40,2048]{1,0:T(8,128)S(1)}, f32[40,2048]{1,0:T(8,128)S(1)}, u32[]{:S(2)}, u32[]{:S(2)}) collective-permute-start(f32[40,2048]{1,0:T(8,128)S(1)} %select_maximum_fusion), channel_id=1, source_target_pairs={{15,0},{0,1},{1,2},{2,3},{3,4},{4,5},{5,6},{6,7},{7,8},{8,9},{9,10... | collective-permute-start | bytes 983048 | tf_op jit(solution)/shard_map/ppermute | solution.py:13
  22.1 13.6 %all-to-all-start = ((f32[32,1,408]{2,1,0:T(1,128)}), f32[32,1,408]{2,1,0:T(1,128)S(1)}, u32[]{:S(2)}, u32[]{:S(2)}) async-start(f32[32,1,408]{2,1,0:T(1,128)} %broadcast_in_dim.12), calls=%async_computation | async-start | bytes 131072 | tf_op jit(solution)/shard_map/all_to_all | solution.py:48

commit v10 on v9

--- a/solution.py
+++ b/solution.py
@@ -110,7 +110,8 @@
     gram_matrix = summed[terms:].reshape(-1)[: terms * terms].reshape(terms, terms)
     factor = jnp.linalg.cholesky(gram_matrix)
     weights = jax.scipy.linalg.cho_solve((factor, True), nuisance_matrix.T)
-    return spike_free_series - precise_product(weights.T, cross_products)
+    fit = jnp.dot(weights.T, cross_products, precision=lax.Precision.HIGH, preferred_element_type=jnp.float32)
+    return spike_free_series - fit
 
 
 def solution(mesh):

time: 112 us -> 112 us (level)
    dot_general x4 -> x3, matrix products: 3.9 us -> 1.9 us  [precise_product(): jnp.dot(left, right, precision=lax.Precision.HIGHEST, preferred_element_t...]
    dot_general x0 -> x1, matrix products: none -> 1.59 us  [local(): jnp.dot(weights.T, cross_products, precision=lax.Precision.HIGH, preferre...]
where the time goes in v10:
time: 112 us
  blocking collectives  63.5 us (57%)
  other arithmetic  18.2 us (16%)
  starting transfers between devices  12.1 us (11%)
  waiting for transfers between devices  8.98 us (8%)
  local copies, waits for them, and re-layouts  4.35 us (4%)
  matrix products  3.9 us (3%)
    all_to_all x1, blocking collectives, sum_over_tm(): owned = lax.all_to_all(parts, 'tm', 0, 0, tiled=False).sum(axis=0)  35.9 us
    all_to_all x1, blocking collectives, sum_over_tm(): gathered = lax.all_to_all(copies, 'tm', 0, 0, tiled=False)  27.6 us
    mul x11, other arithmetic, despike_trimmed(): approx = (current + lagged) * 0.5  8.04 us
    all_to_all x1, waiting for transfers between devices, sum_over_vox(): lax.all_to_all(copies, 'vox', 0, 0, tiled=False).sum(axis=0)  7.44 us
    all_to_all x1, starting transfers between devices, sum_over_vox(): lax.all_to_all(copies, 'vox', 0, 0, tiled=False).sum(axis=0)  6.16 us
    ppermute x2, starting transfers between devices, from_behind(): return lax.ppermute(block, axis, route)  5.97 us
    another operation x3, other arithmetic, local(): factor = jnp.linalg.cholesky(gram_matrix)  3.96 us
    another operation x2, other arithmetic, local(): weights = jax.scipy.linalg.cho_solve((factor, True), nuisance_matrix.T)  3.4 us
  transfers between devices with their start and end apart: 3, of which 2 were waited for; matrix products, arithmetic and copies ran while one was open for 6% of the time, Pallas kernels for 0%

profile of v10, /device:TPU:64, one launch (start us, length us, event | category | flops | bytes accessed | tf_op | source)
XLA Modules:
  0.0 111.5 jit_solution(18377683311057441290)
XLA Ops:
  0.0 1.1 fusion.111
  1.1 1.0 slice_convert_fusion.3
  2.1 2.1 %collective-permute-start.1 = (f32[32,2048]{1,0:T(8,128)S(1)}, f32[32,2048]{1,0:T(8,128)S(1)}, u32[]{:S(2)}, u32[]{:S(2)}) collective-permute-start(f32[32,2048]{1,0:T(8,128)S(1)} %pad_maximum_fusion.10), channel_id=1, source_target_pairs={{1,0},{2,1},{3,2},{4,3},{5,4},{6,5},{7,6},{8,7},{9,8},{10,9},{11,1... | collective-permute-start | bytes 786440 | tf_op jit(solution)/shard_map/ppermute | solution.py:13
  4.4 0.1 copy.41
  4.5 3.8 %collective-permute-start = (f32[40,2048]{1,0:T(8,128)S(1)}, f32[40,2048]{1,0:T(8,128)S(1)}, u32[]{:S(2)}, u32[]{:S(2)}) collective-permute-start(f32[40,2048]{1,0:T(8,128)S(1)} %select_maximum_fusion), channel_id=1, source_target_pairs={{15,0},{0,1},{1,2},{2,3},{3,4},{4,5},{5,6},{6,7},{7,8},{8,9},{9,10... | collective-permute-start | bytes 983048 | tf_op jit(solution)/shard_map/ppermute | solution.py:13
  8.4 0.8 add_multiply_fusion.2
  9.2 1.3 %add_multiply_fusion.1 = (f32[125,2048]{1,0:T(8,128)S(1)}, f32[125,2048]{1,0:T(8,128)S(1)}) fusion(f32[127,2048]{1,0:T(8,128)S(1)} %get-tuple-element.21, s32[128,2048]{1,0:T(8,128)S(1)} %copy-done.1), kind=kLoop, calls=%fused_computation.47 | loop fusion | flops 8448000 | bytes 5120000 | tf_op jit(solution)/shard_map/mul | solution.py:35
  10.5 1.3 %add_multiply_fusion = (f32[121,2048]{1,0:T(8,128)S(1)}, f32[121,2048]{1,0:T(8,128)S(1)}) fusion(f32[125,2048]{1,0:T(8,128)S(1)} %get-tuple-element.19, s32[128,2048]{1,0:T(8,128)S(1)} %copy-done.1), kind=kLoop, calls=%fused_computation.46 | loop fusion | flops 8177664 | bytes 4956160 | tf_op jit(solution)/shard_map/mul | solution.py:35
  11.8 1.2 %add_multiply_fusion.3 = (f32[113,2048]{1,0:T(8,128)S(1)}, f32[113,2048]{1,0:T(8,128)S(1)}) fusion(f32[121,2048]{1,0:T(8,128)S(1)} %get-tuple-element.17, s32[128,2048]{1,0:T(8,128)S(1)} %copy-done.1), kind=kLoop, calls=%fused_computation.57 | loop fusion | flops 7636992 | bytes 4628480 | tf_op jit(solution)/shard_map/mul | solution.py:35
  13.0 0.1 fusion.24
  13.1 0.2 fusion.28
  13.4 0.3 fusion.26
  13.7 0.4 fusion.113
  14.0 0.3 fusion.30
  14.5 0.3 add_multiply_fusion.6
  14.8 0.5 add_multiply_fusion.5
  15.4 1.5 %collective-permute-done = f32[40,2048]{1,0:T(8,128)S(1)} collective-permute-done((f32[40,2048]{1,0:T(8,128)S(1)}, f32[40,2048]{1,0:T(8,128)S(1)}, u32[]{:S(2)}, u32[]{:S(2)}) %collective-permute-start) | collective-permute-done | bytes 327712 | tf_op jit(solution)/shard_map/ppermute | solution.py:13
  16.9 0.3 add_multiply_fusion.9
  17.2 0.5 add_multiply_fusion.8
  17.8 1.0 add_multiply_fusion.4
  18.8 0.4 add_multiply_fusion.10
  19.4 0.4 add_multiply_fusion.11
  20.2 1.1 fusion
  21.3 0.2 reshape.71
  21.5 0.7 broadcast_in_dim.12
  22.1 6.2 %all-to-all-start = ((f32[32,1,408]{2,1,0:T(1,128)}), f32[32,1,408]{2,1,0:T(1,128)S(1)}, u32[]{:S(2)}, u32[]{:S(2)}) async-start(f32[32,1,408]{2,1,0:T(1,128)} %broadcast_in_dim.12), calls=%async_computation | async-start | bytes 131072 | tf_op jit(solution)/shard_map/all_to_all | solution.py:48
  28.3 7.4 %all-to-all-done = f32[32,1,408]{2,1,0:T(1,128)S(1)} async-done(((f32[32,1,408]{2,1,0:T(1,128)}), f32[32,1,408]{2,1,0:T(1,128)S(1)}, u32[]{:S(2)}, u32[]{:S(2)}) %all-to-all-start) | async-done | bytes 52256 | tf_op jit(solution)/shard_map/all_to_all | solution.py:48
  35.9 0.1 slice_bitcast_fusion
  36.1 0.1 copy.34
  36.2 0.2 slice.486
  36.5 0.1 fusion.109
  36.6 0.4 concatenate.66
  37.0 0.2 fusion.119
  37.2 0.1 reshape.72
  37.3 0.7 fusion.31
  38.0 0.1 copy.36
  38.2 35.9 %all_to_all.15 = f32[16,37,128]{2,1,0:T(8,128)S(1)} all-to-all(f32[16,37,128]{2,1,0:T(8,128)S(1)} %maximum_bitcast_fusion), channel_id=1, replica_groups=mesh['vox'=32,'tm'=16] {'tm'}, dimensions={0} | all-to-all | bytes 606208 | tf_op jit(solution)/shard_map/all_to_all | solution.py:55
  74.1 27.6 %all_to_all.16 = f32[16,37,128]{2,1,0:T(8,128)S(1)} all-to-all(f32[16,37,128]{2,1,0:T(8,128)S(1)} %broadcast_in_dim.13), channel_id=1, replica_groups=mesh['vox'=32,'tm'=16] {'tm'}, dimensions={0} | all-to-all | bytes 606208 | tf_op jit(solution)/shard_map/all_to_all | solution.py:57
  101.7 0.1 reshape.74
  101.8 0.1 copy.37
  101.9 3.3 %cholesky.16 = f32[36,36]{1,0:T(8,128)S(1)} custom-call(f32[36,36]{1,0:T(8,128)S(1)} %fusion.104), custom_call_target="Cholesky" | custom-call | tf_op jit(solution)/shard_map/jit(cholesky)/cholesky | solution.py:111
  105.2 0.6 compare_reduce_fusion
  105.9 0.7 fusion.99
  106.5 2.8 %custom-call.10 = f32[1,36,36]{1,2,0:T(8,128)S(1)} custom-call(f32[1,36,36]{2,1,0:T(8,128)S(1)} %fusion.99), custom_call_target="InvertDiagBlocksLowerTriangular" | custom-call | tf_op jit(solution)/shard_map/jit(_cho_solve)/triangular_solve | solution.py:112
  109.3 0.2 fusion.102
  109.5 0.2 fusion.100
  109.8 0.1 copy.43
  109.9 1.6 %convolution_subtract_fusion = f32[128,2048]{1,0:T(8,128)} fusion(f32[36,128]{1,0:T(8,128)S(1)} %fusion.100, f32[36,2048]{1,0:T(8,128)S(1)} %bitcast.37, f32[16,2048]{1,0:T(8,128)S(1)} %fusion.98, f32[96,2048]{1,0:T(8,128)S(1)} %fusion.30, f32[16,2048]{1,0:T(8,128)S(1)} %slice.527), kind=kOutput, calls=%fused_computation | convolution fusion | flops 57409536 | bytes 2410496 | tf_op jit(solution)/shard_map/dot_general | solution.py:113
  (47 shorter events, 1.5 us)
Async XLA Ops:
  0.0 20.2 %copy-start = (f32[3,2048]{1,0:T(4,128)S(1)}, f32[3,2048]{1,0:T(4,128)}, u32[]{:S(2)}) copy-start(f32[3,2048]{1,0:T(4,128)} %param.7) | copy-start | bytes 73732
  0.0 8.3 %copy-start.2 = (f32[128,2048]{1,0:T(8,128)S(1)}, f32[128,2048]{1,0:T(8,128)}, u32[]{:S(2)}) copy-start(f32[128,2048]{1,0:T(8,128)} %param.4) | copy-start | bytes 3145732
  0.0 4.3 %copy-start.3 = (f32[128,6]{0,1:T(8,128)S(1)}, f32[128,6]{0,1:T(8,128)}, u32[]{:S(2)}) copy-start(f32[128,6]{0,1:T(8,128)} %param.6) | copy-start | bytes 9220
  2.1 6.3 %copy-start.1 = (s32[128,2048]{1,0:T(8,128)S(1)}, s32[128,2048]{1,0:T(8,128)}, u32[]{:S(2)}) copy-start(s32[128,2048]{1,0:T(8,128)} %param.5) | copy-start | bytes 3145732
  2.1 12.3 %collective-permute-start.1 = (f32[32,2048]{1,0:T(8,128)S(1)}, f32[32,2048]{1,0:T(8,128)S(1)}, u32[]{:S(2)}, u32[]{:S(2)}) collective-permute-start(f32[32,2048]{1,0:T(8,128)S(1)} %pad_maximum_fusion.10), channel_id=1, source_target_pairs={{1,0},{2,1},{3,2},{4,3},{5,4},{6,5},{7,6},{8,7},{9,8},{10,9},{11,1... | collective-permute-start | bytes 786440 | tf_op jit(solution)/shard_map/ppermute | solution.py:13
  4.5 12.4 %collective-permute-start = (f32[40,2048]{1,0:T(8,128)S(1)}, f32[40,2048]{1,0:T(8,128)S(1)}, u32[]{:S(2)}, u32[]{:S(2)}) collective-permute-start(f32[40,2048]{1,0:T(8,128)S(1)} %select_maximum_fusion), channel_id=1, source_target_pairs={{15,0},{0,1},{1,2},{2,3},{3,4},{4,5},{5,6},{6,7},{7,8},{8,9},{9,10... | collective-permute-start | bytes 983048 | tf_op jit(solution)/shard_map/ppermute | solution.py:13
  22.1 13.6 %all-to-all-start = ((f32[32,1,408]{2,1,0:T(1,128)}), f32[32,1,408]{2,1,0:T(1,128)S(1)}, u32[]{:S(2)}, u32[]{:S(2)}) async-start(f32[32,1,408]{2,1,0:T(1,128)} %broadcast_in_dim.12), calls=%async_computation | async-start | bytes 131072 | tf_op jit(solution)/shard_map/all_to_all | solution.py:48

commit v11 on v9

--- a/solution.py
+++ b/solution.py
@@ -2,6 +2,7 @@
 import jax.numpy as jnp
 from jax import lax
 from jax.sharding import PartitionSpec as P
+from jax.experimental import pallas as pl
 
 LEVELS = 4
 HALO = 16
@@ -58,6 +59,57 @@
     return gathered.transpose(1, 0, 2).reshape(rows, cols)
 
 
+def solve_kernel(terms, gram_ref, rhs_ref, out_ref):
+    size = gram_ref.shape[0]
+    sub = lax.broadcasted_iota(jnp.int32, (size, size), 0)
+    lane = lax.broadcasted_iota(jnp.int32, (size, size), 1)
+    rsub = lax.broadcasted_iota(jnp.int32, rhs_ref.shape, 0)
+
+    def factor_step(k, carry):
+        a, low, low_t = carry
+        col = jnp.sum(jnp.where(lane == k, a, 0.0), axis=1, keepdims=True)
+        row = jnp.sum(jnp.where(sub == k, a, 0.0), axis=0, keepdims=True)
+        root = jnp.sqrt(jnp.sum(jnp.where(lane[:1] == k, row, 0.0)))
+        lcol = jnp.where(sub[:, :1] >= k, col / root, 0.0)
+        lrow = jnp.where(lane[:1] >= k, row / root, 0.0)
+        return a - lcol * lrow, low + jnp.where(lane == k, lcol, 0.0), low_t + jnp.where(sub == k, lrow, 0.0)
+
+    zero = jnp.zeros((size, size), jnp.float32)
+    _, low, low_t = lax.fori_loop(0, terms, factor_step, (gram_ref[...], zero, zero))
+    diag = jnp.sum(jnp.where(sub == lane, low, 0.0), axis=1, keepdims=True)
+
+    def forward(k, carry):
+        b, y = carry
+        yk = jnp.sum(jnp.where(rsub == k, b, 0.0), axis=0, keepdims=True) / jnp.sum(jnp.where(sub[:, :1] == k, diag, 0.0))
+        lcol = jnp.sum(jnp.where(lane == k, low, 0.0), axis=1, keepdims=True)
+        return b - lcol * yk, y + jnp.where(rsub == k, yk, 0.0)
+
+    _, y = lax.fori_loop(0, terms, forward, (rhs_ref[...], jnp.zeros(rhs_ref.shape, jnp.float32)))
+
+    def backward(step, carry):
+        k = terms - 1 - step
+        y, x = carry
+        xk = jnp.sum(jnp.where(rsub == k, y, 0.0), axis=0, keepdims=True) / jnp.sum(jnp.where(sub[:, :1] == k, diag, 0.0))
+        ucol = jnp.where(sub[:, :1] < k, jnp.sum(jnp.where(lane == k, low_t, 0.0), axis=1, keepdims=True), 0.0)
+        return y - ucol * xk, x + jnp.where(rsub == k, xk, 0.0)
+
+    _, x = lax.fori_loop(0, terms, backward, (y, jnp.zeros(rhs_ref.shape, jnp.float32)))
+    out_ref[...] = x
+
+
+def cholesky_solve(gram_matrix, rhs):
+    terms = gram_matrix.shape[0]
+    size = 128
+    padded = jnp.eye(size, dtype=jnp.float32).at[:terms, :terms].set(gram_matrix)
+    rows = -(-terms // 8) * 8
+    rhs_padded = jnp.pad(rhs, ((0, size - terms), (0, 0)))
+    out = pl.pallas_call(
+        lambda g, b, o: solve_kernel(terms, g, b, o),
+        out_shape=jax.ShapeDtypeStruct(rhs_padded.shape, jnp.float32),
+    )(padded, rhs_padded)
+    return out[:terms]
+
+
 def local(series, spikes, motion, tissue):
     frames = series.shape[0]
     voxels = series.shape[1]
@@ -108,8 +160,7 @@
     summed = sum_over_tm(packed)
     cross_products = summed[:terms]
     gram_matrix = summed[terms:].reshape(-1)[: terms * terms].reshape(terms, terms)
-    factor = jnp.linalg.cholesky(gram_matrix)
-    weights = jax.scipy.linalg.cho_solve((factor, True), nuisance_matrix.T)
+    weights = cholesky_solve(gram_matrix, nuisance_matrix.T)
     return spike_free_series - precise_product(weights.T, cross_products)
 
 

time: 112 us -> 129 us (1.15)
  blocking collectives: 63.5 us -> 35.9 us
  Pallas kernels: 0 us -> 21 us
  waiting for transfers between devices: 8.98 us -> 29 us
  other arithmetic: 18.2 us -> 10.9 us
  starting transfers between devices: 12.1 us -> 19.3 us
  local copies, waits for them, and re-layouts: 4.35 us -> 6.96 us
    all_to_all x1 -> x0, blocking collectives: 27.6 us -> none  [sum_over_tm(): gathered = lax.all_to_all(copies, 'tm', 0, 0, tiled=False)]
    pallas_call x0 -> x1, Pallas kernels: none -> 21 us  [cholesky_solve(): pl.pallas_call(lambda g, b, o: solve_kernel(terms, g, b, o), out_shape=ja...]
    all_to_all x0 -> x1, waiting for transfers between devices: none -> 20 us  [sum_over_tm(): gathered = lax.all_to_all(copies, 'tm', 0, 0, tiled=False)]
    another operation x5 -> x0, other arithmetic: 7.36 us -> none  [the longest x3 3.96 us: local(): factor = jnp.linalg.cholesky(gram_matrix)]
    all_to_all x0 -> x1, starting transfers between devices: none -> 7.15 us  [sum_over_tm(): gathered = lax.all_to_all(copies, 'tm', 0, 0, tiled=False)]
  transfers between devices with their start and end apart: 3 -> 4, of which waited for: 2 -> 3; matrix products, arithmetic and copies ran while one was open for 6% -> 6% of each run, Pallas kernels for 0% -> 0%
where the time goes in v11:
time: 129 us; the launch traced here: 128 us
  blocking collectives  35.9 us (28%)
  waiting for transfers between devices  29 us (22%)
  Pallas kernels  21 us (16%)
  starting transfers between devices  19.3 us (15%)
  other arithmetic  10.9 us (8%)
  local copies, waits for them, and re-layouts  6.96 us (5%)
  matrix products  4.62 us (4%)
    all_to_all x1, blocking collectives, sum_over_tm(): owned = lax.all_to_all(parts, 'tm', 0, 0, tiled=False).sum(axis=0)  35.9 us
    pallas_call x1, Pallas kernels, cholesky_solve(): pl.pallas_call(lambda g, b, o: solve_kernel(terms, g, b, o), out_shape=ja...  21 us
    all_to_all x1, waiting for transfers between devices, sum_over_tm(): gathered = lax.all_to_all(copies, 'tm', 0, 0, tiled=False)  20 us
    mul x11, other arithmetic, despike_trimmed(): approx = (current + lagged) * 0.5  8.04 us
    all_to_all x1, waiting for transfers between devices, sum_over_vox(): lax.all_to_all(copies, 'vox', 0, 0, tiled=False).sum(axis=0)  7.44 us
    all_to_all x1, starting transfers between devices, sum_over_tm(): gathered = lax.all_to_all(copies, 'tm', 0, 0, tiled=False)  7.15 us
    all_to_all x1, starting transfers between devices, sum_over_vox(): lax.all_to_all(copies, 'vox', 0, 0, tiled=False).sum(axis=0)  6.16 us
    ppermute x2, starting transfers between devices, from_behind(): return lax.ppermute(block, axis, route)  5.97 us
  transfers between devices with their start and end apart: 4, of which 3 were waited for; matrix products, arithmetic and copies ran while one was open for 6% of the time, Pallas kernels for 0%

profile of v11, /device:TPU:64, one launch (start us, length us, event | category | flops | bytes accessed | tf_op | source)
XLA Modules:
  0.0 128.0 jit_solution(2851837252588693468)
XLA Ops:
  0.0 1.1 fusion.107
  1.1 1.0 slice_convert_fusion.3
  2.1 2.1 %collective-permute-start.1 = (f32[32,2048]{1,0:T(8,128)S(1)}, f32[32,2048]{1,0:T(8,128)S(1)}, u32[]{:S(2)}, u32[]{:S(2)}) collective-permute-start(f32[32,2048]{1,0:T(8,128)S(1)} %pad_maximum_fusion.10), channel_id=1, source_target_pairs={{1,0},{2,1},{3,2},{4,3},{5,4},{6,5},{7,6},{8,7},{9,8},{10,9},{11,1... | collective-permute-start | bytes 786440 | tf_op jit(solution)/shard_map/ppermute | solution.py:14
  4.4 0.1 copy.42
  4.5 3.8 %collective-permute-start = (f32[40,2048]{1,0:T(8,128)S(1)}, f32[40,2048]{1,0:T(8,128)S(1)}, u32[]{:S(2)}, u32[]{:S(2)}) collective-permute-start(f32[40,2048]{1,0:T(8,128)S(1)} %select_maximum_fusion), channel_id=1, source_target_pairs={{15,0},{0,1},{1,2},{2,3},{3,4},{4,5},{5,6},{6,7},{7,8},{8,9},{9,10... | collective-permute-start | bytes 983048 | tf_op jit(solution)/shard_map/ppermute | solution.py:14
  8.4 0.8 add_multiply_fusion.2
  9.2 1.3 %add_multiply_fusion.1 = (f32[125,2048]{1,0:T(8,128)S(1)}, f32[125,2048]{1,0:T(8,128)S(1)}) fusion(f32[127,2048]{1,0:T(8,128)S(1)} %get-tuple-element.33, s32[128,2048]{1,0:T(8,128)S(1)} %copy-done.1), kind=kLoop, calls=%fused_computation.47 | loop fusion | flops 8448000 | bytes 5120000 | tf_op jit(solution)/shard_map/mul | solution.py:36
  10.5 1.3 %add_multiply_fusion = (f32[121,2048]{1,0:T(8,128)S(1)}, f32[121,2048]{1,0:T(8,128)S(1)}) fusion(f32[125,2048]{1,0:T(8,128)S(1)} %get-tuple-element.31, s32[128,2048]{1,0:T(8,128)S(1)} %copy-done.1), kind=kLoop, calls=%fused_computation.46 | loop fusion | flops 8177664 | bytes 4956160 | tf_op jit(solution)/shard_map/mul | solution.py:36
  11.8 1.2 add_multiply_fusion.3
  13.0 0.1 fusion.24
  13.1 0.2 fusion.28
  13.4 0.3 fusion.26
  13.7 0.4 fusion.109
  14.0 0.3 fusion.30
  14.5 0.3 add_multiply_fusion.6
  14.8 0.5 add_multiply_fusion.5
  15.4 1.5 %collective-permute-done = f32[40,2048]{1,0:T(8,128)S(1)} collective-permute-done((f32[40,2048]{1,0:T(8,128)S(1)}, f32[40,2048]{1,0:T(8,128)S(1)}, u32[]{:S(2)}, u32[]{:S(2)}) %collective-permute-start) | collective-permute-done | bytes 327712 | tf_op jit(solution)/shard_map/ppermute | solution.py:14
  16.9 0.3 add_multiply_fusion.9
  17.2 0.5 add_multiply_fusion.8
  17.8 1.0 add_multiply_fusion.4
  18.8 0.4 add_multiply_fusion.10
  19.4 0.4 add_multiply_fusion.11
  20.2 1.1 fusion
  21.3 0.2 reshape.89
  21.5 0.7 broadcast_in_dim.10
  22.1 6.2 %all-to-all-start = ((f32[32,1,408]{2,1,0:T(1,128)}), f32[32,1,408]{2,1,0:T(1,128)S(1)}, u32[]{:S(2)}, u32[]{:S(2)}) async-start(f32[32,1,408]{2,1,0:T(1,128)} %broadcast_in_dim.10), calls=%async_computation | async-start | bytes 131072 | tf_op jit(solution)/shard_map/all_to_all | solution.py:49
  28.3 7.4 %all-to-all-done = f32[32,1,408]{2,1,0:T(1,128)S(1)} async-done(((f32[32,1,408]{2,1,0:T(1,128)}), f32[32,1,408]{2,1,0:T(1,128)S(1)}, u32[]{:S(2)}, u32[]{:S(2)}) %all-to-all-start) | async-done | bytes 52256 | tf_op jit(solution)/shard_map/all_to_all | solution.py:49
  35.9 0.1 slice_bitcast_fusion
  36.0 0.1 pad_maximum_fusion.12
  36.1 0.1 copy.36
  36.2 0.2 slice.492
  36.5 0.1 fusion.105
  36.6 0.4 concatenate.68
  37.0 0.2 fusion.115
  37.2 0.1 reshape.90
  37.3 0.7 fusion.31
  38.0 0.1 copy.38
  38.2 35.9 %all_to_all.15 = f32[16,37,128]{2,1,0:T(8,128)S(1)} all-to-all(f32[16,37,128]{2,1,0:T(8,128)S(1)} %maximum_bitcast_fusion), channel_id=1, replica_groups=mesh['vox'=32,'tm'=16] {'tm'}, dimensions={0} | all-to-all | bytes 606208 | tf_op jit(solution)/shard_map/all_to_all | solution.py:56
  74.1 0.7 broadcast_in_dim.11
  74.8 7.2 %all-to-all-start.2 = ((f32[16,37,128]{2,1,0:T(8,128)}), f32[16,37,128]{2,1,0:T(8,128)S(1)}, u32[]{:S(2)}, u32[]{:S(2)}) async-start(f32[16,37,128]{2,1,0:T(8,128)} %broadcast_in_dim.11), calls=%async_computation.2 | async-start | bytes 655360 | tf_op jit(solution)/shard_map/all_to_all | solution.py:58
  82.0 0.6 pad.19.b
  82.6 20.0 %all-to-all-done.2 = f32[16,37,128]{2,1,0:T(8,128)S(1)} async-done(((f32[16,37,128]{2,1,0:T(8,128)}), f32[16,37,128]{2,1,0:T(8,128)S(1)}, u32[]{:S(2)}, u32[]{:S(2)}) %all-to-all-start.2) | async-done | bytes 303136 | tf_op jit(solution)/shard_map/all_to_all | solution.py:58
  102.6 0.1 reshape.92
  102.8 0.1 copy.44
  103.0 0.7 scatter.4.g
  103.7 0.6 copy-done.3
  104.3 21.0 %shard_map.46 = f32[128,128]{1,0:T(8,128)} custom-call(f32[128,128]{1,0:T(8,128)} %copy-done.3, f32[128,128]{1,0:T(8,128)} %pad.19.b), custom_call_target="tpu_custom_call" | custom-call | tf_op jit(solution)/shard_map/pallas_call | solution.py:106
  125.3 2.7 %convolution_subtract_fusion = f32[128,2048]{1,0:T(8,128)} fusion(f32[36,2048]{1,0:T(8,128)S(1)} %bitcast.24, f32[16,2048]{1,0:T(8,128)S(1)} %fusion.98, f32[96,2048]{1,0:T(8,128)S(1)} %fusion.30, f32[16,2048]{1,0:T(8,128)S(1)} %slice.534, f32[128,128]{1,0:T(8,128)} %shard_map.46), kind=kOutput, calls=%fused_computation | convolution fusion | flops 114032640 | bytes 2412544 | tf_op jit(solution)/shard_map/dot_general | solution.py:18
  (46 shorter events, 1.4 us)
Async XLA Ops:
  0.0 20.2 %copy-start = (f32[3,2048]{1,0:T(4,128)S(1)}, f32[3,2048]{1,0:T(4,128)}, u32[]{:S(2)}) copy-start(f32[3,2048]{1,0:T(4,128)} %param.9) | copy-start | bytes 73732
  0.0 8.3 %copy-start.2 = (f32[128,2048]{1,0:T(8,128)S(1)}, f32[128,2048]{1,0:T(8,128)}, u32[]{:S(2)}) copy-start(f32[128,2048]{1,0:T(8,128)} %param.6) | copy-start | bytes 3145732
  0.0 4.3 %copy-start.4 = (f32[128,6]{0,1:T(8,128)S(1)}, f32[128,6]{0,1:T(8,128)}, u32[]{:S(2)}) copy-start(f32[128,6]{0,1:T(8,128)} %param.8) | copy-start | bytes 9220
  2.1 6.3 %copy-start.1 = (s32[128,2048]{1,0:T(8,128)S(1)}, s32[128,2048]{1,0:T(8,128)}, u32[]{:S(2)}) copy-start(s32[128,2048]{1,0:T(8,128)} %param.7) | copy-start | bytes 3145732
  2.1 12.3 %collective-permute-start.1 = (f32[32,2048]{1,0:T(8,128)S(1)}, f32[32,2048]{1,0:T(8,128)S(1)}, u32[]{:S(2)}, u32[]{:S(2)}) collective-permute-start(f32[32,2048]{1,0:T(8,128)S(1)} %pad_maximum_fusion.10), channel_id=1, source_target_pairs={{1,0},{2,1},{3,2},{4,3},{5,4},{6,5},{7,6},{8,7},{9,8},{10,9},{11,1... | collective-permute-start | bytes 786440 | tf_op jit(solution)/shard_map/ppermute | solution.py:14
  4.5 12.4 %collective-permute-start = (f32[40,2048]{1,0:T(8,128)S(1)}, f32[40,2048]{1,0:T(8,128)S(1)}, u32[]{:S(2)}, u32[]{:S(2)}) collective-permute-start(f32[40,2048]{1,0:T(8,128)S(1)} %select_maximum_fusion), channel_id=1, source_target_pairs={{15,0},{0,1},{1,2},{2,3},{3,4},{4,5},{5,6},{6,7},{7,8},{8,9},{9,10... | collective-permute-start | bytes 983048 | tf_op jit(solution)/shard_map/ppermute | solution.py:14
  22.1 13.6 %all-to-all-start = ((f32[32,1,408]{2,1,0:T(1,128)}), f32[32,1,408]{2,1,0:T(1,128)S(1)}, u32[]{:S(2)}, u32[]{:S(2)}) async-start(f32[32,1,408]{2,1,0:T(1,128)} %broadcast_in_dim.10), calls=%async_computation | async-start | bytes 131072 | tf_op jit(solution)/shard_map/all_to_all | solution.py:49
  74.8 27.8 %all-to-all-start.2 = ((f32[16,37,128]{2,1,0:T(8,128)}), f32[16,37,128]{2,1,0:T(8,128)S(1)}, u32[]{:S(2)}, u32[]{:S(2)}) async-start(f32[16,37,128]{2,1,0:T(8,128)} %broadcast_in_dim.11), calls=%async_computation.2 | async-start | bytes 655360 | tf_op jit(solution)/shard_map/all_to_all | solution.py:58
  103.7 0.6 copy-start.3

commit v12 on v5

--- a/solution.py
+++ b/solution.py
@@ -43,8 +43,12 @@
 
 def sum_over_vox(block):
     n = lax.axis_size("vox")
-    copies = jnp.broadcast_to(block, (n,) + block.shape)
-    return lax.all_to_all(copies, "vox", 0, 0, tiled=False).sum(axis=0)
+    pair = block + lax.ppermute(block, "vox", [(i, i ^ 1) for i in range(n)])
+    flat = pair.reshape(1, pair.size)
+    copies = jnp.broadcast_to(flat, (n // 2,) + flat.shape)
+    groups = [list(range(0, n, 2)), list(range(1, n, 2))]
+    got = lax.all_to_all(copies, "vox", 0, 0, axis_index_groups=groups, tiled=False)
+    return got.sum(axis=0).reshape(block.shape)
 
 
 def sum_over_tm(block):

time: 114 us -> 113 us (level)
  blocking collectives: 63.5 us -> 61.5 us
  starting transfers between devices: 12.3 us -> 14 us
    ppermute x0 -> x1, starting transfers between devices: none -> 2.11 us  [sum_over_vox(): pair = block + lax.ppermute(block, 'vox', [(i, i ^ 1) for i in range(n)])]
    all_to_all x1, blocking collectives: 27.6 us -> 26.2 us  [sum_over_tm(): gathered = lax.all_to_all(copies, 'tm', 0, 0, tiled=False)]
  transfers between devices with their start and end apart: 3 -> 4, of which waited for: 2 -> 3; matrix products, arithmetic and copies ran while one was open for 6% -> 6% of each run, Pallas kernels for 0% -> 0%
where the time goes in v12:
time: 113 us
  blocking collectives  61.5 us (54%)
  other arithmetic  18.2 us (16%)
  starting transfers between devices  14 us (12%)
  waiting for transfers between devices  10 us (9%)
  local copies, waits for them, and re-layouts  4.42 us (4%)
  matrix products  4.27 us (4%)
    all_to_all x1, blocking collectives, sum_over_tm(): owned = lax.all_to_all(parts, 'tm', 0, 0, tiled=False).sum(axis=0)  35.3 us
    all_to_all x1, blocking collectives, sum_over_tm(): gathered = lax.all_to_all(copies, 'tm', 0, 0, tiled=False)  26.2 us
    mul x11, other arithmetic, despike_trimmed(): approx = (current + lagged) * 0.5  8.04 us
    all_to_all x1, waiting for transfers between devices, sum_over_vox(): lax.all_to_all(copies, 'vox', 0, 0, axis_index_groups=groups, tiled=False)  7.56 us
    ppermute x2, starting transfers between devices, from_behind(): return lax.ppermute(block, axis, route)  5.97 us
    all_to_all x1, starting transfers between devices, sum_over_vox(): lax.all_to_all(copies, 'vox', 0, 0, axis_index_groups=groups, tiled=False)  5.87 us
    another operation x3, other arithmetic, local(): factor = jnp.linalg.cholesky(gram_matrix)  3.96 us
    dot_general x4, matrix products, precise_product(): jnp.dot(left, right, precision=lax.Precision.HIGHEST, preferred_element_t...  3.86 us
  transfers between devices with their start and end apart: 4, of which 3 were waited for; matrix products, arithmetic and copies ran while one was open for 6% of the time, Pallas kernels for 0%

profile of v12, /device:TPU:64, one launch (start us, length us, event | category | flops | bytes accessed | tf_op | source)
XLA Modules:
  0.0 112.9 jit_solution(3974862063548036566)
XLA Ops:
  0.0 1.1 fusion.111
  1.1 1.0 slice_convert_fusion.3
  2.1 2.1 %collective-permute-start.1 = (f32[32,2048]{1,0:T(8,128)S(1)}, f32[32,2048]{1,0:T(8,128)S(1)}, u32[]{:S(2)}, u32[]{:S(2)}) collective-permute-start(f32[32,2048]{1,0:T(8,128)S(1)} %pad_maximum_fusion.10), channel_id=1, source_target_pairs={{1,0},{2,1},{3,2},{4,3},{5,4},{6,5},{7,6},{8,7},{9,8},{10,9},{11,1... | collective-permute-start | bytes 786440 | tf_op jit(solution)/shard_map/ppermute | solution.py:13
  4.4 0.1 copy.40
  4.5 3.8 %collective-permute-start = (f32[40,2048]{1,0:T(8,128)S(1)}, f32[40,2048]{1,0:T(8,128)S(1)}, u32[]{:S(2)}, u32[]{:S(2)}) collective-permute-start(f32[40,2048]{1,0:T(8,128)S(1)} %select_maximum_fusion), channel_id=1, source_target_pairs={{15,0},{0,1},{1,2},{2,3},{3,4},{4,5},{5,6},{6,7},{7,8},{8,9},{9,10... | collective-permute-start | bytes 983048 | tf_op jit(solution)/shard_map/ppermute | solution.py:13
  8.4 0.8 add_multiply_fusion.2
  9.2 1.3 %add_multiply_fusion.1 = (f32[125,2048]{1,0:T(8,128)S(1)}, f32[125,2048]{1,0:T(8,128)S(1)}) fusion(f32[127,2048]{1,0:T(8,128)S(1)} %get-tuple-element.21, s32[128,2048]{1,0:T(8,128)S(1)} %copy-done.1), kind=kLoop, calls=%fused_computation.47 | loop fusion | flops 8448000 | bytes 5120000 | tf_op jit(solution)/shard_map/mul | solution.py:35
  10.5 1.3 %add_multiply_fusion = (f32[121,2048]{1,0:T(8,128)S(1)}, f32[121,2048]{1,0:T(8,128)S(1)}) fusion(f32[125,2048]{1,0:T(8,128)S(1)} %get-tuple-element.19, s32[128,2048]{1,0:T(8,128)S(1)} %copy-done.1), kind=kLoop, calls=%fused_computation.46 | loop fusion | flops 8177664 | bytes 4956160 | tf_op jit(solution)/shard_map/mul | solution.py:35
  11.8 1.2 %add_multiply_fusion.3 = (f32[113,2048]{1,0:T(8,128)S(1)}, f32[113,2048]{1,0:T(8,128)S(1)}) fusion(f32[121,2048]{1,0:T(8,128)S(1)} %get-tuple-element.17, s32[128,2048]{1,0:T(8,128)S(1)} %copy-done.1), kind=kLoop, calls=%fused_computation.57 | loop fusion | flops 7636992 | bytes 4628480 | tf_op jit(solution)/shard_map/mul | solution.py:35
  13.0 0.1 fusion.24
  13.1 0.2 fusion.28
  13.4 0.3 fusion.26
  13.7 0.4 fusion.113
  14.0 0.3 fusion.30
  14.5 0.3 add_multiply_fusion.6
  14.8 0.5 add_multiply_fusion.5
  15.4 1.5 %collective-permute-done = f32[40,2048]{1,0:T(8,128)S(1)} collective-permute-done((f32[40,2048]{1,0:T(8,128)S(1)}, f32[40,2048]{1,0:T(8,128)S(1)}, u32[]{:S(2)}, u32[]{:S(2)}) %collective-permute-start) | collective-permute-done | bytes 327712 | tf_op jit(solution)/shard_map/ppermute | solution.py:13
  16.9 0.3 add_multiply_fusion.9
  17.2 0.5 add_multiply_fusion.8
  17.8 1.0 add_multiply_fusion.4
  18.8 0.4 add_multiply_fusion.10
  19.4 0.4 add_multiply_fusion.11
  20.2 1.0 fusion
  21.2 2.1 %collective-permute-start.2 = (f32[136,3]{0,1:T(4,128)S(1)}, f32[136,3]{0,1:T(4,128)S(1)}, u32[]{:S(2)}, u32[]{:S(2)}) collective-permute-start(f32[136,3]{0,1:T(4,128)S(1)} %fusion), channel_id=1, source_target_pairs={{0,16},{16,0},{32,48},{48,32},{64,80},{80,64},{96,112},{112,96},{1... | collective-permute-start | bytes 4904 | tf_op jit(solution)/shard_map/ppermute | solution.py:46
  23.3 1.0 collective-permute-done.2
  24.3 0.1 copy.31
  24.4 0.2 reshape.71
  24.6 0.6 broadcast_in_dim.12
  25.2 5.9 %all-to-all-start = ((f32[16,1,408]{2,1,0:T(1,128)}), f32[16,1,408]{2,1,0:T(1,128)S(1)}, u32[]{:S(2)}, u32[]{:S(2)}) async-start(f32[16,1,408]{2,1,0:T(1,128)} %broadcast_in_dim.12), calls=%async_computation | async-start | bytes 65536 | tf_op jit(solution)/shard_map/all_to_all | solution.py:50
  31.2 7.6 %all-to-all-done = f32[16,1,408]{2,1,0:T(1,128)S(1)} async-done(((f32[16,1,408]{2,1,0:T(1,128)}), f32[16,1,408]{2,1,0:T(1,128)S(1)}, u32[]{:S(2)}, u32[]{:S(2)}) %all-to-all-start) | async-done | bytes 26144 | tf_op jit(solution)/shard_map/all_to_all | solution.py:50
  39.0 0.1 copy.34
  39.1 0.2 slice.486
  39.5 0.4 concatenate.66
  39.9 0.2 fusion.119
  40.1 0.1 reshape.72
  40.2 0.7 fusion.31
  41.0 0.1 copy.36
  41.1 35.3 %all_to_all.15 = f32[16,37,128]{2,1,0:T(8,128)S(1)} all-to-all(f32[16,37,128]{2,1,0:T(8,128)S(1)} %maximum_bitcast_fusion), channel_id=1, replica_groups=mesh['vox'=32,'tm'=16] {'tm'}, dimensions={0} | all-to-all | bytes 606208 | tf_op jit(solution)/shard_map/all_to_all | solution.py:58
  76.4 26.2 %all_to_all.16 = f32[16,37,128]{2,1,0:T(8,128)S(1)} all-to-all(f32[16,37,128]{2,1,0:T(8,128)S(1)} %broadcast_in_dim.13), channel_id=1, replica_groups=mesh['vox'=32,'tm'=16] {'tm'}, dimensions={0} | all-to-all | bytes 606208 | tf_op jit(solution)/shard_map/all_to_all | solution.py:60
  102.6 0.1 reshape.74
  102.9 3.3 %cholesky.16 = f32[36,36]{1,0:T(8,128)S(1)} custom-call(f32[36,36]{1,0:T(8,128)S(1)} %fusion.104), custom_call_target="Cholesky" | custom-call | tf_op jit(solution)/shard_map/jit(cholesky)/cholesky | solution.py:114
  106.2 0.6 compare_reduce_fusion
  106.8 0.7 fusion.99
  107.5 2.8 %custom-call.10 = f32[1,36,36]{1,2,0:T(8,128)S(1)} custom-call(f32[1,36,36]{2,1,0:T(8,128)S(1)} %fusion.99), custom_call_target="InvertDiagBlocksLowerTriangular" | custom-call | tf_op jit(solution)/shard_map/jit(_cho_solve)/triangular_solve | solution.py:115
  110.2 0.2 fusion.102
  110.5 0.2 fusion.100
  110.7 0.1 copy.42
  110.9 2.0 %convolution_subtract_fusion = f32[128,2048]{1,0:T(8,128)} fusion(f32[36,128]{1,0:T(8,128)S(1)} %fusion.100, f32[36,2048]{1,0:T(8,128)S(1)} %bitcast.37, f32[16,2048]{1,0:T(8,128)S(1)} %fusion.98, f32[96,2048]{1,0:T(8,128)S(1)} %fusion.30, f32[16,2048]{1,0:T(8,128)S(1)} %slice.527), kind=kOutput, calls=%fused_computation | convolution fusion | flops 114032640 | bytes 2410496 | tf_op jit(solution)/shard_map/dot_general | solution.py:17
  (51 shorter events, 1.7 us)
Async XLA Ops:
  0.0 20.2 %copy-start = (f32[3,2048]{1,0:T(4,128)S(1)}, f32[3,2048]{1,0:T(4,128)}, u32[]{:S(2)}) copy-start(f32[3,2048]{1,0:T(4,128)} %param.7) | copy-start | bytes 73732
  0.0 8.3 %copy-start.2 = (f32[128,2048]{1,0:T(8,128)S(1)}, f32[128,2048]{1,0:T(8,128)}, u32[]{:S(2)}) copy-start(f32[128,2048]{1,0:T(8,128)} %param.4) | copy-start | bytes 3145732
  0.0 4.3 %copy-start.3 = (f32[128,6]{0,1:T(8,128)S(1)}, f32[128,6]{0,1:T(8,128)}, u32[]{:S(2)}) copy-start(f32[128,6]{0,1:T(8,128)} %param.6) | copy-start | bytes 9220
  2.1 6.3 %copy-start.1 = (s32[128,2048]{1,0:T(8,128)S(1)}, s32[128,2048]{1,0:T(8,128)}, u32[]{:S(2)}) copy-start(s32[128,2048]{1,0:T(8,128)} %param.5) | copy-start | bytes 3145732
  2.1 12.3 %collective-permute-start.1 = (f32[32,2048]{1,0:T(8,128)S(1)}, f32[32,2048]{1,0:T(8,128)S(1)}, u32[]{:S(2)}, u32[]{:S(2)}) collective-permute-start(f32[32,2048]{1,0:T(8,128)S(1)} %pad_maximum_fusion.10), channel_id=1, source_target_pairs={{1,0},{2,1},{3,2},{4,3},{5,4},{6,5},{7,6},{8,7},{9,8},{10,9},{11,1... | collective-permute-start | bytes 786440 | tf_op jit(solution)/shard_map/ppermute | solution.py:13
  4.5 12.4 %collective-permute-start = (f32[40,2048]{1,0:T(8,128)S(1)}, f32[40,2048]{1,0:T(8,128)S(1)}, u32[]{:S(2)}, u32[]{:S(2)}) collective-permute-start(f32[40,2048]{1,0:T(8,128)S(1)} %select_maximum_fusion), channel_id=1, source_target_pairs={{15,0},{0,1},{1,2},{2,3},{3,4},{4,5},{5,6},{6,7},{7,8},{8,9},{9,10... | collective-permute-start | bytes 983048 | tf_op jit(solution)/shard_map/ppermute | solution.py:13
  21.2 3.1 %collective-permute-start.2 = (f32[136,3]{0,1:T(4,128)S(1)}, f32[136,3]{0,1:T(4,128)S(1)}, u32[]{:S(2)}, u32[]{:S(2)}) collective-permute-start(f32[136,3]{0,1:T(4,128)S(1)} %fusion), channel_id=1, source_target_pairs={{0,16},{16,0},{32,48},{48,32},{64,80},{80,64},{96,112},{112,96},{1... | collective-permute-start | bytes 4904 | tf_op jit(solution)/shard_map/ppermute | solution.py:46
  25.2 13.5 %all-to-all-start = ((f32[16,1,408]{2,1,0:T(1,128)}), f32[16,1,408]{2,1,0:T(1,128)S(1)}, u32[]{:S(2)}, u32[]{:S(2)}) async-start(f32[16,1,408]{2,1,0:T(1,128)} %broadcast_in_dim.12), calls=%async_computation | async-start | bytes 65536 | tf_op jit(solution)/shard_map/all_to_all | solution.py:50

commit v13 on v9

--- a/solution.py
+++ b/solution.py
@@ -78,11 +78,10 @@
         jnp.concatenate([spikes[frames - edge :], after[HALO:].astype(jnp.int32)], axis=0),
     )
     spike_free_series = jnp.concatenate([head_window[1 : HALO + 1], inner[1 : frames - 31], tail_window[1 : HALO + 1]], axis=0)
-    despiked_window = jnp.concatenate([jnp.zeros((HALO - 1, voxels), jnp.float32), head_window[:1], spike_free_series], axis=0)
 
-    rows = despiked_window[HALO - 8 : HALO + frames]
+    rows = jnp.concatenate([head_window[:1], spike_free_series], axis=0)
     numer = sum_over_vox(precise_product(rows, tissue.T))
-    voxel_signals = numer / float(tissue.shape[1] * lax.axis_size("vox"))
+    voxel_signals = jnp.pad(numer, ((7, 0), (0, 0))) / float(tissue.shape[1] * lax.axis_size("vox"))
 
     first = lax.axis_index("tm") == 0
     base_before = jnp.concatenate([motion_before, voxel_signals[7:8]], axis=1)

time: 112 us -> 112 us (level)
  no operation moved by 1% of the time
where the time goes in v13:
time: 112 us
  blocking collectives  63.5 us (57%)
  other arithmetic  18.2 us (16%)
  starting transfers between devices  12.1 us (11%)
  waiting for transfers between devices  9.05 us (8%)
  matrix products  4.23 us (4%)
  local copies, waits for them, and re-layouts  4.13 us (4%)
    all_to_all x1, blocking collectives, sum_over_tm(): owned = lax.all_to_all(parts, 'tm', 0, 0, tiled=False).sum(axis=0)  35.9 us
    all_to_all x1, blocking collectives, sum_over_tm(): gathered = lax.all_to_all(copies, 'tm', 0, 0, tiled=False)  27.6 us
    mul x11, other arithmetic, despike_trimmed(): approx = (current + lagged) * 0.5  8.04 us
    all_to_all x1, waiting for transfers between devices, sum_over_vox(): lax.all_to_all(copies, 'vox', 0, 0, tiled=False).sum(axis=0)  7.44 us
    all_to_all x1, starting transfers between devices, sum_over_vox(): lax.all_to_all(copies, 'vox', 0, 0, tiled=False).sum(axis=0)  6.16 us
    ppermute x2, starting transfers between devices, from_behind(): return lax.ppermute(block, axis, route)  5.97 us
    another operation x3, other arithmetic, local(): factor = jnp.linalg.cholesky(gram_matrix)  3.96 us
    dot_general x4, matrix products, precise_product(): jnp.dot(left, right, precision=lax.Precision.HIGHEST, preferred_element_t...  3.83 us
  transfers between devices with their start and end apart: 3, of which 2 were waited for; matrix products, arithmetic and copies ran while one was open for 6% of the time, Pallas kernels for 0%

profile of v13, /device:TPU:64, one launch (start us, length us, event | category | flops | bytes accessed | tf_op | source)
XLA Modules:
  0.0 111.7 jit_solution(3557844336719497800)
XLA Ops:
  0.0 1.1 fusion.115
  1.1 1.0 slice_convert_fusion.3
  2.1 2.1 %collective-permute-start.1 = (f32[32,2048]{1,0:T(8,128)S(1)}, f32[32,2048]{1,0:T(8,128)S(1)}, u32[]{:S(2)}, u32[]{:S(2)}) collective-permute-start(f32[32,2048]{1,0:T(8,128)S(1)} %pad_maximum_fusion.4), channel_id=1, source_target_pairs={{1,0},{2,1},{3,2},{4,3},{5,4},{6,5},{7,6},{8,7},{9,8},{10,9},{11,1... | collective-permute-start | bytes 786440 | tf_op jit(solution)/shard_map/ppermute | solution.py:13
  4.4 0.1 copy.43
  4.5 3.8 %collective-permute-start = (f32[40,2048]{1,0:T(8,128)S(1)}, f32[40,2048]{1,0:T(8,128)S(1)}, u32[]{:S(2)}, u32[]{:S(2)}) collective-permute-start(f32[40,2048]{1,0:T(8,128)S(1)} %select_maximum_fusion), channel_id=1, source_target_pairs={{15,0},{0,1},{1,2},{2,3},{3,4},{4,5},{5,6},{6,7},{7,8},{8,9},{9,10... | collective-permute-start | bytes 983048 | tf_op jit(solution)/shard_map/ppermute | solution.py:13
  8.4 0.8 add_multiply_fusion.2
  9.2 1.3 %add_multiply_fusion.1 = (f32[125,2048]{1,0:T(8,128)S(1)}, f32[125,2048]{1,0:T(8,128)S(1)}) fusion(f32[127,2048]{1,0:T(8,128)S(1)} %get-tuple-element.21, s32[128,2048]{1,0:T(8,128)S(1)} %copy-done.1), kind=kLoop, calls=%fused_computation.49 | loop fusion | flops 8448000 | bytes 5120000 | tf_op jit(solution)/shard_map/mul | solution.py:35
  10.5 1.3 %add_multiply_fusion = (f32[121,2048]{1,0:T(8,128)S(1)}, f32[121,2048]{1,0:T(8,128)S(1)}) fusion(f32[125,2048]{1,0:T(8,128)S(1)} %get-tuple-element.19, s32[128,2048]{1,0:T(8,128)S(1)} %copy-done.1), kind=kLoop, calls=%fused_computation.48 | loop fusion | flops 8177664 | bytes 4956160 | tf_op jit(solution)/shard_map/mul | solution.py:35
  11.8 1.2 %add_multiply_fusion.3 = (f32[113,2048]{1,0:T(8,128)S(1)}, f32[113,2048]{1,0:T(8,128)S(1)}) fusion(f32[121,2048]{1,0:T(8,128)S(1)} %get-tuple-element.17, s32[128,2048]{1,0:T(8,128)S(1)} %copy-done.1), kind=kLoop, calls=%fused_computation.59 | loop fusion | flops 7636992 | bytes 4628480 | tf_op jit(solution)/shard_map/mul | solution.py:35
  13.0 0.1 fusion.29
  13.1 0.2 fusion.33
  13.4 0.3 fusion.31
  13.7 0.4 fusion.117
  14.0 0.3 fusion.35
  14.4 0.3 add_multiply_fusion.6
  14.7 0.5 add_multiply_fusion.5
  15.3 1.6 %collective-permute-done = f32[40,2048]{1,0:T(8,128)S(1)} collective-permute-done((f32[40,2048]{1,0:T(8,128)S(1)}, f32[40,2048]{1,0:T(8,128)S(1)}, u32[]{:S(2)}, u32[]{:S(2)}) %collective-permute-start) | collective-permute-done | bytes 327712 | tf_op jit(solution)/shard_map/ppermute | solution.py:13
  16.9 0.3 add_multiply_fusion.9
  17.2 0.5 add_multiply_fusion.8
  17.8 1.0 add_multiply_fusion.4
  18.8 0.4 add_multiply_fusion.10
  19.4 0.4 add_multiply_fusion.11
  20.2 1.0 fusion
  21.2 0.2 reshape.69
  21.4 0.7 broadcast_in_dim.8
  22.1 6.2 %all-to-all-start = ((f32[32,1,387]{2,1,0:T(1,128)}), f32[32,1,387]{2,1,0:T(1,128)S(1)}, u32[]{:S(2)}, u32[]{:S(2)}) async-start(f32[32,1,387]{2,1,0:T(1,128)} %broadcast_in_dim.8), calls=%async_computation | async-start | bytes 131072 | tf_op jit(solution)/shard_map/all_to_all | solution.py:48
  28.3 7.4 %all-to-all-done = f32[32,1,387]{2,1,0:T(1,128)S(1)} async-done(((f32[32,1,387]{2,1,0:T(1,128)}), f32[32,1,387]{2,1,0:T(1,128)S(1)}, u32[]{:S(2)}, u32[]{:S(2)}) %all-to-all-start) | async-done | bytes 49568 | tf_op jit(solution)/shard_map/all_to_all | solution.py:48
  35.8 0.2 reshape.70
  36.1 0.1 broadcast_select_fusion
  36.2 0.1 copy.36
  36.3 0.1 fusion.113
  36.4 0.4 concatenate.66
  36.8 0.2 fusion.123
  37.0 0.1 reshape.71
  37.1 0.7 fusion.36
  37.9 0.1 copy.38
  38.0 35.9 %all_to_all.15 = f32[16,37,128]{2,1,0:T(8,128)S(1)} all-to-all(f32[16,37,128]{2,1,0:T(8,128)S(1)} %maximum_bitcast_fusion), channel_id=1, replica_groups=mesh['vox'=32,'tm'=16] {'tm'}, dimensions={0} | all-to-all | bytes 606208 | tf_op jit(solution)/shard_map/all_to_all | solution.py:55
  73.9 27.6 %all_to_all.16 = f32[16,37,128]{2,1,0:T(8,128)S(1)} all-to-all(f32[16,37,128]{2,1,0:T(8,128)S(1)} %broadcast_in_dim.9), channel_id=1, replica_groups=mesh['vox'=32,'tm'=16] {'tm'}, dimensions={0} | all-to-all | bytes 606208 | tf_op jit(solution)/shard_map/all_to_all | solution.py:57
  101.5 0.1 reshape.73
  101.6 0.1 copy.39
  101.7 3.3 %cholesky.16 = f32[36,36]{1,0:T(8,128)S(1)} custom-call(f32[36,36]{1,0:T(8,128)S(1)} %fusion.108), custom_call_target="Cholesky" | custom-call | tf_op jit(solution)/shard_map/jit(cholesky)/cholesky | solution.py:110
  105.1 0.6 compare_reduce_fusion
  105.7 0.7 fusion.103
  106.4 2.8 %custom-call.10 = f32[1,36,36]{1,2,0:T(8,128)S(1)} custom-call(f32[1,36,36]{2,1,0:T(8,128)S(1)} %fusion.103), custom_call_target="InvertDiagBlocksLowerTriangular" | custom-call | tf_op jit(solution)/shard_map/jit(_cho_solve)/triangular_solve | solution.py:111
  109.1 0.2 fusion.106
  109.4 0.2 fusion.104
  109.6 0.1 copy.45
  109.7 2.0 %convolution_subtract_fusion = f32[128,2048]{1,0:T(8,128)} fusion(f32[36,128]{1,0:T(8,128)S(1)} %fusion.104, f32[36,2048]{1,0:T(8,128)S(1)} %bitcast.35, f32[16,2048]{1,0:T(8,128)S(1)} %fusion.102, f32[96,2048]{1,0:T(8,128)S(1)} %fusion.35, f32[16,2048]{1,0:T(8,128)S(1)} %slice.515), kind=kOutput, calls=%fused_computation | convolution fusion | flops 114032640 | bytes 2410496 | tf_op jit(solution)/shard_map/dot_general | solution.py:17
  (45 shorter events, 1.3 us)
Async XLA Ops:
  0.0 20.2 %copy-start = (f32[3,2048]{1,0:T(4,128)S(1)}, f32[3,2048]{1,0:T(4,128)}, u32[]{:S(2)}) copy-start(f32[3,2048]{1,0:T(4,128)} %param.7) | copy-start | bytes 73732
  0.0 8.3 %copy-start.2 = (f32[128,2048]{1,0:T(8,128)S(1)}, f32[128,2048]{1,0:T(8,128)}, u32[]{:S(2)}) copy-start(f32[128,2048]{1,0:T(8,128)} %param.4) | copy-start | bytes 3145732
  0.0 4.3 %copy-start.3 = (f32[128,6]{0,1:T(8,128)S(1)}, f32[128,6]{0,1:T(8,128)}, u32[]{:S(2)}) copy-start(f32[128,6]{0,1:T(8,128)} %param.6) | copy-start | bytes 9220
  2.1 6.3 %copy-start.1 = (s32[128,2048]{1,0:T(8,128)S(1)}, s32[128,2048]{1,0:T(8,128)}, u32[]{:S(2)}) copy-start(s32[128,2048]{1,0:T(8,128)} %param.5) | copy-start | bytes 3145732
  2.1 12.3 %collective-permute-start.1 = (f32[32,2048]{1,0:T(8,128)S(1)}, f32[32,2048]{1,0:T(8,128)S(1)}, u32[]{:S(2)}, u32[]{:S(2)}) collective-permute-start(f32[32,2048]{1,0:T(8,128)S(1)} %pad_maximum_fusion.4), channel_id=1, source_target_pairs={{1,0},{2,1},{3,2},{4,3},{5,4},{6,5},{7,6},{8,7},{9,8},{10,9},{11,1... | collective-permute-start | bytes 786440 | tf_op jit(solution)/shard_map/ppermute | solution.py:13
  4.5 12.4 %collective-permute-start = (f32[40,2048]{1,0:T(8,128)S(1)}, f32[40,2048]{1,0:T(8,128)S(1)}, u32[]{:S(2)}, u32[]{:S(2)}) collective-permute-start(f32[40,2048]{1,0:T(8,128)S(1)} %select_maximum_fusion), channel_id=1, source_target_pairs={{15,0},{0,1},{1,2},{2,3},{3,4},{4,5},{5,6},{6,7},{7,8},{8,9},{9,10... | collective-permute-start | bytes 983048 | tf_op jit(solution)/shard_map/ppermute | solution.py:13
  22.1 13.6 %all-to-all-start = ((f32[32,1,387]{2,1,0:T(1,128)}), f32[32,1,387]{2,1,0:T(1,128)S(1)}, u32[]{:S(2)}, u32[]{:S(2)}) async-start(f32[32,1,387]{2,1,0:T(1,128)} %broadcast_in_dim.8), calls=%async_computation | async-start | bytes 131072 | tf_op jit(solution)/shard_map/all_to_all | solution.py:48

commit v14 on v7

--- a/solution.py
+++ b/solution.py
@@ -43,8 +43,9 @@
 
 def sum_over_vox(block):
     n = lax.axis_size("vox")
-    copies = jnp.broadcast_to(block, (n,) + block.shape)
-    return lax.all_to_all(copies, "vox", 0, 0, tiled=False).sum(axis=0)
+    flat = block.reshape(1, block.size)
+    copies = jnp.broadcast_to(flat, (n,) + flat.shape)
+    return lax.all_to_all(copies, "vox", 0, 0, tiled=False).sum(axis=0).reshape(block.shape)
 
 
 def sum_over_tm(block):
@@ -66,8 +67,8 @@
     )
     tail = jnp.concatenate([series[frames - HALO :], jnp.pad(last_rows, ((0, 6), (0, 0)))], axis=0)
     head = jnp.concatenate([series[:HALO], spikes[:HALO].astype(jnp.float32)], axis=0)
+    after = from_behind(head, "tm", -1)
     before = from_behind(tail, "tm", 1)
-    after = from_behind(head, "tm", -1)
     motion_before = before[HALO + 1 : HALO + 2, : motion.shape[1]]
     flags_before = jnp.concatenate(
         [jnp.zeros((HALO - 1, voxels), jnp.int32), before[HALO : HALO + 1].astype(jnp.int32)], axis=0
@@ -83,11 +84,10 @@
         jnp.concatenate([spikes[frames - edge :], after[HALO:].astype(jnp.int32)], axis=0),
     )
     spike_free_series = jnp.concatenate([head_window[1 : HALO + 1], inner[1 : frames - 31], tail_window[1 : HALO + 1]], axis=0)
-    despiked_window = jnp.concatenate([jnp.zeros((HALO - 1, voxels), jnp.float32), head_window[:1], spike_free_series], axis=0)
 
-    rows = despiked_window[HALO - 8 : HALO + frames]
+    rows = jnp.concatenate([head_window[:1], spike_free_series], axis=0)
     numer = sum_over_vox(precise_product(rows, tissue.T))
-    voxel_signals = numer / float(tissue.shape[1] * lax.axis_size("vox"))
+    voxel_signals = jnp.pad(numer, ((7, 0), (0, 0))) / float(tissue.shape[1] * lax.axis_size("vox"))
 
     first = lax.axis_index("tm") == 0
     base_before = jnp.concatenate([motion_before, voxel_signals[7:8]], axis=1)

time: 115 us -> 113 us (0.983)
  no operation moved by 1% of the time
where the time goes in v14:
time: 113 us
  blocking collectives  60.7 us (54%)
  other arithmetic  19.1 us (17%)
  starting transfers between devices  13.3 us (12%)
  waiting for transfers between devices  10.2 us (9%)
  local copies, waits for them, and re-layouts  4.83 us (4%)
  matrix products  4.23 us (4%)
    all_to_all x1, blocking collectives, sum_over_tm(): owned = lax.all_to_all(parts, 'tm', 0, 0, tiled=False).sum(axis=0)  33.1 us
    all_to_all x1, blocking collectives, sum_over_tm(): gathered = lax.all_to_all(copies, 'tm', 0, 0, tiled=False)  27.6 us
    mul x11, other arithmetic, despike_trimmed(): approx = (current + lagged) * 0.5  8.02 us
    all_to_all x1, waiting for transfers between devices, sum_over_vox(): lax.all_to_all(copies, 'vox', 0, 0, tiled=False).sum(axis=0)  7.44 us
    all_to_all x1, starting transfers between devices, sum_over_vox(): lax.all_to_all(copies, 'vox', 0, 0, tiled=False).sum(axis=0)  7.32 us
    ppermute x2, starting transfers between devices, from_behind(): return lax.ppermute(block, axis, route)  5.97 us
    another operation x3, other arithmetic, local(): factor = jnp.linalg.cholesky(gram_matrix)  3.96 us
    dot_general x4, matrix products, precise_product(): jnp.dot(left, right, precision=lax.Precision.HIGHEST, preferred_element_t...  3.83 us
  transfers between devices with their start and end apart: 3, of which 2 were waited for; matrix products, arithmetic and copies ran while one was open for 6% of the time, Pallas kernels for 0%

profile of v14, /device:TPU:64, one launch (start us, length us, event | category | flops | bytes accessed | tf_op | source)
XLA Modules:
  0.0 112.9 jit_solution(4884514008102017657)
XLA Ops:
  0.0 0.8 slice.375
  0.9 0.1 copy.43
  0.9 0.8 slice_convert_fusion.3
  1.8 1.0 fusion.113
  2.8 4.0 %collective-permute-start = (f32[24,2048]{1,0:T(8,128)S(1)}, f32[24,2048]{1,0:T(8,128)S(1)}, u32[]{:S(2)}, u32[]{:S(2)}) collective-permute-start(f32[24,2048]{1,0:T(8,128)S(1)} %select_maximum_fusion), channel_id=1, source_target_pairs={{15,0},{0,1},{1,2},{2,3},{3,4},{4,5},{5,6},{6,7},{7,8},{8,9},{9,10... | collective-permute-start | bytes 589832 | tf_op jit(solution)/shard_map/ppermute | solution.py:13
  6.8 0.9 slice_convert_fusion.1
  7.8 2.0 %collective-permute-start.1 = (f32[32,2048]{1,0:T(8,128)S(1)}, f32[32,2048]{1,0:T(8,128)S(1)}, u32[]{:S(2)}, u32[]{:S(2)}) collective-permute-start(f32[32,2048]{1,0:T(8,128)S(1)} %pad_maximum_fusion.4), channel_id=1, source_target_pairs={{1,0},{2,1},{3,2},{4,3},{5,4},{6,5},{7,6},{8,7},{9,8},{10,9},{11,1... | collective-permute-start | bytes 786440 | tf_op jit(solution)/shard_map/ppermute | solution.py:13
  9.8 0.8 add_multiply_fusion.2
  10.6 1.3 %add_multiply_fusion.1 = (f32[125,2048]{1,0:T(8,128)S(1)}, f32[125,2048]{1,0:T(8,128)S(1)}) fusion(f32[127,2048]{1,0:T(8,128)S(1)} %get-tuple-element.19, s32[128,2048]{1,0:T(8,128)S(1)} %copy-done.1), kind=kLoop, calls=%fused_computation.49 | loop fusion | flops 8448000 | bytes 5120000 | tf_op jit(solution)/shard_map/mul | solution.py:35
  11.9 1.3 %add_multiply_fusion = (f32[121,2048]{1,0:T(8,128)S(1)}, f32[121,2048]{1,0:T(8,128)S(1)}) fusion(f32[125,2048]{1,0:T(8,128)S(1)} %get-tuple-element.17, s32[128,2048]{1,0:T(8,128)S(1)} %copy-done.1), kind=kLoop, calls=%fused_computation.48 | loop fusion | flops 8177664 | bytes 4956160 | tf_op jit(solution)/shard_map/mul | solution.py:35
  13.3 1.2 %add_multiply_fusion.3 = (f32[113,2048]{1,0:T(8,128)S(1)}, f32[113,2048]{1,0:T(8,128)S(1)}) fusion(f32[121,2048]{1,0:T(8,128)S(1)} %get-tuple-element.15, s32[128,2048]{1,0:T(8,128)S(1)} %copy-done.1), kind=kLoop, calls=%fused_computation.59 | loop fusion | flops 7636992 | bytes 4628480 | tf_op jit(solution)/shard_map/mul | solution.py:35
  14.5 0.1 fusion.29
  14.6 0.2 fusion.33
  14.8 0.3 fusion.31
  15.1 0.4 fusion.115
  15.5 0.3 fusion.35
  15.9 0.1 pad_add_fusion.1
  16.0 2.8 %collective-permute-done.1 = f32[32,2048]{1,0:T(8,128)S(1)} collective-permute-done((f32[32,2048]{1,0:T(8,128)S(1)}, f32[32,2048]{1,0:T(8,128)S(1)}, u32[]{:S(2)}, u32[]{:S(2)}) %collective-permute-start.1) | collective-permute-done | bytes 262176 | tf_op jit(solution)/shard_map/ppermute | solution.py:13
  18.8 0.6 add_multiply_fusion.6
  19.4 0.5 add_multiply_fusion.5
  20.0 0.5 add_multiply_fusion.4
  20.5 0.4 add_multiply_fusion.10
  21.1 0.5 add_multiply_fusion.8
  21.7 0.5 add_multiply_fusion.7
  22.2 0.4 add_multiply_fusion.11
  22.9 1.0 fusion
  23.9 0.2 reshape.69
  24.2 0.7 broadcast_in_dim.12
  24.8 7.3 %all-to-all-start = ((f32[32,1,387]{2,1,0:T(1,128)}), f32[32,1,387]{2,1,0:T(1,128)S(1)}, u32[]{:S(2)}, u32[]{:S(2)}) async-start(f32[32,1,387]{2,1,0:T(1,128)} %broadcast_in_dim.12), calls=%async_computation | async-start | bytes 131072 | tf_op jit(solution)/shard_map/all_to_all | solution.py:48
  32.2 7.4 %all-to-all-done = f32[32,1,387]{2,1,0:T(1,128)S(1)} async-done(((f32[32,1,387]{2,1,0:T(1,128)}), f32[32,1,387]{2,1,0:T(1,128)S(1)}, u32[]{:S(2)}, u32[]{:S(2)}) %all-to-all-start) | async-done | bytes 49568 | tf_op jit(solution)/shard_map/all_to_all | solution.py:48
  39.7 0.2 reshape.70
  40.1 0.1 copy.36
  40.3 0.4 concatenate.74
  40.7 0.2 fusion.120
  40.9 0.1 reshape.71
  41.0 0.7 fusion.36
  41.8 0.1 copy.38
  41.9 33.1 %all_to_all.15 = f32[16,37,128]{2,1,0:T(8,128)S(1)} all-to-all(f32[16,37,128]{2,1,0:T(8,128)S(1)} %maximum_bitcast_fusion), channel_id=1, replica_groups=mesh['vox'=32,'tm'=16] {'tm'}, dimensions={0} | all-to-all | bytes 606208 | tf_op jit(solution)/shard_map/all_to_all | solution.py:55
  75.1 27.6 %all_to_all.16 = f32[16,37,128]{2,1,0:T(8,128)S(1)} all-to-all(f32[16,37,128]{2,1,0:T(8,128)S(1)} %broadcast_in_dim.13), channel_id=1, replica_groups=mesh['vox'=32,'tm'=16] {'tm'}, dimensions={0} | all-to-all | bytes 606208 | tf_op jit(solution)/shard_map/all_to_all | solution.py:57
  102.7 0.1 reshape.73
  102.9 3.3 %cholesky.16 = f32[36,36]{1,0:T(8,128)S(1)} custom-call(f32[36,36]{1,0:T(8,128)S(1)} %fusion.105), custom_call_target="Cholesky" | custom-call | tf_op jit(solution)/shard_map/jit(cholesky)/cholesky | solution.py:116
  106.2 0.6 compare_reduce_fusion
  106.9 0.7 fusion.100
  107.5 2.8 %custom-call.10 = f32[1,36,36]{1,2,0:T(8,128)S(1)} custom-call(f32[1,36,36]{2,1,0:T(8,128)S(1)} %fusion.100), custom_call_target="InvertDiagBlocksLowerTriangular" | custom-call | tf_op jit(solution)/shard_map/jit(_cho_solve)/triangular_solve | solution.py:117
  110.3 0.2 fusion.103
  110.5 0.2 fusion.101
  110.8 0.1 copy.45
  110.9 2.0 %convolution_subtract_fusion = f32[128,2048]{1,0:T(8,128)} fusion(f32[36,128]{1,0:T(8,128)S(1)} %fusion.101, f32[36,2048]{1,0:T(8,128)S(1)} %bitcast.35, f32[16,2048]{1,0:T(8,128)S(1)} %fusion.99, f32[96,2048]{1,0:T(8,128)S(1)} %fusion.35, f32[16,2048]{1,0:T(8,128)S(1)} %slice.510), kind=kOutput, calls=%fused_computation | convolution fusion | flops 114032640 | bytes 2410496 | tf_op jit(solution)/shard_map/dot_general | solution.py:17
  (51 shorter events, 1.5 us)
Async XLA Ops:
  0.0 22.9 %copy-start = (f32[3,2048]{1,0:T(4,128)S(1)}, f32[3,2048]{1,0:T(4,128)}, u32[]{:S(2)}) copy-start(f32[3,2048]{1,0:T(4,128)} %param.7) | copy-start | bytes 73732
  0.0 9.8 %copy-start.2 = (f32[128,2048]{1,0:T(8,128)S(1)}, f32[128,2048]{1,0:T(8,128)}, u32[]{:S(2)}) copy-start(f32[128,2048]{1,0:T(8,128)} %param.4) | copy-start | bytes 3145732
  2.8 7.0 %copy-start.1 = (s32[128,2048]{1,0:T(8,128)S(1)}, s32[128,2048]{1,0:T(8,128)}, u32[]{:S(2)}) copy-start(s32[128,2048]{1,0:T(8,128)} %param.5) | copy-start | bytes 3145732
  2.8 13.0 %collective-permute-start = (f32[24,2048]{1,0:T(8,128)S(1)}, f32[24,2048]{1,0:T(8,128)S(1)}, u32[]{:S(2)}, u32[]{:S(2)}) collective-permute-start(f32[24,2048]{1,0:T(8,128)S(1)} %select_maximum_fusion), channel_id=1, source_target_pairs={{15,0},{0,1},{1,2},{2,3},{3,4},{4,5},{5,6},{6,7},{7,8},{8,9},{9,10... | collective-permute-start | bytes 589832 | tf_op jit(solution)/shard_map/ppermute | solution.py:13
  7.8 11.1 %collective-permute-start.1 = (f32[32,2048]{1,0:T(8,128)S(1)}, f32[32,2048]{1,0:T(8,128)S(1)}, u32[]{:S(2)}, u32[]{:S(2)}) collective-permute-start(f32[32,2048]{1,0:T(8,128)S(1)} %pad_maximum_fusion.4), channel_id=1, source_target_pairs={{1,0},{2,1},{3,2},{4,3},{5,4},{6,5},{7,6},{8,7},{9,8},{10,9},{11,1... | collective-permute-start | bytes 786440 | tf_op jit(solution)/shard_map/ppermute | solution.py:13
  22.9 17.3 %copy-start.3 = (f32[128,6]{0,1:T(8,128)S(1)}, f32[128,6]{0,1:T(8,128)}, u32[]{:S(2)}) copy-start(f32[128,6]{0,1:T(8,128)} %param.6) | copy-start | bytes 9220
  24.8 14.8 %all-to-all-start = ((f32[32,1,387]{2,1,0:T(1,128)}), f32[32,1,387]{2,1,0:T(1,128)S(1)}, u32[]{:S(2)}, u32[]{:S(2)}) async-start(f32[32,1,387]{2,1,0:T(1,128)} %broadcast_in_dim.12), calls=%async_computation | async-start | bytes 131072 | tf_op jit(solution)/shard_map/all_to_all | solution.py:48

commit v15 on v13

--- a/solution.py
+++ b/solution.py
@@ -107,7 +107,7 @@
     summed = sum_over_tm(packed)
     cross_products = summed[:terms]
     gram_matrix = summed[terms:].reshape(-1)[: terms * terms].reshape(terms, terms)
-    factor = jnp.linalg.cholesky(gram_matrix)
+    factor = lax.linalg.cholesky(gram_matrix, symmetrize_input=False)
     weights = jax.scipy.linalg.cho_solve((factor, True), nuisance_matrix.T)
     return spike_free_series - precise_product(weights.T, cross_products)
 

time: 112 us -> 112 us (level)
  no operation moved by 1% of the time
where the time goes in v15:
time: 112 us
  blocking collectives  63.5 us (57%)
  other arithmetic  18.2 us (16%)
  starting transfers between devices  12.1 us (11%)
  waiting for transfers between devices  9.05 us (8%)
  matrix products  4.23 us (4%)
  local copies, waits for them, and re-layouts  4.04 us (4%)
    all_to_all x1, blocking collectives, sum_over_tm(): owned = lax.all_to_all(parts, 'tm', 0, 0, tiled=False).sum(axis=0)  35.9 us
    all_to_all x1, blocking collectives, sum_over_tm(): gathered = lax.all_to_all(copies, 'tm', 0, 0, tiled=False)  27.6 us
    mul x11, other arithmetic, despike_trimmed(): approx = (current + lagged) * 0.5  8.04 us
    all_to_all x1, waiting for transfers between devices, sum_over_vox(): lax.all_to_all(copies, 'vox', 0, 0, tiled=False).sum(axis=0)  7.44 us
    all_to_all x1, starting transfers between devices, sum_over_vox(): lax.all_to_all(copies, 'vox', 0, 0, tiled=False).sum(axis=0)  6.16 us
    ppermute x2, starting transfers between devices, from_behind(): return lax.ppermute(block, axis, route)  5.97 us
    another operation x3, other arithmetic, local(): factor = lax.linalg.cholesky(gram_matrix, symmetrize_input=False)  3.96 us
    dot_general x4, matrix products, precise_product(): jnp.dot(left, right, precision=lax.Precision.HIGHEST, preferred_element_t...  3.83 us
  transfers between devices with their start and end apart: 3, of which 2 were waited for; matrix products, arithmetic and copies ran while one was open for 6% of the time, Pallas kernels for 0%

profile of v15, /device:TPU:64, one launch (start us, length us, event | category | flops | bytes accessed | tf_op | source)
XLA Modules:
  0.0 111.6 jit_solution(7048475131324896745)
XLA Ops:
  0.0 1.1 fusion.114
  1.1 1.0 slice_convert_fusion.3
  2.1 2.1 %collective-permute-start.1 = (f32[32,2048]{1,0:T(8,128)S(1)}, f32[32,2048]{1,0:T(8,128)S(1)}, u32[]{:S(2)}, u32[]{:S(2)}) collective-permute-start(f32[32,2048]{1,0:T(8,128)S(1)} %pad_maximum_fusion.4), channel_id=1, source_target_pairs={{1,0},{2,1},{3,2},{4,3},{5,4},{6,5},{7,6},{8,7},{9,8},{10,9},{11,1... | collective-permute-start | bytes 786440 | tf_op jit(solution)/shard_map/ppermute | solution.py:13
  4.3 0.1 slice.374
  4.4 0.1 copy.38
  4.5 3.8 %collective-permute-start = (f32[40,2048]{1,0:T(8,128)S(1)}, f32[40,2048]{1,0:T(8,128)S(1)}, u32[]{:S(2)}, u32[]{:S(2)}) collective-permute-start(f32[40,2048]{1,0:T(8,128)S(1)} %select_maximum_fusion), channel_id=1, source_target_pairs={{15,0},{0,1},{1,2},{2,3},{3,4},{4,5},{5,6},{6,7},{7,8},{8,9},{9,10... | collective-permute-start | bytes 983048 | tf_op jit(solution)/shard_map/ppermute | solution.py:13
  8.4 0.8 add_multiply_fusion.2
  9.2 1.3 %add_multiply_fusion.1 = (f32[125,2048]{1,0:T(8,128)S(1)}, f32[125,2048]{1,0:T(8,128)S(1)}) fusion(f32[127,2048]{1,0:T(8,128)S(1)} %get-tuple-element.21, s32[128,2048]{1,0:T(8,128)S(1)} %copy-done.1), kind=kLoop, calls=%fused_computation.49 | loop fusion | flops 8448000 | bytes 5120000 | tf_op jit(solution)/shard_map/mul | solution.py:35
  10.5 1.3 %add_multiply_fusion = (f32[121,2048]{1,0:T(8,128)S(1)}, f32[121,2048]{1,0:T(8,128)S(1)}) fusion(f32[125,2048]{1,0:T(8,128)S(1)} %get-tuple-element.19, s32[128,2048]{1,0:T(8,128)S(1)} %copy-done.1), kind=kLoop, calls=%fused_computation.48 | loop fusion | flops 8177664 | bytes 4956160 | tf_op jit(solution)/shard_map/mul | solution.py:35
  11.8 1.2 %add_multiply_fusion.3 = (f32[113,2048]{1,0:T(8,128)S(1)}, f32[113,2048]{1,0:T(8,128)S(1)}) fusion(f32[121,2048]{1,0:T(8,128)S(1)} %get-tuple-element.17, s32[128,2048]{1,0:T(8,128)S(1)} %copy-done.1), kind=kLoop, calls=%fused_computation.59 | loop fusion | flops 7636992 | bytes 4628480 | tf_op jit(solution)/shard_map/mul | solution.py:35
  13.0 0.1 fusion.29
  13.1 0.2 fusion.33
  13.4 0.3 fusion.31
  13.7 0.4 fusion.116
  14.0 0.3 fusion.35
  14.4 0.3 add_multiply_fusion.6
  14.7 0.5 add_multiply_fusion.5
  15.3 1.6 %collective-permute-done = f32[40,2048]{1,0:T(8,128)S(1)} collective-permute-done((f32[40,2048]{1,0:T(8,128)S(1)}, f32[40,2048]{1,0:T(8,128)S(1)}, u32[]{:S(2)}, u32[]{:S(2)}) %collective-permute-start) | collective-permute-done | bytes 327712 | tf_op jit(solution)/shard_map/ppermute | solution.py:13
  16.9 0.3 add_multiply_fusion.9
  17.2 0.5 add_multiply_fusion.8
  17.8 1.0 add_multiply_fusion.4
  18.8 0.4 add_multiply_fusion.10
  19.4 0.4 add_multiply_fusion.11
  20.2 1.0 fusion
  21.2 0.2 reshape.68
  21.4 0.7 broadcast_in_dim.7
  22.1 6.2 %all-to-all-start = ((f32[32,1,387]{2,1,0:T(1,128)}), f32[32,1,387]{2,1,0:T(1,128)S(1)}, u32[]{:S(2)}, u32[]{:S(2)}) async-start(f32[32,1,387]{2,1,0:T(1,128)} %broadcast_in_dim.7), calls=%async_computation | async-start | bytes 131072 | tf_op jit(solution)/shard_map/all_to_all | solution.py:48
  28.3 7.4 %all-to-all-done = f32[32,1,387]{2,1,0:T(1,128)S(1)} async-done(((f32[32,1,387]{2,1,0:T(1,128)}), f32[32,1,387]{2,1,0:T(1,128)S(1)}, u32[]{:S(2)}, u32[]{:S(2)}) %all-to-all-start) | async-done | bytes 49568 | tf_op jit(solution)/shard_map/all_to_all | solution.py:48
  35.8 0.2 reshape.69
  36.1 0.1 broadcast_select_fusion
  36.2 0.1 copy.32
  36.3 0.1 fusion.112
  36.4 0.4 concatenate.66
  36.8 0.2 fusion.122
  37.0 0.1 reshape.70
  37.1 0.7 fusion.36
  37.9 0.1 copy.34
  38.0 35.9 %all_to_all.15 = f32[16,37,128]{2,1,0:T(8,128)S(1)} all-to-all(f32[16,37,128]{2,1,0:T(8,128)S(1)} %maximum_bitcast_fusion), channel_id=1, replica_groups=mesh['vox'=32,'tm'=16] {'tm'}, dimensions={0} | all-to-all | bytes 606208 | tf_op jit(solution)/shard_map/all_to_all | solution.py:55
  73.9 27.6 %all_to_all.16 = f32[16,37,128]{2,1,0:T(8,128)S(1)} all-to-all(f32[16,37,128]{2,1,0:T(8,128)S(1)} %broadcast_in_dim.8), channel_id=1, replica_groups=mesh['vox'=32,'tm'=16] {'tm'}, dimensions={0} | all-to-all | bytes 606208 | tf_op jit(solution)/shard_map/all_to_all | solution.py:57
  101.5 0.1 reshape.72
  101.6 3.3 %cholesky.16 = f32[36,36]{1,0:T(8,128)S(1)} custom-call(f32[36,36]{1,0:T(8,128)S(1)} %reshape.72), custom_call_target="Cholesky" | custom-call | tf_op jit(solution)/shard_map/cholesky | solution.py:110
  104.9 0.6 compare_reduce_fusion
  105.6 0.7 fusion.103
  106.2 2.8 %custom-call.9 = f32[1,36,36]{1,2,0:T(8,128)S(1)} custom-call(f32[1,36,36]{2,1,0:T(8,128)S(1)} %fusion.103), custom_call_target="InvertDiagBlocksLowerTriangular" | custom-call | tf_op jit(solution)/shard_map/jit(_cho_solve)/triangular_solve | solution.py:111
  109.0 0.2 fusion.106
  109.3 0.2 fusion.104
  109.5 0.1 copy.40
  109.6 2.0 %convolution_subtract_fusion = f32[128,2048]{1,0:T(8,128)} fusion(f32[36,128]{1,0:T(8,128)S(1)} %fusion.104, f32[36,2048]{1,0:T(8,128)S(1)} %bitcast.31, f32[16,2048]{1,0:T(8,128)S(1)} %fusion.102, f32[96,2048]{1,0:T(8,128)S(1)} %fusion.35, f32[16,2048]{1,0:T(8,128)S(1)} %slice.513), kind=kOutput, calls=%fused_computation | convolution fusion | flops 114032640 | bytes 2410496 | tf_op jit(solution)/shard_map/dot_general | solution.py:17
  (43 shorter events, 1.2 us)
Async XLA Ops:
  0.0 20.2 %copy-start = (f32[3,2048]{1,0:T(4,128)S(1)}, f32[3,2048]{1,0:T(4,128)}, u32[]{:S(2)}) copy-start(f32[3,2048]{1,0:T(4,128)} %param.7) | copy-start | bytes 73732
  0.0 8.3 %copy-start.2 = (f32[128,2048]{1,0:T(8,128)S(1)}, f32[128,2048]{1,0:T(8,128)}, u32[]{:S(2)}) copy-start(f32[128,2048]{1,0:T(8,128)} %param.4) | copy-start | bytes 3145732
  0.0 4.3 %copy-start.3 = (f32[128,6]{0,1:T(8,128)S(1)}, f32[128,6]{0,1:T(8,128)}, u32[]{:S(2)}) copy-start(f32[128,6]{0,1:T(8,128)} %param.6) | copy-start | bytes 9220
  2.1 6.3 %copy-start.1 = (s32[128,2048]{1,0:T(8,128)S(1)}, s32[128,2048]{1,0:T(8,128)}, u32[]{:S(2)}) copy-start(s32[128,2048]{1,0:T(8,128)} %param.5) | copy-start | bytes 3145732
  2.1 12.3 %collective-permute-start.1 = (f32[32,2048]{1,0:T(8,128)S(1)}, f32[32,2048]{1,0:T(8,128)S(1)}, u32[]{:S(2)}, u32[]{:S(2)}) collective-permute-start(f32[32,2048]{1,0:T(8,128)S(1)} %pad_maximum_fusion.4), channel_id=1, source_target_pairs={{1,0},{2,1},{3,2},{4,3},{5,4},{6,5},{7,6},{8,7},{9,8},{10,9},{11,1... | collective-permute-start | bytes 786440 | tf_op jit(solution)/shard_map/ppermute | solution.py:13
  4.5 12.4 %collective-permute-start = (f32[40,2048]{1,0:T(8,128)S(1)}, f32[40,2048]{1,0:T(8,128)S(1)}, u32[]{:S(2)}, u32[]{:S(2)}) collective-permute-start(f32[40,2048]{1,0:T(8,128)S(1)} %select_maximum_fusion), channel_id=1, source_target_pairs={{15,0},{0,1},{1,2},{2,3},{3,4},{4,5},{5,6},{6,7},{7,8},{8,9},{9,10... | collective-permute-start | bytes 983048 | tf_op jit(solution)/shard_map/ppermute | solution.py:13
  22.1 13.6 %all-to-all-start = ((f32[32,1,387]{2,1,0:T(1,128)}), f32[32,1,387]{2,1,0:T(1,128)S(1)}, u32[]{:S(2)}, u32[]{:S(2)}) async-start(f32[32,1,387]{2,1,0:T(1,128)} %broadcast_in_dim.7), calls=%async_computation | async-start | bytes 131072 | tf_op jit(solution)/shard_map/all_to_all | solution.py:48
